TPU v7x, 128 devices: a whole 4x4x4 slice. The times are simulated.
128 devices in a mesh: band: 32 (over z, x, core), seg: 4 (over y).
Axes of the slice: x: 4, y: 4, z: 4, core: 2. Of those that a mesh axis runs over, the one named last changes fastest.
Arguments:
- voltages: float32 [4, 1, 2, 2, 1024, 3072], P('seg', None, None, None, 'band'), may hold values from -6 to 6
- chirp_phase: float32 [1, 1024, 4096], P(None, 'seg', 'band'), may hold values from -3.140625 to 3.140625
Outputs:
- dedispersed: float32 [4, 1, 2, 2, 1024, 3072], P('seg', None, None, None, 'band')
All inputs are finite; a program needn't handle non-finite values.
Results may differ from a plain program's by a relative error of at most 0.00015.
Values sent between devices are 32-bit elements; how exact they have to be, the bound alone decides.
No kernel may reach another device: no remote copies, remote signals or barrier semaphores. Data moves between devices by JAX's collectives and lax.ppermute only.
A program may use at most 64 MiB of HBM per device.

v0:
```python
import math

import jax
import jax.numpy as jnp
from jax import lax
from jax.sharding import PartitionSpec as P


def passed_along(block, axis, distance):
    devices = range(lax.axis_size(axis))
    route = [(i - distance, i) for i in devices if i - distance in devices]
    return lax.ppermute(block, axis, route)


def gathered(block, axis, dim):
    size = lax.axis_size(axis)
    pieces = [block]
    for shift in range(1, size):
        route = [((i + shift) % size, i) for i in range(size)]
        pieces.append(lax.ppermute(block, axis, route))
    ahead = jnp.stack(pieces, axis=0)
    ordered = jnp.roll(ahead, lax.axis_index(axis), axis=0)
    ordered = jnp.moveaxis(ordered, 0, dim)
    shape = list(block.shape)
    shape[dim] *= size
    return ordered.reshape(shape)


def split_factor(length):
    factor = int(math.isqrt(length))
    while length % factor:
        factor -= 1
    return factor


def tables(length, direction):
    places = jnp.arange(length, dtype=jnp.int32)
    product = places[:, None] * places[None, :] % length
    angles = direction * 2.0 * math.pi / length * product.astype(jnp.float32)
    return (jnp.cos(angles), jnp.sin(angles))


def rotate(real_part, imag_part, product, scale):
    angles = scale * product.astype(jnp.float32)
    cosine = jnp.cos(angles)
    sine = jnp.sin(angles)
    return (real_part * cosine - imag_part * sine, real_part * sine + imag_part * cosine)


def transform_last(real_part, imag_part, direction):
    length = real_part.shape[-1]
    inner = split_factor(length)
    outer = length // inner
    leading = real_part.shape[:-1]
    real_part = real_part.reshape(leading + (outer, inner))
    imag_part = imag_part.reshape(leading + (outer, inner))
    cos_outer, sin_outer = tables(outer, direction)
    highest = lax.Precision.HIGHEST
    first_real = jnp.einsum(
        "...nj,nk->...kj", real_part, cos_outer, precision=highest
    ) - jnp.einsum("...nj,nk->...kj", imag_part, sin_outer, precision=highest)
    first_imag = jnp.einsum(
        "...nj,nk->...kj", real_part, sin_outer, precision=highest
    ) + jnp.einsum("...nj,nk->...kj", imag_part, cos_outer, precision=highest)
    outer_index = jnp.arange(outer, dtype=jnp.int32)[:, None]
    inner_index = jnp.arange(inner, dtype=jnp.int32)[None, :]
    first_real, first_imag = rotate(
        first_real,
        first_imag,
        outer_index * inner_index % length,
        direction * 2.0 * math.pi / length,
    )
    cos_inner, sin_inner = tables(inner, direction)
    last_real = jnp.matmul(first_real, cos_inner, precision=highest) - jnp.matmul(
        first_imag, sin_inner, precision=highest
    )
    last_imag = jnp.matmul(first_real, sin_inner, precision=highest) + jnp.matmul(
        first_imag, cos_inner, precision=highest
    )
    last_real = jnp.swapaxes(last_real, -1, -2).reshape(leading + (length,))
    last_imag = jnp.swapaxes(last_imag, -1, -2).reshape(leading + (length,))
    return (last_real, last_imag)


def transform_rows(real_part, imag_part, direction):
    result_real, result_imag = transform_last(
        jnp.swapaxes(real_part, -1, -2), jnp.swapaxes(imag_part, -1, -2), direction
    )
    return (jnp.swapaxes(result_real, -1, -2), jnp.swapaxes(result_imag, -1, -2))


def row_pass(spread):
    result_real, result_imag = transform_rows(spread[:, :, 0], spread[:, :, 1], -1.0)
    return jnp.stack([result_real, result_imag], axis=2)


def column_pass(gathered):
    cols = gathered.shape[-1]
    length_scale = 1.0 / (gathered.shape[-2] * lax.axis_size("band") * cols)
    result_real, result_imag = transform_last(gathered[:, :, 0], gathered[:, :, 1], 1.0)
    result = jnp.stack([result_real * length_scale, result_imag * length_scale], axis=2)
    return result[..., cols // 4 :]


def per_device(voltages, chirp_phase):
    block = voltages[0]
    rows_dev = block.shape[3]
    valid_cols = block.shape[4]
    cols = valid_cols * 4 // 3
    bands = lax.axis_size("band")
    rows = rows_dev * bands
    length = rows * cols
    width = cols // bands
    tail = block[..., valid_cols - cols // 4 :]
    history = passed_along(tail, "seg", 1)
    buffer = jnp.concatenate([history, block], axis=-1)
    real_part, imag_part = transform_last(buffer[:, :, 0], buffer[:, :, 1], -1.0)
    row_index = lax.axis_index("band") * rows_dev + jnp.arange(rows_dev, dtype=jnp.int32)
    col_index = jnp.arange(cols, dtype=jnp.int32)
    real_part, imag_part = rotate(
        real_part,
        imag_part,
        row_index[:, None] * col_index[None, :] % length,
        -2.0 * math.pi / length,
    )
    stacked = jnp.stack([real_part, imag_part], axis=2)
    spectra = row_pass(lax.all_to_all(stacked, "band", split_axis=4, concat_axis=3, tiled=True))
    real_part, imag_part = (spectra[:, :, 0], spectra[:, :, 1])
    phases = gathered(chirp_phase, "seg", 1)
    cosine = jnp.cos(phases)[:, None]
    sine = jnp.sin(phases)[:, None]
    real_part, imag_part = (
        real_part * cosine - imag_part * sine,
        real_part * sine + imag_part * cosine,
    )
    real_part, imag_part = transform_rows(real_part, imag_part, 1.0)
    full_rows = jnp.arange(rows, dtype=jnp.int32)
    own_cols = lax.axis_index("band") * width + jnp.arange(width, dtype=jnp.int32)
    real_part, imag_part = rotate(
        real_part,
        imag_part,
        full_rows[:, None] * own_cols[None, :] % length,
        2.0 * math.pi / length,
    )
    columns = jnp.stack([real_part, imag_part], axis=2)
    result = column_pass(lax.all_to_all(columns, "band", split_axis=3, concat_axis=4, tiled=True))
    return result[None]


def solution(mesh):
    in_specs = (P("seg", None, None, None, "band", None), P(None, "seg", "band"))
    out_specs = P("seg", None, None, None, "band", None)
    return jax.shard_map(
        per_device, mesh=mesh, in_specs=in_specs, out_specs=out_specs, check_vma=False
    )
```

profile of v0, /device:TPU:0, one launch (start us, length us, event | category | flops | bytes accessed | tf_op | source)
XLA Modules:
  0.0 269.6 jit_solution(694913317675415932)
XLA Ops:
  0.0 3.1 %collective-permute-start.1 = (f32[1,256,128]{2,1,0:T(8,128)}, f32[1,256,128]{2,1,0:T(8,128)S(1)}, u32[]{:S(2)}, u32[]{:S(2)}) collective-permute-start(f32[1,256,128]{2,1,0:T(8,128)} %param.3), channel_id=1, source_target_pairs={{1,0},{2,1},{3,2},{0,3},{5,4},{6,5},{7,6},{4,7},{9,8},{10,9},{11,1... | collective-permute-start | bytes 393224 | tf_op jit(solution)/shard_map/ppermute | solution.py:20
  5.8 4.6 %collective-permute-start = (f32[1,2,2,32,1024]{4,3,2,1,0:T(8,128)S(1)}, f32[1,2,2,32,1024]{4,3,2,1,0:T(8,128)}, u32[]{:S(2)}, u32[]{:S(2)}) collective-permute-start(f32[1,2,2,32,1024]{4,3,2,1,0:T(8,128)S(1)} %slice.32), channel_id=1, source_target_pairs={{0,1},{1,2},{2,3},{4,5},{5,6},{6,7},{8,9},{9,10},{10,11},{12,13},{... | collective-permute-start | bytes 1572872 | tf_op jit(solution)/shard_map/ppermute | solution.py:12
  10.4 3.2 %fusion.81 = (f32[32,4096]{1,0:T(8,128)}, f32[32,4096]{1,0:T(8,128)}) fusion(s32[32]{0:T(128)S(1)} %iota_add_fusion.1), kind=kLoop, calls=%fused_computation.117 | loop fusion | flops 1835008 | bytes 1048704 | tf_op jit(solution)/shard_map/cos | solution.py:45
  13.8 2.9 %fusion.79 = (f32[1024,128]{1,0:T(8,128)}, f32[1024,128]{1,0:T(8,128)}) fusion(s32[128]{0:T(128)S(1)} %iota_add_fusion), kind=kLoop, calls=%fused_computation.115 | loop fusion | flops 1835008 | bytes 1049088 | tf_op jit(solution)/shard_map/cos | solution.py:45
  16.7 3.8 %collective-permute-done = f32[1,2,2,32,1024]{4,3,2,1,0:T(8,128)} collective-permute-done((f32[1,2,2,32,1024]{4,3,2,1,0:T(8,128)S(1)}, f32[1,2,2,32,1024]{4,3,2,1,0:T(8,128)}, u32[]{:S(2)}, u32[]{:S(2)}) %collective-permute-start) | collective-permute-done | bytes 524320 | tf_op jit(solution)/shard_map/ppermute | solution.py:12
  20.5 2.2 fusion.37
  22.6 2.3 reshape.541
  24.9 3.3 %fusion.92 = f32[64,2,32,64]{3,0,2,1:T(8,128)} fusion(f32[2,32,64,64]{3,2,1,0:T(8,128)S(1)} %reshape.541), kind=kOutput, calls=%fused_computation.141 | convolution fusion | flops 201383936 | bytes 2097152 | tf_op jit(solution)/shard_map/...nj,nk->...kj/dot_general | solution.py:61
  28.3 3.4 %fusion.96 = f32[64,2,32,64]{3,0,2,1:T(8,128)} fusion(f32[2,32,64,64]{3,2,1,0:T(8,128)S(1)} %reshape.541), kind=kOutput, calls=%fused_computation.145 | convolution fusion | flops 201383936 | bytes 2097152 | tf_op jit(solution)/shard_map/...nj,nk->...kj/dot_general | solution.py:64
  31.6 2.2 reshape.540
  33.8 4.4 %convolution_subtract_fusion.1 = f32[64,2,32,64]{3,0,2,1:T(8,128)S(1)} fusion(f32[64,2,32,64]{3,0,2,1:T(8,128)} %fusion.92, f32[2,32,64,64]{3,2,1,0:T(8,128)} %reshape.540), kind=kOutput, calls=%fused_computation.39 | convolution fusion | flops 201646080 | bytes 3145728 | tf_op jit(solution)/shard_map/...nj,nk->...kj/dot_general | solution.py:59
  38.2 2.1 convolution_add_fusion.1
  40.3 2.1 fusion.12
  42.4 3.9 %fusion.10 = f32[2,32,64,64]{3,2,1,0:T(8,128)} fusion(f32[64,2,32,64]{3,0,2,1:T(8,128)S(1)} %convolution_add_fusion.1, f32[64,2,32,64]{3,0,2,1:T(8,128)S(1)} %convolution_subtract_fusion.1, f32[64,64]{1,0:T(8,128)S(1)} %get-tuple-element.25, f32[64,64]{1,0:T(8,128)S(1)} %get-tuple-element.26), kind=kOutput, calls=%fused_computation.18 | convolution fusion | flops 202170368 | bytes 3178496 | tf_op jit(solution)/shard_map/dot_general | solution.py:77
  46.3 3.4 %subtract_bitcast_fusion = f32[1,2,32,64,64]{3,4,2,1,0:T(8,128)} fusion(f32[2,32,64,64]{3,2,1,0:T(8,128)S(1)} %fusion.12, f32[64,2,32,64]{3,0,2,1:T(8,128)S(1)} %convolution_add_fusion.1, f32[64,2,32,64]{3,0,2,1:T(8,128)S(1)} %convolution_subtract_fusion.1, f32[64,64]{1,0:T(8,128)S(1)} %get-tuple-element.25, f32[64,64]{1,0:T(8,128)S(1)} %get-tuple-element.26), kind=kOutput, calls=%fused_computation.35 | convolution fusion | flops 202432512 | bytes 4227072 | tf_op jit(solution)/shard_map/dot_general | solution.py:74
  49.7 3.0 %copy.119 = f32[1,2,32,64,64]{4,3,2,1,0:T(8,128)} copy(f32[1,2,32,64,64]{3,4,2,1,0:T(8,128)} %subtract_bitcast_fusion) | data formatting | bytes 2097152 | tf_op jit(solution)/shard_map/transpose | solution.py:80
  52.7 2.1 reshape.544
  54.8 5.5 %add_bitcast_fusion = f32[1,2,32,64,64]{3,4,2,1,0:T(8,128)} fusion(f32[2,32,64,64]{3,2,1,0:T(8,128)} %fusion.10, f32[64,2,32,64]{3,0,2,1:T(8,128)} %copy-done, f32[64,2,32,64]{3,0,2,1:T(8,128)S(1)} %convolution_subtract_fusion.1, f32[64,64]{1,0:T(8,128)S(1)} %get-tuple-element.25, f32[64,64]{1,0:T(8,128)S(1)} %get-tuple-element.26), kind=kOutput, calls=%fused_computation.34 | convolution fusion | flops 202432512 | bytes 4227072 | tf_op jit(solution)/shard_map/dot_general | solution.py:77
  60.3 1.9 copy.120
  62.2 1.6 reshape.545
  63.9 1.8 multiply_subtract_fusion.1
  65.8 8.4 %copy.121 = f32[1,2,2,32,4096]{3,1,2,0,4:T(2,128)} copy(f32[1,2,2,32,4096]{4,3,1,2,0:T(8,128)S(1)} %pad_maximum_fusion) | data formatting | bytes 4194304 | tf_op jit(solution)/shard_map/stack | solution.py:126
  74.2 10.9 %reshape.578 = f32[32,1,16384]{2,1,0:T(1,128)} reshape(f32[4096,1,2,2,32]{4,3,2,1,0:T(2,128)} %bitcast.361) | data formatting | bytes 4194304
  85.0 8.5 %all-to-all-start = ((f32[32,1,16384]{2,1,0:T(1,128)}), f32[32,1,16384]{2,1,0:T(1,128)S(1)}, u32[]{:S(2)}, u32[]{:S(2)}) async-start(f32[32,1,16384]{2,1,0:T(1,128)} %reshape.578), calls=%async_computation | async-start | bytes 4194304 | tf_op jit(solution)/shard_map/all_to_all | solution.py:127
  95.7 1.6 bitcast_dynamic-update-slice_fusion
  99.3 1.6 bitcast_dynamic-update-slice_fusion.1
  100.9 2.8 %dynamic-slice_cosine_fusion = (f32[4,1,256,128]{3,2,1,0:T(8,128)S(1)}, f32[4,1,256,128]{3,2,1,0:T(8,128)S(1)}) fusion(f32[8,1,256,128]{3,2,1,0:T(8,128)} %bitcast_dynamic-update-slice_fusion.1, s32[]{:T(128)S(6)} %select_n.195), kind=kLoop, calls=%fused_computation.113 | loop fusion | bytes 1572868 | tf_op jit(solution)/shard_map/cos | solution.py:130
  104.3 19.2 %all-to-all-done = f32[32,1,16384]{2,1,0:T(1,128)S(1)} async-done(((f32[32,1,16384]{2,1,0:T(1,128)}), f32[32,1,16384]{2,1,0:T(1,128)S(1)}, u32[]{:S(2)}, u32[]{:S(2)}) %all-to-all-start) | async-done | bytes 2097184 | tf_op jit(solution)/shard_map/all_to_all | solution.py:127
  123.5 1.3 copy-done.6
  125.3 7.4 %reduce.4 = f32[32,16384]{1,0:T(8,128)S(1)} reduce(f32[32,1,16384]{2,1,0:T(1,128)} %copy-done.6, f32[]{:T(128)} %broadcast.762), dimensions={1}, to_apply=%all_to_all.26.reduce_sub_computation | reduce | bytes 4194308 | tf_op jit(solution)/shard_map/all_to_all | solution.py:127
  132.7 8.5 %reshape.579 = f32[4096,1,2,2,32]{4,3,2,1,0:T(2,128)} reshape(f32[32,16384]{1,0:T(8,128)S(1)} %reduce.4) | data formatting | bytes 4194304
  141.2 10.7 %copy.122 = f32[1,2,2,32,4096]{4,0,3,2,1:T(1,128)S(1)} copy(f32[1,2,2,32,4096]{3,1,2,0,4:T(2,128)} %bitcast.362) | data formatting | bytes 4194304 | tf_op jit(solution)/shard_map/all_to_all | solution.py:127
  153.2 1.6 fusion.54
  154.8 1.6 fusion.56
  156.4 1.6 fusion.35
  158.1 2.0 add_bitcast_fusion.2
  160.1 1.7 fusion.50
  161.8 1.7 fusion.48
  163.5 2.2 fusion.34
  165.7 1.8 fusion.33
  170.9 1.6 add_bitcast_fusion.1
  172.5 1.7 fusion.44
  174.3 1.7 fusion.42
  176.0 1.9 fusion.30
  178.5 1.7 fusion.29
  181.2 3.0 %copy.140 = f32[1,2,2,1024,128]{4,1,2,0,3:T(2,128)} copy(f32[1,2,2,1024,128]{4,3,1,2,0:T(8,128)S(1)} %pad_maximum_fusion.1) | data formatting | bytes 4194304 | tf_op jit(solution)/shard_map/stack | solution.py:145
  184.2 4.0 %all-to-all-start.1 = ((f32[1,2,2,1024,128]{4,1,2,0,3:T(2,128)}), f32[1,2,2,1024,128]{4,1,2,0,3:T(2,128)S(1)}, u32[]{:S(2)}, u32[]{:S(2)}) async-start(f32[1,2,2,1024,128]{4,1,2,0,3:T(2,128)} %copy.140), calls=%async_computation.1 | async-start | bytes 4194304 | tf_op jit(solution)/shard_map/all_to_all | solution.py:146
  188.3 29.8 %all-to-all-done.1 = f32[1,2,2,1024,128]{4,1,2,0,3:T(2,128)S(1)} async-done(((f32[1,2,2,1024,128]{4,1,2,0,3:T(2,128)}), f32[1,2,2,1024,128]{4,1,2,0,3:T(2,128)S(1)}, u32[]{:S(2)}, u32[]{:S(2)}) %all-to-all-start.1) | async-done | bytes 2097184 | tf_op jit(solution)/shard_map/all_to_all | solution.py:146
  219.5 6.4 %slice_reduce_fusion = (f32[2,32,4096]{2,1,0:T(8,128)S(1)}, f32[2,32,4096]{2,1,0:T(8,128)}) fusion(f32[1,2,2,32,4096]{4,0,3,2,1:T(1,128)S(1)} %bitcast.369), kind=kLoop, calls=%fused_computation.59 | loop fusion | bytes 4194304 | tf_op jit(solution)/shard_map/slice | solution.py:100
  225.9 2.2 reshape.556
  228.2 3.3 %fusion.102 = f32[64,2,32,64]{3,0,2,1:T(8,128)} fusion(f32[2,32,64,64]{3,2,1,0:T(8,128)S(1)} %reshape.556), kind=kOutput, calls=%fused_computation.151 | convolution fusion | flops 201383936 | bytes 2097152 | tf_op jit(solution)/shard_map/...nj,nk->...kj/dot_general | solution.py:59
  231.5 3.4 %fusion.86 = f32[64,2,32,64]{3,0,2,1:T(8,128)} fusion(f32[2,32,64,64]{3,2,1,0:T(8,128)S(1)} %reshape.556), kind=kOutput, calls=%fused_computation.135 | convolution fusion | flops 201383936 | bytes 2097152 | tf_op jit(solution)/shard_map/...nj,nk->...kj/dot_general | solution.py:62
  234.9 2.2 reshape.557
  237.0 4.4 %convolution_subtract_fusion = f32[64,2,32,64]{3,0,2,1:T(8,128)S(1)} fusion(f32[64,2,32,64]{3,0,2,1:T(8,128)} %fusion.102, f32[2,32,64,64]{3,2,1,0:T(8,128)} %reshape.557), kind=kOutput, calls=%fused_computation.37 | convolution fusion | flops 201646080 | bytes 3145728 | tf_op jit(solution)/shard_map/...nj,nk->...kj/dot_general | solution.py:61
  241.4 2.1 convolution_add_fusion
  243.5 2.1 fusion.2
  245.6 3.6 %fusion = f32[2,32,64,64]{3,2,1,0:T(8,128)} fusion(f32[64,2,32,64]{3,0,2,1:T(8,128)S(1)} %convolution_add_fusion, f32[64,2,32,64]{3,0,2,1:T(8,128)S(1)} %convolution_subtract_fusion, f32[64,64]{1,0:T(8,128)S(1)} %get-tuple-element.31, f32[64,64]{1,0:T(8,128)S(1)} %get-tuple-element.32), kind=kOutput, calls=%fused_computation.4 | convolution fusion | flops 202170368 | bytes 3178496 | tf_op jit(solution)/shard_map/dot_general | solution.py:77
  249.2 3.4 %multiply_bitcast_fusion.1 = f32[1,2,32,64,64]{3,4,2,1,0:T(8,128)} fusion(f32[2,32,64,64]{3,2,1,0:T(8,128)S(1)} %fusion.2, f32[64,2,32,64]{3,0,2,1:T(8,128)S(1)} %convolution_add_fusion, f32[64,2,32,64]{3,0,2,1:T(8,128)S(1)} %convolution_subtract_fusion, f32[64,64]{1,0:T(8,128)S(1)} %get-tuple-element.31, f32[64,64]{1,0:T(8,128)S(1)} %get-tuple-element.32), kind=kOutput, calls=%fused_computation.33 | convolution fusion | flops 202694656 | bytes 4227072 | tf_op jit(solution)/shard_map/dot_general | solution.py:74
  252.6 3.0 %copy.147 = f32[1,2,32,64,64]{4,3,2,1,0:T(8,128)} copy(f32[1,2,32,64,64]{3,4,2,1,0:T(8,128)} %multiply_bitcast_fusion.1) | data formatting | bytes 2097152 | tf_op jit(solution)/shard_map/mul | solution.py:101
  255.6 2.1 mul.1027
  257.7 5.5 %multiply_bitcast_fusion = f32[1,2,32,64,64]{3,4,2,1,0:T(8,128)} fusion(f32[2,32,64,64]{3,2,1,0:T(8,128)} %fusion, f32[64,2,32,64]{3,0,2,1:T(8,128)} %copy-done.1, f32[64,2,32,64]{3,0,2,1:T(8,128)S(1)} %convolution_subtract_fusion, f32[64,64]{1,0:T(8,128)S(1)} %get-tuple-element.31, f32[64,64]{1,0:T(8,128)S(1)} %get-tuple-element.32), kind=kOutput, calls=%fused_computation.32 | convolution fusion | flops 202694656 | bytes 4227072 | tf_op jit(solution)/shard_map/dot_general | solution.py:77
  263.2 1.9 copy.148
  265.2 1.6 mul.1031
  268.0 1.3 copy.149
  (55 shorter events, 17.4 us)
Async XLA Ops:
  0.0 20.5 %copy-start.7 = (f32[1,1,2,2,32,3072]{5,4,3,2,1,0:T(8,128)S(1)}, f32[1,1,2,2,32,3072]{5,4,3,2,1,0:T(8,128)}, u32[]{:S(2)}) copy-start(f32[1,1,2,2,32,3072]{5,4,3,2,1,0:T(8,128)} %param.2) | copy-start | bytes 4718596
  0.0 94.4 %collective-permute-start.1 = (f32[1,256,128]{2,1,0:T(8,128)}, f32[1,256,128]{2,1,0:T(8,128)S(1)}, u32[]{:S(2)}, u32[]{:S(2)}) collective-permute-start(f32[1,256,128]{2,1,0:T(8,128)} %param.3), channel_id=1, source_target_pairs={{1,0},{2,1},{3,2},{0,3},{5,4},{6,5},{7,6},{4,7},{9,8},{10,9},{11,1... | collective-permute-start | bytes 393224 | tf_op jit(solution)/shard_map/ppermute | solution.py:20
  3.1 92.0 %collective-permute-start.2 = (f32[1,256,128]{2,1,0:T(8,128)}, f32[1,256,128]{2,1,0:T(8,128)S(1)}, u32[]{:S(2)}, u32[]{:S(2)}) collective-permute-start(f32[1,256,128]{2,1,0:T(8,128)} %param.3), channel_id=1, source_target_pairs={{2,0},{3,1},{0,2},{1,3},{6,4},{7,5},{4,6},{5,7},{10,8},{11,9},{8,1... | collective-permute-start | bytes 393224 | tf_op jit(solution)/shard_map/ppermute | solution.py:20
  3.7 92.0 %collective-permute-start.3 = (f32[1,256,128]{2,1,0:T(8,128)}, f32[1,256,128]{2,1,0:T(8,128)}, u32[]{:S(2)}, u32[]{:S(2)}) collective-permute-start(f32[1,256,128]{2,1,0:T(8,128)} %param.3), channel_id=1, source_target_pairs={{3,0},{0,1},{1,2},{2,3},{7,4},{4,5},{5,6},{6,7},{11,8},{8,9},{9,10... | collective-permute-start | bytes 393224 | tf_op jit(solution)/shard_map/ppermute | solution.py:20
  5.8 14.7 %collective-permute-start = (f32[1,2,2,32,1024]{4,3,2,1,0:T(8,128)S(1)}, f32[1,2,2,32,1024]{4,3,2,1,0:T(8,128)}, u32[]{:S(2)}, u32[]{:S(2)}) collective-permute-start(f32[1,2,2,32,1024]{4,3,2,1,0:T(8,128)S(1)} %slice.32), channel_id=1, source_target_pairs={{0,1},{1,2},{2,3},{4,5},{5,6},{6,7},{8,9},{9,10},{10,11},{12,13},{... | collective-permute-start | bytes 1572872 | tf_op jit(solution)/shard_map/ppermute | solution.py:12
  33.8 4.4 %copy-start.2 = (f32[2,32,64,64]{3,2,1,0:T(8,128)S(1)}, f32[2,32,64,64]{3,2,1,0:T(8,128)}, u32[]{:S(2)}) copy-start(f32[2,32,64,64]{3,2,1,0:T(8,128)} %reshape.540) | copy-start | bytes 3145732
  33.8 4.4 %copy-start.4 = (f32[64,2,32,64]{3,0,2,1:T(8,128)S(1)}, f32[64,2,32,64]{3,0,2,1:T(8,128)}, u32[]{:S(2)}) copy-start(f32[64,2,32,64]{3,0,2,1:T(8,128)} %fusion.96) | copy-start | bytes 3145732
  40.3 6.0 %copy-start = (f32[64,2,32,64]{3,0,2,1:T(8,128)}, f32[64,2,32,64]{3,0,2,1:T(8,128)S(1)}, u32[]{:S(2)}) copy-start(f32[64,2,32,64]{3,0,2,1:T(8,128)S(1)} %convolution_add_fusion.1) | copy-start | bytes 3145732
  85.0 8.5 %copy-start.10 = (f32[1,256,128]{2,1,0:T(8,128)S(1)}, f32[1,256,128]{2,1,0:T(8,128)}, u32[]{:S(2)}) copy-start(f32[1,256,128]{2,1,0:T(8,128)} %param.3) | copy-start | bytes 393220
  85.0 38.4 %all-to-all-start = ((f32[32,1,16384]{2,1,0:T(1,128)}), f32[32,1,16384]{2,1,0:T(1,128)S(1)}, u32[]{:S(2)}, u32[]{:S(2)}) async-start(f32[32,1,16384]{2,1,0:T(1,128)} %reshape.578), calls=%async_computation | async-start | bytes 4194304 | tf_op jit(solution)/shard_map/all_to_all | solution.py:127
  123.5 1.3 copy-start.6
  178.5 2.4 copy-start.8
  178.5 2.4 copy-start.9
  184.2 34.0 %all-to-all-start.1 = ((f32[1,2,2,1024,128]{4,1,2,0,3:T(2,128)}), f32[1,2,2,1024,128]{4,1,2,0,3:T(2,128)S(1)}, u32[]{:S(2)}, u32[]{:S(2)}) async-start(f32[1,2,2,1024,128]{4,1,2,0,3:T(2,128)} %copy.140), calls=%async_computation.1 | async-start | bytes 4194304 | tf_op jit(solution)/shard_map/all_to_all | solution.py:146
  237.0 4.4 %copy-start.3 = (f32[2,32,64,64]{3,2,1,0:T(8,128)S(1)}, f32[2,32,64,64]{3,2,1,0:T(8,128)}, u32[]{:S(2)}) copy-start(f32[2,32,64,64]{3,2,1,0:T(8,128)} %reshape.557) | copy-start | bytes 3145732
  237.0 4.4 %copy-start.5 = (f32[64,2,32,64]{3,0,2,1:T(8,128)S(1)}, f32[64,2,32,64]{3,0,2,1:T(8,128)}, u32[]{:S(2)}) copy-start(f32[64,2,32,64]{3,0,2,1:T(8,128)} %fusion.86) | copy-start | bytes 3145732
  243.5 5.7 %copy-start.1 = (f32[64,2,32,64]{3,0,2,1:T(8,128)}, f32[64,2,32,64]{3,0,2,1:T(8,128)S(1)}, u32[]{:S(2)}) copy-start(f32[64,2,32,64]{3,0,2,1:T(8,128)S(1)} %convolution_add_fusion) | copy-start | bytes 3145732
where the time goes:
time: 275 us; the launch traced here: 270 us
  local copies, waits for them, and re-layouts  92.5 us (34%)
  matrix products  82 us (30%)
  waiting for transfers between devices  52.8 us (19%)
  starting transfers between devices  21.8 us (8%)
  other arithmetic  19.7 us (7%)
    all_to_all x1, waiting for transfers between devices, per_device(): lax.all_to_all(columns, 'band', split_axis=3, concat_axis=4, tiled=True)  29.8 us
    unnamed x31, local copies, waits for them, and re-layouts  26.3 us
    all_to_all x1, waiting for transfers between devices, per_device(): lax.all_to_all(stacked, 'band', split_axis=4, concat_axis=3, tiled=True)  19.2 us
    dot_general x4, matrix products, transform_last(): jnp.matmul(first_real, sin_inner, precision=highest)  14.5 us
    all_to_all x3, local copies, waits for them, and re-layouts, per_device(): lax.all_to_all(stacked, 'band', split_axis=4, concat_axis=3, tiled=True)  12.4 us
    dot_general x4, matrix products, transform_last(): jnp.einsum('...nj,nk->...kj', imag_part, sin_outer, precision=highest)  11.3 us
    dot_general x4, matrix products, transform_last(): jnp.matmul(first_imag, cos_inner, precision=highest)  10.9 us
    dot_general x4, matrix products, transform_last(): jnp.einsum('...nj,nk->...kj', real_part, cos_outer, precision=highest)  10.5 us
  transfers between devices with their start and end apart: 6, of which 3 were waited for; matrix products, arithmetic and copies ran while one was open for 31% of the time, Pallas kernels for 0%

commit v1 on v0

v1 whole, which is shorter than its diff:
```python
import math

import numpy as np
import jax
import jax.numpy as jnp
from jax import lax
from jax.experimental import pallas as pl
from jax.experimental.pallas import tpu as pltpu
from jax.sharding import PartitionSpec as P

INTERPRET = False
HIGHEST = lax.Precision.HIGHEST
F32 = jnp.float32
ROWS_DEV = 32
COLS = 4096
HIST = 1024
LENGTH = 1024 * 4096


def passed_along(block, axis, distance):
    devices = range(lax.axis_size(axis))
    route = [(i - distance, i) for i in devices if i - distance in devices]
    return lax.ppermute(block, axis, route)


def gathered(block, axis, dim):
    size = lax.axis_size(axis)
    pieces = [block]
    for shift in range(1, size):
        route = [((i + shift) % size, i) for i in range(size)]
        pieces.append(lax.ppermute(block, axis, route))
    ahead = jnp.stack(pieces, axis=0)
    ordered = jnp.roll(ahead, lax.axis_index(axis), axis=0)
    ordered = jnp.moveaxis(ordered, 0, dim)
    shape = list(block.shape)
    shape[dim] *= size
    return ordered.reshape(shape)


def fft_list(xr, xi, sign):
    n = len(xr)
    if n == 1:
        return list(xr), list(xi)
    er, ei = fft_list(xr[0::2], xi[0::2], sign)
    odd_r, odd_i = fft_list(xr[1::2], xi[1::2], sign)
    half = n // 2
    outr = [None] * n
    outi = [None] * n
    for k in range(half):
        a, b = odd_r[k], odd_i[k]
        if k == 0:
            tr, ti = a, b
        elif 4 * k == n:
            tr, ti = (-b, a) if sign > 0 else (b, -a)
        else:
            angle = sign * 2.0 * math.pi * k / n
            c, s = math.cos(angle), math.sin(angle)
            tr = a * c - b * s
            ti = a * s + b * c
        outr[k] = er[k] + tr
        outi[k] = ei[k] + ti
        outr[k + half] = er[k] - tr
        outi[k + half] = ei[k] - ti
    return outr, outi


def unit(m, n, sign):
    angle = (m % n).astype(F32) * F32(sign * 2.0 * math.pi / n)
    return jnp.cos(angle), jnp.sin(angle)


def send_matrices():
    row = np.arange(256)
    dd, pp, ks = row // 8, (row // 4) % 2, row % 4
    k2 = 4 * dd + ks
    col = np.arange(512)
    pin, riin, lane = col // 256, (col // 128) % 2, col % 128
    ang = -2.0 * np.pi * np.outer(k2, lane) / 128.0
    c, s = np.cos(ang), np.sin(ang)
    same = (pp[:, None] == pin[None, :])
    real = np.where(riin[None, :] == 0, c, -s) * same
    imag = np.where(riin[None, :] == 0, s, c) * same
    return real.astype(np.float32), imag.astype(np.float32)


def row_block(sign):
    idx = np.arange(128)
    q, r = idx // 32, idx % 32
    ang = sign * 2.0 * np.pi * np.outer(r, r) / 32.0
    same = q[:, None] == q[None, :]
    wr = np.cos(ang) * same
    wi = np.sin(ang) * same
    top = np.concatenate([wr, wi], axis=1)
    bottom = np.concatenate([-wi, wr], axis=1)
    return np.concatenate([top, bottom], axis=0).astype(np.float32)


def row_twiddle(sign):
    g = np.arange(32)[:, None]
    r = (np.arange(1024) % 32)[None, :]
    ang = sign * 2.0 * np.pi * (g * r) / 1024.0
    return np.cos(ang).astype(np.float32), np.sin(ang).astype(np.float32)


def receive_matrix():
    row = np.arange(512)
    riin, dd, pp, ks = row // 256, (row // 8) % 32, (row // 4) % 2, row % 4
    k2 = 4 * dd + ks
    col = np.arange(512)
    pout, riout, lc = col // 256, (col // 128) % 2, col % 128
    ang = 2.0 * np.pi * np.outer(k2, lc) / 128.0
    c, s = np.cos(ang), np.sin(ang)
    same = pp[:, None] == pout[None, :]
    val = np.where(riin[:, None] == 0,
                   np.where(riout[None, :] == 0, c, s),
                   np.where(riout[None, :] == 0, -s, c))
    return (val * same / LENGTH).astype(np.float32)


def column_twiddle():
    ka = np.arange(32)[:, None]
    lc = (np.arange(256) % 128)[None, :]
    ang = 2.0 * np.pi * (ka * lc) / 4096.0
    return np.cos(ang).astype(np.float32), np.sin(ang).astype(np.float32)


def column_forward_kernel(blk_ref, hist_ref, pre_c, pre_s, lr_ref, li_ref, post_c, post_s, out_ref, xs_ref):
    for p in range(2):
        xr, xi = [], []
        for t in range(32):
            if t < 8:
                xr.append(hist_ref[p, 0, :, t * 128:(t + 1) * 128])
                xi.append(hist_ref[p, 1, :, t * 128:(t + 1) * 128])
            else:
                xr.append(blk_ref[p, 0, :, (t - 8) * 128:(t - 7) * 128])
                xi.append(blk_ref[p, 1, :, (t - 8) * 128:(t - 7) * 128])
        ar, ai = fft_list(xr, xi, -1)
        for k in range(32):
            c = pre_c[k * 32:(k + 1) * 32, :]
            s = pre_s[k * 32:(k + 1) * 32, :]
            xs_ref[k * 32:(k + 1) * 32, p * 256:p * 256 + 128] = ar[k] * c - ai[k] * s
            xs_ref[k * 32:(k + 1) * 32, p * 256 + 128:p * 256 + 256] = ar[k] * s + ai[k] * c
    x = xs_ref[...]
    dims = (((1,), (1,)), ((), ()))
    ore = lax.dot_general(lr_ref[...], x, dims, precision=HIGHEST, preferred_element_type=F32)
    oim = lax.dot_general(li_ref[...], x, dims, precision=HIGHEST, preferred_element_type=F32)
    c = post_c[...]
    s = post_s[...]
    out_ref[:, 0:1024] = ore * c - oim * s
    out_ref[:, 1024:2048] = ore * s + oim * c


def row_kernel(x_ref, twc_ref, tws_ref, bf_ref, bb_ref, chc_ref, chs_ref, post_c, post_s, out_ref, y_ref, w_ref):
    er = [x_ref[8 * d:8 * d + 8, 0:1024] for d in range(32)]
    ei = [x_ref[8 * d:8 * d + 8, 1024:2048] for d in range(32)]
    fr, fi = fft_list(er, ei, -1)
    for g in range(32):
        c = twc_ref[g:g + 1, :]
        s = tws_ref[g:g + 1, :]
        a = fr[g] * c - fi[g] * s
        b = fr[g] * s + fi[g] * c
        for j in range(8):
            y_ref[256 * j + 8 * g:256 * j + 8 * g + 8, 0:128] = a[:, 128 * j:128 * (j + 1)]
            y_ref[256 * j + 8 * g:256 * j + 8 * g + 8, 128:256] = b[:, 128 * j:128 * (j + 1)]
    z = jnp.dot(y_ref[...], bf_ref[...], precision=HIGHEST, preferred_element_type=F32)
    zr = z[:, 0:128]
    zi = z[:, 128:256]
    c = chc_ref[...]
    s = chs_ref[...]
    y_ref[:, 0:128] = zr * c - zi * s
    y_ref[:, 128:256] = zr * s + zi * c
    w_ref[...] = jnp.dot(y_ref[...], bb_ref[...], precision=HIGHEST, preferred_element_type=F32)
    gr, gi = [], []
    for g in range(32):
        a = jnp.concatenate([w_ref[256 * j + 8 * g:256 * j + 8 * g + 8, 0:128] for j in range(8)], axis=1)
        b = jnp.concatenate([w_ref[256 * j + 8 * g:256 * j + 8 * g + 8, 128:256] for j in range(8)], axis=1)
        c = twc_ref[g:g + 1, :]
        s = -tws_ref[g:g + 1, :]
        gr.append(a * c - b * s)
        gi.append(a * s + b * c)
    ur, ui = fft_list(gr, gi, 1)
    for d in range(32):
        c = post_c[8 * d:8 * d + 8, :]
        s = post_s[8 * d:8 * d + 8, :]
        out_ref[8 * d:8 * d + 8, 0:1024] = ur[d] * c - ui[d] * s
        out_ref[8 * d:8 * d + 8, 1024:2048] = ur[d] * s + ui[d] * c


def column_inverse_kernel(x_ref, m_ref, twc_ref, tws_ref, out_ref, s_ref):
    lhs = jnp.concatenate([x_ref[:, 0:1024].T, x_ref[:, 1024:2048].T], axis=1)
    s_ref[...] = jnp.dot(lhs, m_ref[...], precision=HIGHEST, preferred_element_type=F32)
    er, ei = [], []
    for k in range(32):
        rows = slice(32 * k, 32 * (k + 1))
        a = jnp.concatenate([s_ref[rows, 0:128], s_ref[rows, 256:384]], axis=1)
        b = jnp.concatenate([s_ref[rows, 128:256], s_ref[rows, 384:512]], axis=1)
        c = twc_ref[k:k + 1, :]
        s = tws_ref[k:k + 1, :]
        er.append(a * c - b * s)
        ei.append(a * s + b * c)
    tr, ti = fft_list(er, ei, 1)
    for t in range(8, 32):
        for p in range(2):
            out_ref[p, 0, :, (t - 8) * 128:(t - 7) * 128] = tr[t][:, 128 * p:128 * (p + 1)]
            out_ref[p, 1, :, (t - 8) * 128:(t - 7) * 128] = ti[t][:, 128 * p:128 * (p + 1)]


def call(kernel, out_shape, scratch, *args):
    return pl.pallas_call(
        kernel,
        out_shape=jax.ShapeDtypeStruct(out_shape, F32),
        scratch_shapes=[pltpu.VMEM(s, F32) for s in scratch],
        interpret=INTERPRET,
    )(*args)


def per_device(voltages, chirp_phase):
    block = voltages[0, 0]
    band = lax.axis_index("band")
    history = passed_along(block[..., 3072 - HIST:], "seg", 1)
    phases = gathered(chirp_phase, "seg", 1)[0]

    ka = jnp.arange(1024, dtype=jnp.int32)[:, None] // 32
    rl = jnp.arange(1024, dtype=jnp.int32)[:, None] % 32
    lane = jnp.arange(128, dtype=jnp.int32)[None, :]
    pre_c, pre_s = unit(ka * (1024 * lane + 32 * band + rl), LENGTH, -1)
    row = jnp.arange(256, dtype=jnp.int32)[:, None]
    k2 = 4 * (row // 8) + row % 4
    r_lane = jnp.arange(1024, dtype=jnp.int32)[None, :] % 32
    ka_lane = jnp.arange(1024, dtype=jnp.int32)[None, :] // 32
    post_c, post_s = unit(32 * (32 * band + r_lane) * k2, LENGTH, -1)
    back_c, back_s = unit((32 * (row // 8) + r_lane) * (128 * band + ka_lane + 32 * (row % 4)), LENGTH, 1)

    chirp = phases.reshape(32, 32, 4, 8, 4).transpose(3, 1, 2, 4, 0)
    chirp = jnp.broadcast_to(chirp[:, :, None], (8, 32, 2, 4, 4, 32)).reshape(2048, 128)
    ch_c, ch_s = jnp.cos(chirp), jnp.sin(chirp)

    lr, li = send_matrices()
    send = call(column_forward_kernel, (256, 2048), [(1024, 512)],
                block, history, pre_c, pre_s, jnp.asarray(lr), jnp.asarray(li), post_c, post_s)
    received = lax.all_to_all(send.reshape(32, 8, 2048), "band", 0, 0, tiled=True).reshape(256, 2048)

    twc, tws = row_twiddle(-1)
    sent = call(row_kernel, (256, 2048), [(2048, 256), (2048, 256)],
                received, jnp.asarray(twc), jnp.asarray(tws), jnp.asarray(row_block(-1)),
                jnp.asarray(row_block(1)), ch_c, ch_s, back_c, back_s)
    returned = lax.all_to_all(sent.reshape(32, 8, 2048), "band", 0, 0, tiled=True).reshape(256, 2048)

    cc, cs = column_twiddle()
    out = call(column_inverse_kernel, (2, 2, ROWS_DEV, 3072), [(1024, 512)],
               returned, jnp.asarray(receive_matrix()), jnp.asarray(cc), jnp.asarray(cs))
    return out[None, None]


def solution(mesh):
    in_specs = (P("seg", None, None, None, "band", None), P(None, "seg", "band"))
    out_specs = P("seg", None, None, None, "band", None)
    return jax.shard_map(
        per_device, mesh=mesh, in_specs=in_specs, out_specs=out_specs, check_vma=False
    )
```

time: 275 us -> 127 us (0.46); the launches traced: 270 us -> 125 us
  matrix products: 82 us -> 0 us
  local copies, waits for them, and re-layouts: 92.5 us -> 27.6 us
  waiting for transfers between devices: 52.8 us -> 1.38 us
  blocking collectives: 0 us -> 35.8 us
  Pallas kernels: 0 us -> 28.1 us
  starting transfers between devices: 21.8 us -> 17 us
  other arithmetic: 19.7 us -> 15.3 us
    dot_general x32 -> x0, matrix products: 82 us -> none  [the longest x4 14.5 us: transform_last(): jnp.matmul(first_real, sin_inner, precision=highest)]
    all_to_all x2 -> x1, waiting for transfers between devices: 49 us -> 0.01 us  [per_device(): lax.all_to_all(send.reshape(32, 8, 2048), 'band', 0, 0, tiled=True)]
    all_to_all x0 -> x1, blocking collectives: none -> 35.8 us  [per_device(): lax.all_to_all(sent.reshape(32, 8, 2048), 'band', 0, 0, tiled=True)]
    pallas_call x0 -> x3, Pallas kernels: none -> 28.1 us  [call(): pl.pallas_call(kernel, out_shape=jax.ShapeDtypeStruct(out_shape, F32), sc...]
    unnamed x31 -> x11, local copies, waits for them, and re-layouts: 26.3 us -> 0.91 us
    another operation x5 -> x0, local copies, waits for them, and re-layouts: 18 us -> none  [the longest x1 8.36 us: per_device(): stacked = jnp.stack([real_part, imag_part], axis=2)]
    sin x4 -> x3, other arithmetic: 0.46 us -> 15.3 us  [unit(): return (jnp.cos(angle), jnp.sin(angle))]
    all_to_all x5 -> x0, local copies, waits for them, and re-layouts: 13.7 us -> none  [the longest x3 12.4 us: per_device(): lax.all_to_all(stacked, 'band', split_axis=4, concat_axis=3, tiled=True)]
  transfers between devices with their start and end apart: 6 -> 5, of which waited for: 3 -> 1; matrix products, arithmetic and copies ran while one was open for 31% -> 34% of each run, Pallas kernels for 0% -> 7%
where the time goes in v1:
time: 127 us; the launch traced here: 125 us
  blocking collectives  35.8 us (28%)
  Pallas kernels  28.1 us (22%)
  local copies, waits for them, and re-layouts  27.6 us (22%)
  starting transfers between devices  17 us (13%)
  other arithmetic  15.3 us (12%)
  waiting for transfers between devices  1.38 us (1%)
    all_to_all x1, blocking collectives, per_device(): lax.all_to_all(sent.reshape(32, 8, 2048), 'band', 0, 0, tiled=True)  35.8 us
    pallas_call x3, Pallas kernels, call(): pl.pallas_call(kernel, out_shape=jax.ShapeDtypeStruct(out_shape, F32), sc...  28.1 us
    sin x3, other arithmetic, unit(): return (jnp.cos(angle), jnp.sin(angle))  15.3 us
    sin x5, local copies, waits for them, and re-layouts, per_device(): ch_c, ch_s = (jnp.cos(chirp), jnp.sin(chirp))  11 us
    cos x4, local copies, waits for them, and re-layouts, per_device(): ch_c, ch_s = (jnp.cos(chirp), jnp.sin(chirp))  9.17 us
    all_to_all x1, starting transfers between devices, per_device(): lax.all_to_all(send.reshape(32, 8, 2048), 'band', 0, 0, tiled=True)  8.47 us
    broadcast_in_dim x2, local copies, waits for them, and re-layouts, per_device(): jnp.broadcast_to(chirp[:, :, None], (8, 32, 2, 4, 4, 32)).reshape(2048, 128)  5.36 us
    ppermute x3, starting transfers between devices, gathered(): pieces.append(lax.ppermute(block, axis, route))  4.7 us
  transfers between devices with their start and end apart: 5, of which 1 were waited for; matrix products, arithmetic and copies ran while one was open for 34% of the time, Pallas kernels for 7%

profile of v1, /device:TPU:0, one launch (start us, length us, event | category | flops | bytes accessed | tf_op | source)
XLA Modules:
  0.0 125.4 jit_solution(14145168053446135560)
XLA Ops:
  0.0 3.1 %collective-permute-start.1 = (f32[1,256,128]{2,1,0:T(8,128)}, f32[1,256,128]{2,1,0:T(8,128)S(1)}, u32[]{:S(2)}, u32[]{:S(2)}) collective-permute-start(f32[1,256,128]{2,1,0:T(8,128)} %param.12), channel_id=1, source_target_pairs={{1,0},{2,1},{3,2},{0,3},{5,4},{6,5},{7,6},{4,7},{9,8},{10,9},{11,1... | collective-permute-start | bytes 393224 | tf_op jit(solution)/shard_map/ppermute | solution.py:31
  3.1 0.6 collective-permute-start.2
  3.7 1.0 collective-permute-start.3
  4.7 1.1 slice.4
  5.8 3.8 %collective-permute-start = (f32[2,2,32,1024]{3,2,1,0:T(8,128)S(1)}, f32[2,2,32,1024]{3,2,1,0:T(8,128)S(1)}, u32[]{:S(2)}, u32[]{:S(2)}) collective-permute-start(f32[2,2,32,1024]{3,2,1,0:T(8,128)S(1)} %slice.4), channel_id=1, source_target_pairs={{0,1},{1,2},{2,3},{4,5},{5,6},{6,7},{8,9},{9,10},{10,11},{12,13},{... | collective-permute-start | bytes 1572872 | tf_op jit(solution)/shard_map/ppermute | solution.py:23
  9.7 3.6 %fusion.13 = (f32[1024,128]{1,0:T(8,128)}, f32[1024,128]{1,0:T(8,128)}) fusion(s32[1024]{0:T(1024)S(1)} %get-tuple-element.13, s32[128]{0:T(128)S(1)} %multiply_add_fusion.1, s32[1024]{0:T(1024)S(1)} %get-tuple-element.14), kind=kLoop, calls=%fused_computation.26 | loop fusion | flops 1966080 | bytes 1057280 | tf_op jit(solution)/shard_map/sin | solution.py:69
  13.3 5.7 %fusion.11 = (f32[256,1024]{1,0:T(8,128)}, f32[256,1024]{1,0:T(8,128)}) fusion(s32[256]{0:T(256)S(1)} %multiply_add_fusion, s32[1024]{0:T(1024)S(1)} %add_multiply_fusion), kind=kLoop, calls=%fused_computation.22 | loop fusion | flops 3670016 | bytes 2102272 | tf_op jit(solution)/shard_map/sin | solution.py:69
  19.1 1.4 %collective-permute-done.hist_ref = f32[2,2,32,1024]{3,2,1,0:T(8,128)S(1)} collective-permute-done((f32[2,2,32,1024]{3,2,1,0:T(8,128)S(1)}, f32[2,2,32,1024]{3,2,1,0:T(8,128)S(1)}, u32[]{:S(2)}, u32[]{:S(2)}) %collective-permute-start) | collective-permute-done | bytes 524320 | tf_op jit(solution)/shard_map/ppermute | solution.py:23
  20.5 0.0 copy-start
  20.5 0.8 copy-done
  21.3 8.6 %shard_map.109 = f32[256,2048]{1,0:T(8,128)} custom-call(f32[2,2,32,3072]{3,2,1,0:T(8,128)} %bitcast.30, f32[2,2,32,1024]{3,2,1,0:T(8,128)} %copy-done, f32[1024,128]{1,0:T(8,128)} %get-tuple-element.10.pre_c, f32[1024,128]{1,0:T(8,128)} %get-tuple-element.9.pre_s, f32[256,512]{1,0:T(8,128)} %constant.169.clone.lr_ref, f32[256,512]{1,0:T(8,128)} %constant.170.clone.li_ref, ...), custom_call_target="tpu_custom_call" | custom-call | tf_op jit(solution)/shard_map/pallas_call | solution.py:209
  29.9 8.5 %all-to-all-start = ((f32[32,8,2048]{2,1,0:T(8,128)}), f32[32,8,2048]{2,1,0:T(8,128)}, u32[]{:S(2)}, u32[]{:S(2)}) async-start(f32[32,8,2048]{2,1,0:T(8,128)} %bitcast.27), calls=%async_computation | async-start | bytes 4194304 | tf_op jit(solution)/shard_map/all_to_all | solution.py:241
  38.3 0.0 copy-start.1
  38.4 5.9 %fusion.6 = (f32[256,1024]{1,0:T(8,128)}, f32[256,1024]{1,0:T(8,128)}) fusion(s32[256]{0:T(256)S(1)} %get-tuple-element.15, s32[1024]{0:T(1024)S(1)} %broadcast_add_fusion, s32[1024]{0:T(1024)S(1)} %get-tuple-element.13, s32[256]{0:T(256)S(1)} %get-tuple-element.16), kind=kLoop, calls=%fused_computation.17 | loop fusion | flops 4194304 | bytes 2107392 | tf_op jit(solution)/shard_map/sin | solution.py:69
  44.2 0.0 copy-done.1
  44.2 0.0 collective-permute-done.1
  44.3 0.0 collective-permute-done.2
  44.3 0.0 collective-permute-done.3
  44.4 1.9 %dynamic-slice_sine_fusion = (f32[4,1,256,128]{3,2,1,0:T(8,128)S(1)}, f32[4,1,256,128]{3,2,1,0:T(8,128)S(1)}) fusion(f32[8,1,256,128]{3,2,1,0:T(8,128)S(1)} %bitcast_dynamic-update-slice_fusion.1, s32[]{:T(128)S(6)} %select_n.117), kind=kLoop, calls=%fused_computation.24 | loop fusion | bytes 1572868 | tf_op jit(solution)/shard_map/sin | solution.py:236
  46.3 0.2 copy.14
  46.5 1.9 %cos.21 = f32[32,32,4,8,4]{1,0,4,3,2:T(8,128)} reshape(f32[4,1,256,128]{2,0,3,1:T(4,128)S(1)} %copy.14) | data formatting | bytes 1048576 | tf_op jit(solution)/shard_map/cos | solution.py:236
  48.4 2.5 %copy.15 = f32[8,32,4,4,32]{4,3,2,1,0:T(4,128)S(1)} copy(f32[8,32,4,4,32]{1,4,3,0,2:T(8,128)} %bitcast.25) | data formatting | bytes 1048576 | tf_op jit(solution)/shard_map/cos | solution.py:236
  50.9 2.7 %broadcast_in_dim.6 = f32[8,32,2,4,4,32]{5,4,3,2,1,0:T(4,128)} broadcast(f32[8,32,4,4,32]{4,3,2,1,0:T(4,128)S(1)} %copy.15), dimensions={0,1,3,4,5} | broadcast | bytes 1572864 | tf_op jit(solution)/shard_map/broadcast_in_dim | solution.py:235
  53.6 4.5 %cos.23.chc_ref = f32[2048,128]{1,0:T(8,128)} reshape(f32[8,32,2,4,4,32]{5,4,3,2,1,0:T(4,128)} %broadcast_in_dim.6) | data formatting | bytes 2097152 | tf_op jit(solution)/shard_map/cos | solution.py:236
  58.2 0.2 copy.16
  58.4 1.9 %sin.21 = f32[32,32,4,8,4]{1,0,4,3,2:T(8,128)} reshape(f32[4,1,256,128]{2,0,3,1:T(4,128)S(1)} %copy.16) | data formatting | bytes 1048576 | tf_op jit(solution)/shard_map/sin | solution.py:236
  60.3 2.5 %copy.17 = f32[8,32,4,4,32]{4,3,2,1,0:T(4,128)S(1)} copy(f32[8,32,4,4,32]{1,4,3,0,2:T(8,128)} %bitcast.26) | data formatting | bytes 1048576 | tf_op jit(solution)/shard_map/sin | solution.py:236
  62.8 2.7 %broadcast_in_dim.7 = f32[8,32,2,4,4,32]{5,4,3,2,1,0:T(4,128)} broadcast(f32[8,32,4,4,32]{4,3,2,1,0:T(4,128)S(1)} %copy.17), dimensions={0,1,3,4,5} | broadcast | bytes 1572864 | tf_op jit(solution)/shard_map/broadcast_in_dim | solution.py:235
  65.5 4.5 %sin.23.chs_ref = f32[2048,128]{1,0:T(8,128)} reshape(f32[8,32,2,4,4,32]{5,4,3,2,1,0:T(4,128)} %broadcast_in_dim.7) | data formatting | bytes 2097152 | tf_op jit(solution)/shard_map/sin | solution.py:236
  70.0 0.0 all-to-all-done
  70.0 12.5 %shard_map.110 = f32[256,2048]{1,0:T(8,128)} custom-call(f32[256,2048]{1,0:T(8,128)} %bitcast.2.x_ref, f32[32,1024]{1,0:T(8,128)} %constant.171.clone.twc_ref, f32[32,1024]{1,0:T(8,128)} %constant.172.clone.tws_ref, f32[256,256]{1,0:T(8,128)} %constant.173.clone.bf_ref, f32[256,256]{1,0:T(8,128)} %constant.174.clone.bb_ref, f32[2048,128]{1,0:T(8,128)} %cos.23.chc_ref, ...), custom_call_target="tpu_custom_call" | custom-call | tf_op jit(solution)/shard_map/pallas_call | solution.py:209
  82.5 35.8 %all_to_all.10 = f32[32,8,2048]{2,1,0:T(8,128)} all-to-all(f32[32,8,2048]{2,1,0:T(8,128)} %bitcast.28), channel_id=1, replica_groups=mesh['band'=32,'seg'=4] {'band'}, dimensions={0} | all-to-all | bytes 4194304 | tf_op jit(solution)/shard_map/all_to_all | solution.py:247
  118.3 7.1 %shard_map.111 = f32[2,2,32,3072]{3,2,1,0:T(8,128)} custom-call(f32[256,2048]{1,0:T(8,128)} %bitcast.24, f32[512,512]{1,0:T(8,128)} %constant.175.clone.m_ref, f32[32,256]{1,0:T(8,128)} %constant.176.clone.twc_ref, f32[32,256]{1,0:T(8,128)} %constant.177.clone.tws_ref), custom_call_target="tpu_custom_call" | custom-call | tf_op jit(solution)/shard_map/pallas_call | solution.py:209
  (14 shorter events, 0.1 us)
Async XLA Ops:
  0.0 44.2 %collective-permute-start.1 = (f32[1,256,128]{2,1,0:T(8,128)}, f32[1,256,128]{2,1,0:T(8,128)S(1)}, u32[]{:S(2)}, u32[]{:S(2)}) collective-permute-start(f32[1,256,128]{2,1,0:T(8,128)} %param.12), channel_id=1, source_target_pairs={{1,0},{2,1},{3,2},{0,3},{5,4},{6,5},{7,6},{4,7},{9,8},{10,9},{11,1... | collective-permute-start | bytes 393224 | tf_op jit(solution)/shard_map/ppermute | solution.py:31
  3.1 41.2 %collective-permute-start.2 = (f32[1,256,128]{2,1,0:T(8,128)}, f32[1,256,128]{2,1,0:T(8,128)S(1)}, u32[]{:S(2)}, u32[]{:S(2)}) collective-permute-start(f32[1,256,128]{2,1,0:T(8,128)} %param.12), channel_id=1, source_target_pairs={{2,0},{3,1},{0,2},{1,3},{6,4},{7,5},{4,6},{5,7},{10,8},{11,9},{8,1... | collective-permute-start | bytes 393224 | tf_op jit(solution)/shard_map/ppermute | solution.py:31
  3.7 40.6 %collective-permute-start.3 = (f32[1,256,128]{2,1,0:T(8,128)}, f32[1,256,128]{2,1,0:T(8,128)S(1)}, u32[]{:S(2)}, u32[]{:S(2)}) collective-permute-start(f32[1,256,128]{2,1,0:T(8,128)} %param.12), channel_id=1, source_target_pairs={{3,0},{0,1},{1,2},{2,3},{7,4},{4,5},{5,6},{6,7},{11,8},{8,9},{9,10... | collective-permute-start | bytes 393224 | tf_op jit(solution)/shard_map/ppermute | solution.py:31
  5.8 14.7 %collective-permute-start = (f32[2,2,32,1024]{3,2,1,0:T(8,128)S(1)}, f32[2,2,32,1024]{3,2,1,0:T(8,128)S(1)}, u32[]{:S(2)}, u32[]{:S(2)}) collective-permute-start(f32[2,2,32,1024]{3,2,1,0:T(8,128)S(1)} %slice.4), channel_id=1, source_target_pairs={{0,1},{1,2},{2,3},{4,5},{5,6},{6,7},{8,9},{9,10},{10,11},{12,13},{... | collective-permute-start | bytes 1572872 | tf_op jit(solution)/shard_map/ppermute | solution.py:23
  20.5 0.8 copy-start
  29.9 40.2 %all-to-all-start = ((f32[32,8,2048]{2,1,0:T(8,128)}), f32[32,8,2048]{2,1,0:T(8,128)}, u32[]{:S(2)}, u32[]{:S(2)}) async-start(f32[32,8,2048]{2,1,0:T(8,128)} %bitcast.27), calls=%async_computation | async-start | bytes 4194304 | tf_op jit(solution)/shard_map/all_to_all | solution.py:241
  38.3 5.9 %copy-start.1 = (f32[1,256,128]{2,1,0:T(8,128)S(1)}, f32[1,256,128]{2,1,0:T(8,128)}, u32[]{:S(2)}) copy-start(f32[1,256,128]{2,1,0:T(8,128)} %param.12) | copy-start | bytes 393220

commit v2 on v1

v2 whole, which is shorter than its diff:
```python
import math

import numpy as np
import jax
import jax.numpy as jnp
from jax import lax
from jax.experimental import pallas as pl
from jax.experimental.pallas import tpu as pltpu
from jax.sharding import PartitionSpec as P

INTERPRET = False
HIGHEST = lax.Precision.HIGHEST
F32 = jnp.float32
ROWS_DEV = 32
COLS = 4096
HIST = 1024
LENGTH = 1024 * 4096


def passed_along(block, axis, distance):
    devices = range(lax.axis_size(axis))
    route = [(i - distance, i) for i in devices if i - distance in devices]
    return lax.ppermute(block, axis, route)


def gathered(block, axis, dim):
    size = lax.axis_size(axis)
    pieces = [block]
    for shift in range(1, size):
        route = [((i + shift) % size, i) for i in range(size)]
        pieces.append(lax.ppermute(block, axis, route))
    ahead = jnp.stack(pieces, axis=0)
    ordered = jnp.roll(ahead, lax.axis_index(axis), axis=0)
    ordered = jnp.moveaxis(ordered, 0, dim)
    shape = list(block.shape)
    shape[dim] *= size
    return ordered.reshape(shape)


def fft_list(xr, xi, sign):
    n = len(xr)
    if n == 1:
        return list(xr), list(xi)
    er, ei = fft_list(xr[0::2], xi[0::2], sign)
    odd_r, odd_i = fft_list(xr[1::2], xi[1::2], sign)
    half = n // 2
    outr = [None] * n
    outi = [None] * n
    for k in range(half):
        a, b = odd_r[k], odd_i[k]
        if k == 0:
            tr, ti = a, b
        elif 4 * k == n:
            tr, ti = (-b, a) if sign > 0 else (b, -a)
        else:
            angle = sign * 2.0 * math.pi * k / n
            c, s = math.cos(angle), math.sin(angle)
            tr = a * c - b * s
            ti = a * s + b * c
        outr[k] = er[k] + tr
        outi[k] = ei[k] + ti
        outr[k + half] = er[k] - tr
        outi[k + half] = ei[k] - ti
    return outr, outi


def unit(m, n, sign):
    angle = (m % n).astype(F32) * F32(sign * 2.0 * math.pi / n)
    return jnp.cos(angle), jnp.sin(angle)


def send_matrices():
    row = np.arange(256)
    dd, pp, ks = row // 8, (row // 4) % 2, row % 4
    k2 = 4 * dd + ks
    col = np.arange(512)
    pin, riin, lane = col // 256, (col // 128) % 2, col % 128
    ang = -2.0 * np.pi * np.outer(k2, lane) / 128.0
    c, s = np.cos(ang), np.sin(ang)
    same = (pp[:, None] == pin[None, :])
    real = np.where(riin[None, :] == 0, c, -s) * same
    imag = np.where(riin[None, :] == 0, s, c) * same
    return real.astype(np.float32), imag.astype(np.float32)


def row_block(sign):
    idx = np.arange(128)
    q, r = idx // 32, idx % 32
    ang = sign * 2.0 * np.pi * np.outer(r, r) / 32.0
    same = q[:, None] == q[None, :]
    wr = np.cos(ang) * same
    wi = np.sin(ang) * same
    top = np.concatenate([wr, wi], axis=1)
    bottom = np.concatenate([-wi, wr], axis=1)
    return np.concatenate([top, bottom], axis=0).astype(np.float32)


def row_twiddle(sign):
    g = np.arange(32)[:, None]
    r = (np.arange(512) % 32)[None, :]
    ang = sign * 2.0 * np.pi * (g * r) / 1024.0
    return np.cos(ang).astype(np.float32), np.sin(ang).astype(np.float32)


def receive_matrix():
    row = np.arange(512)
    riin, dd, pp, ks = row // 256, (row // 8) % 32, (row // 4) % 2, row % 4
    k2 = 4 * dd + ks
    col = np.arange(512)
    pout, riout, lc = col // 256, (col // 128) % 2, col % 128
    ang = 2.0 * np.pi * np.outer(k2, lc) / 128.0
    c, s = np.cos(ang), np.sin(ang)
    same = pp[:, None] == pout[None, :]
    val = np.where(riin[:, None] == 0,
                   np.where(riout[None, :] == 0, c, s),
                   np.where(riout[None, :] == 0, -s, c))
    return (val * same / LENGTH).astype(np.float32)


def lane_twiddle(sign, width):
    ka = np.arange(32)[:, None]
    lc = (np.arange(width) % 128)[None, :]
    ang = sign * 2.0 * np.pi * (ka * lc) / 4096.0
    return np.cos(ang).astype(np.float32), np.sin(ang).astype(np.float32)


def cmul(ar, ai, br, bi):
    return ar * br - ai * bi, ar * bi + ai * br


def column_forward_kernel(blk_ref, hist_ref, t1c, t1s, t2c, t2s, lr_ref, li_ref, pac, pas, pbc, pbs,
                          out0_ref, out1_ref, xs_ref):
    for p in range(2):
        xr, xi = [], []
        for t in range(32):
            if t < 8:
                xr.append(hist_ref[p, 0, :, t * 128:(t + 1) * 128])
                xi.append(hist_ref[p, 1, :, t * 128:(t + 1) * 128])
            else:
                xr.append(blk_ref[p, 0, :, (t - 8) * 128:(t - 7) * 128])
                xi.append(blk_ref[p, 1, :, (t - 8) * 128:(t - 7) * 128])
        ar, ai = fft_list(xr, xi, -1)
        for k in range(32):
            wc, ws = cmul(t1c[k:k + 1, :], t1s[k:k + 1, :], t2c[:, k:k + 1], t2s[:, k:k + 1])
            re, im = cmul(ar[k], ai[k], wc, ws)
            xs_ref[k * 32:(k + 1) * 32, p * 256:p * 256 + 128] = re
            xs_ref[k * 32:(k + 1) * 32, p * 256 + 128:p * 256 + 256] = im
    dims = (((1,), (1,)), ((), ()))
    for h, out_ref in enumerate((out0_ref, out1_ref)):
        x = xs_ref[512 * h:512 * (h + 1), :]
        ore = lax.dot_general(lr_ref[...], x, dims, precision=HIGHEST, preferred_element_type=F32)
        oim = lax.dot_general(li_ref[...], x, dims, precision=HIGHEST, preferred_element_type=F32)
        ac = pac[:, 512 * h:512 * (h + 1)]
        as_ = pas[:, 512 * h:512 * (h + 1)]
        for d in range(32):
            bc = pbc[d:d + 1, 512 * h:512 * (h + 1)]
            bs = pbs[d:d + 1, 512 * h:512 * (h + 1)]
            wc, ws = cmul(ac, as_, bc, bs)
            re, im = cmul(ore[8 * d:8 * d + 8], oim[8 * d:8 * d + 8], wc, ws)
            out_ref[8 * d:8 * d + 8, 0:512] = re
            out_ref[8 * d:8 * d + 8, 512:1024] = im


def row_kernel(x_ref, twc_ref, tws_ref, bf_ref, bb_ref, ph_ref, ac_ref, as_ref, bc_ref, bs_ref, cc_ref, cs_ref,
               out_ref, y_ref, w_ref):
    er = [x_ref[8 * d:8 * d + 8, 0:512] for d in range(32)]
    ei = [x_ref[8 * d:8 * d + 8, 512:1024] for d in range(32)]
    fr, fi = fft_list(er, ei, -1)
    for g in range(32):
        a, b = cmul(fr[g], fi[g], twc_ref[g:g + 1, :], tws_ref[g:g + 1, :])
        for j in range(4):
            y_ref[256 * j + 8 * g:256 * j + 8 * g + 8, 0:128] = a[:, 128 * j:128 * (j + 1)]
            y_ref[256 * j + 8 * g:256 * j + 8 * g + 8, 128:256] = b[:, 128 * j:128 * (j + 1)]
    z = jnp.dot(y_ref[...], bf_ref[...], precision=HIGHEST, preferred_element_type=F32)
    phase = ph_ref[...]
    re, im = cmul(z[:, 0:128], z[:, 128:256], jnp.cos(phase), jnp.sin(phase))
    y_ref[:, 0:128] = re
    y_ref[:, 128:256] = im
    w_ref[...] = jnp.dot(y_ref[...], bb_ref[...], precision=HIGHEST, preferred_element_type=F32)
    gr, gi = [], []
    for g in range(32):
        a = jnp.concatenate([w_ref[256 * j + 8 * g:256 * j + 8 * g + 8, 0:128] for j in range(4)], axis=1)
        b = jnp.concatenate([w_ref[256 * j + 8 * g:256 * j + 8 * g + 8, 128:256] for j in range(4)], axis=1)
        a, b = cmul(a, b, twc_ref[g:g + 1, :], -tws_ref[g:g + 1, :])
        gr.append(a)
        gi.append(b)
    ur, ui = fft_list(gr, gi, 1)
    ac = ac_ref[...]
    as_ = as_ref[...]
    for d in range(32):
        wc, ws = cmul(bc_ref[d:d + 1, :], bs_ref[d:d + 1, :], cc_ref[8 * d:8 * d + 8, 0:1], cs_ref[8 * d:8 * d + 8, 0:1])
        wc, ws = cmul(wc, ws, ac, as_)
        re, im = cmul(ur[d], ui[d], wc, ws)
        out_ref[8 * d:8 * d + 8, 0:512] = re
        out_ref[8 * d:8 * d + 8, 512:1024] = im


def column_inverse_kernel(x0_ref, x1_ref, m_ref, twc_ref, tws_ref, out_ref, s_ref):
    lhs_re = jnp.concatenate([x0_ref[:, 0:512].T, x1_ref[:, 0:512].T], axis=0)
    lhs_im = jnp.concatenate([x0_ref[:, 512:1024].T, x1_ref[:, 512:1024].T], axis=0)
    lhs = jnp.concatenate([lhs_re, lhs_im], axis=1)
    s_ref[...] = jnp.dot(lhs, m_ref[...], precision=HIGHEST, preferred_element_type=F32)
    er, ei = [], []
    for k in range(32):
        rows = slice(32 * k, 32 * (k + 1))
        a = jnp.concatenate([s_ref[rows, 0:128], s_ref[rows, 256:384]], axis=1)
        b = jnp.concatenate([s_ref[rows, 128:256], s_ref[rows, 384:512]], axis=1)
        a, b = cmul(a, b, twc_ref[k:k + 1, :], tws_ref[k:k + 1, :])
        er.append(a)
        ei.append(b)
    tr, ti = fft_list(er, ei, 1)
    for t in range(8, 32):
        for p in range(2):
            out_ref[p, 0, :, (t - 8) * 128:(t - 7) * 128] = tr[t][:, 128 * p:128 * (p + 1)]
            out_ref[p, 1, :, (t - 8) * 128:(t - 7) * 128] = ti[t][:, 128 * p:128 * (p + 1)]


def call(kernel, out_shapes, scratch, *args):
    return pl.pallas_call(
        kernel,
        out_shape=[jax.ShapeDtypeStruct(s, F32) for s in out_shapes],
        scratch_shapes=[pltpu.VMEM(s, F32) for s in scratch],
        interpret=INTERPRET,
    )(*args)


def exchanged(block):
    rows, width = block.shape
    out = lax.all_to_all(block.reshape(32, rows // 32, width), "band", 0, 0, tiled=True)
    return out.reshape(rows, width)


def per_device(voltages, chirp_phase):
    block = voltages[0, 0]
    band = lax.axis_index("band")
    history = passed_along(block[..., 3072 - HIST:], "seg", 1)
    phases = gathered(chirp_phase, "seg", 1)[0]
    chirp = phases.reshape(32, 32, 4, 8, 4).transpose(3, 1, 2, 4, 0)
    chirp = jnp.broadcast_to(chirp[:, :, None], (8, 32, 2, 4, 4, 32)).reshape(2048, 128)

    i32 = jnp.int32
    lane = jnp.arange(1024, dtype=i32)[None, :]
    r_lane = 32 * band + lane % 32
    ka_lane = lane // 32
    t2c, t2s = unit(jnp.arange(32, dtype=i32)[None, :] * (32 * band + jnp.arange(32, dtype=i32)[:, None]), LENGTH, -1)
    q = jnp.arange(8, dtype=i32)[:, None]
    dd = jnp.arange(32, dtype=i32)[:, None]
    pac, pas = unit(32 * r_lane * (q % 4), LENGTH, -1)
    pbc, pbs = unit(128 * r_lane * dd, LENGTH, -1)
    kc_lane = 128 * band + ka_lane
    rl_lane = lane % 32
    bac, bas = unit(rl_lane * (kc_lane + 32 * (q % 4)), LENGTH, 1)
    bbc, bbs = unit(32 * dd * kc_lane, LENGTH, 1)
    rows = jnp.arange(256, dtype=i32)[:, None]
    bcc, bcs = unit(jnp.broadcast_to(1024 * (rows // 8) * (rows % 4), (256, 128)), LENGTH, 1)

    t1c, t1s = lane_twiddle(-1, 128)
    lr, li = send_matrices()
    send0, send1 = call(column_forward_kernel, [(256, 1024), (256, 1024)], [(1024, 512)],
                        block, history, jnp.asarray(t1c), jnp.asarray(t1s), t2c, t2s,
                        jnp.asarray(lr), jnp.asarray(li), pac, pas, pbc, pbs)

    twc, tws = row_twiddle(-1)
    fwd, bwd = jnp.asarray(row_block(-1)), jnp.asarray(row_block(1))
    back = []
    for h, send in enumerate((send0, send1)):
        received = exchanged(send)
        lanes = slice(512 * h, 512 * (h + 1))
        (sent,) = call(row_kernel, [(256, 1024)], [(1024, 256), (1024, 256)],
                       received, jnp.asarray(twc), jnp.asarray(tws), fwd, bwd,
                       chirp[1024 * h:1024 * (h + 1)], bac[:, lanes], bas[:, lanes],
                       bbc[:, lanes], bbs[:, lanes], bcc, bcs)
        back.append(exchanged(sent))

    cc, cs = lane_twiddle(1, 256)
    (out,) = call(column_inverse_kernel, [(2, 2, ROWS_DEV, 3072)], [(1024, 512)],
                  back[0], back[1], jnp.asarray(receive_matrix()), jnp.asarray(cc), jnp.asarray(cs))
    return out[None, None]


def solution(mesh):
    in_specs = (P("seg", None, None, None, "band", None), P(None, "seg", "band"))
    out_specs = P("seg", None, None, None, "band", None)
    return jax.shard_map(
        per_device, mesh=mesh, in_specs=in_specs, out_specs=out_specs, check_vma=False
    )
```

time: 127 us -> 130 us (1.024)
  waiting for transfers between devices: 1.38 us -> 28.6 us
  local copies, waits for them, and re-layouts: 27.6 us -> 13.5 us
  blocking collectives: 35.8 us -> 22 us
  starting transfers between devices: 17 us -> 27.3 us
  other arithmetic: 15.3 us -> 5.02 us
  Pallas kernels: 28.1 us -> 31.6 us
    all_to_all x1 -> x3, waiting for transfers between devices: 0.01 us -> 24.5 us  [exchanged(): lax.all_to_all(block.reshape(32, rows // 32, width), 'band', 0, 0, tiled=...]
    all_to_all x1, blocking collectives: 35.8 us -> 22 us  [exchanged(): lax.all_to_all(block.reshape(32, rows // 32, width), 'band', 0, 0, tiled=...]
    sin x5 -> x0, local copies, waits for them, and re-layouts: 11 us -> none  [per_device(): ch_c, ch_s = (jnp.cos(chirp), jnp.sin(chirp))]
    sin x3 -> x6, other arithmetic: 15.3 us -> 4.96 us  [unit(): return (jnp.cos(angle), jnp.sin(angle))]
    all_to_all x1 -> x3, starting transfers between devices: 8.47 us -> 18.7 us  [exchanged(): lax.all_to_all(block.reshape(32, rows // 32, width), 'band', 0, 0, tiled=...]
    cos x4 -> x0, local copies, waits for them, and re-layouts: 9.17 us -> none  [per_device(): ch_c, ch_s = (jnp.cos(chirp), jnp.sin(chirp))]
    slice x0 -> x7, local copies, waits for them, and re-layouts: none -> 7.12 us  [the longest x5 5.76 us: per_device(): chirp[1024 * h:1024 * (h + 1)]]
    broadcast_in_dim x2, local copies, waits for them, and re-layouts: 5.36 us -> 0.71 us  [per_device(): jnp.broadcast_to(chirp[:, :, None], (8, 32, 2, 4, 4, 32)).reshape(2048, 128)]
  transfers between devices with their start and end apart: 5 -> 7, of which waited for: 1 -> 4; matrix products, arithmetic and copies ran while one was open for 34% -> 14% of each run, Pallas kernels for 7% -> 19%
where the time goes in v2:
time: 130 us; the launch traced here: 128 us
  Pallas kernels  31.6 us (24%)
  waiting for transfers between devices  28.6 us (22%)
  starting transfers between devices  27.3 us (21%)
  blocking collectives  22 us (17%)
  local copies, waits for them, and re-layouts  13.5 us (10%)
  other arithmetic  5.02 us (4%)
    pallas_call x4, Pallas kernels, call(): pl.pallas_call(kernel, out_shape=[jax.ShapeDtypeStruct(s, F32) for s in o...  31.6 us
    all_to_all x3, waiting for transfers between devices, exchanged(): lax.all_to_all(block.reshape(32, rows // 32, width), 'band', 0, 0, tiled=...  24.5 us
    all_to_all x1, blocking collectives, exchanged(): lax.all_to_all(block.reshape(32, rows // 32, width), 'band', 0, 0, tiled=...  22 us
    all_to_all x3, starting transfers between devices, exchanged(): lax.all_to_all(block.reshape(32, rows // 32, width), 'band', 0, 0, tiled=...  18.7 us
    slice x5, local copies, waits for them, and re-layouts, per_device(): chirp[1024 * h:1024 * (h + 1)]  5.76 us
    sin x6, other arithmetic, unit(): return (jnp.cos(angle), jnp.sin(angle))  4.96 us
    ppermute x3, starting transfers between devices, gathered(): pieces.append(lax.ppermute(block, axis, route))  4.7 us
    ppermute x1, waiting for transfers between devices, passed_along(): return lax.ppermute(block, axis, route)  4.12 us
  transfers between devices with their start and end apart: 7, of which 4 were waited for; matrix products, arithmetic and copies ran while one was open for 14% of the time, Pallas kernels for 19%

profile of v2, /device:TPU:0, one launch (start us, length us, event | category | flops | bytes accessed | tf_op | source)
XLA Modules:
  0.0 128.1 jit_solution(11938453222980291763)
XLA Ops:
  0.0 3.1 %collective-permute-start.1 = (f32[1,256,128]{2,1,0:T(8,128)}, f32[1,256,128]{2,1,0:T(8,128)S(1)}, u32[]{:S(2)}, u32[]{:S(2)}) collective-permute-start(f32[1,256,128]{2,1,0:T(8,128)} %param.14), channel_id=1, source_target_pairs={{1,0},{2,1},{3,2},{0,3},{5,4},{6,5},{7,6},{4,7},{9,8},{10,9},{11,1... | collective-permute-start | bytes 393224 | tf_op jit(solution)/shard_map/ppermute | solution.py:31
  3.1 0.6 collective-permute-start.2
  3.7 1.0 collective-permute-start.3
  4.7 1.1 slice.54
  5.8 3.8 %collective-permute-start = (f32[2,2,32,1024]{3,2,1,0:T(8,128)S(1)}, f32[2,2,32,1024]{3,2,1,0:T(8,128)S(1)}, u32[]{:S(2)}, u32[]{:S(2)}) collective-permute-start(f32[2,2,32,1024]{3,2,1,0:T(8,128)S(1)} %slice.54), channel_id=1, source_target_pairs={{0,1},{1,2},{2,3},{4,5},{5,6},{6,7},{8,9},{9,10},{10,11},{12,13},{... | collective-permute-start | bytes 1572872 | tf_op jit(solution)/shard_map/ppermute | solution.py:23
  9.6 0.9 bitcast_dynamic-update-slice_fusion.6
  10.6 1.2 fusion.13
  11.9 0.8 fusion.31
  12.6 0.8 fusion.26
  13.5 0.2 fusion.21
  13.7 1.3 %fusion.6 = (f32[256,128]{1,0:T(8,128)}, f32[256,128]{1,0:T(8,128)}) fusion(s32[256]{0:T(256)S(1)} %get-tuple-element.37, s32[256]{0:T(256)S(1)} %get-tuple-element.38, pred[256]{0:T(512)(128)(4,1)S(1)} %compare_and_fusion), kind=kLoop, calls=%fused_computation.23 | loop fusion | flops 98304 | bytes 264448 | tf_op jit(solution)/shard_map/sin | solution.py:69
  15.0 0.6 fusion.11
  15.6 0.7 fusion.43
  16.3 4.1 %collective-permute-done.hist_ref = f32[2,2,32,1024]{3,2,1,0:T(8,128)S(1)} collective-permute-done((f32[2,2,32,1024]{3,2,1,0:T(8,128)S(1)}, f32[2,2,32,1024]{3,2,1,0:T(8,128)S(1)}, u32[]{:S(2)}, u32[]{:S(2)}) %collective-permute-start) | collective-permute-done | bytes 524320 | tf_op jit(solution)/shard_map/ppermute | solution.py:23
  20.5 0.0 copy-start.2
  20.5 0.8 copy-done.2
  21.3 7.5 %shard_map.127 = (f32[256,1024]{1,0:T(8,128)}, f32[256,1024]{1,0:T(8,128)}) custom-call(f32[2,2,32,3072]{3,2,1,0:T(8,128)} %bitcast.31, f32[2,2,32,1024]{3,2,1,0:T(8,128)} %copy-done.2, f32[32,128]{1,0:T(8,128)} %constant.186.clone.t1c, f32[32,128]{1,0:T(8,128)} %constant.187.clone.t1s, f32[32,32]{1,0:T(8,128)} %get-tuple-element.30.t2c, ...), custom_call_target="tpu_custom_call" | custom-call | tf_op jit(solution)/shard_map/pallas_call | solution.py:219
  28.8 0.0 copy-start.3
  28.8 8.3 %all-to-all-start.2 = ((f32[32,8,1024]{2,1,0:T(8,128)}), f32[32,8,1024]{2,1,0:T(8,128)S(1)}, u32[]{:S(2)}, u32[]{:S(2)}) async-start(f32[32,8,1024]{2,1,0:T(8,128)} %bitcast.32), calls=%async_computation.2 | async-start | bytes 2097152 | tf_op jit(solution)/shard_map/all_to_all | solution.py:229
  37.1 0.6 fusion.45
  37.7 0.0 collective-permute-done.1
  37.7 0.0 collective-permute-done.2
  37.8 0.0 collective-permute-done.3
  37.8 0.0 copy-done.3
  37.8 16.6 %all-to-all-done.2 = f32[32,8,1024]{2,1,0:T(8,128)S(1)} async-done(((f32[32,8,1024]{2,1,0:T(8,128)}), f32[32,8,1024]{2,1,0:T(8,128)S(1)}, u32[]{:S(2)}, u32[]{:S(2)}) %all-to-all-start.2) | async-done | bytes 1048608 | tf_op jit(solution)/shard_map/all_to_all | solution.py:229
  54.4 0.0 copy-start
  54.4 4.8 %all-to-all-start = ((f32[32,8,1024]{2,1,0:T(8,128)}), f32[32,8,1024]{2,1,0:T(8,128)}, u32[]{:S(2)}, u32[]{:S(2)}) async-start(f32[32,8,1024]{2,1,0:T(8,128)} %bitcast.1), calls=%async_computation | async-start | bytes 2097152 | tf_op jit(solution)/shard_map/all_to_all | solution.py:229
  59.4 1.0 copy.14
  60.4 0.0 copy-done
  60.4 1.7 %reshape_squeeze_reshape_transpose.3 = f32[32,32,4,8,4]{1,0,4,3,2:T(8,128)S(1)} reshape(f32[4,1,256,128]{2,0,3,1:T(4,128)} %copy.14) | data formatting | bytes 1048576 | tf_op jit(solution)/shard_map/reshape;squeeze;reshape;transpose | solution.py:238
  62.1 1.2 fusion.42
  63.3 0.6 copy.16
  63.9 0.4 broadcast_in_dim.48
  64.3 1.7 %slice.49.ph_ref = f32[1024,128]{1,0:T(8,128)} reshape(f32[4,32,2,4,4,32]{5,4,3,2,1,0:T(4,128)S(1)} %broadcast_in_dim.48) | data formatting | bytes 1048576 | tf_op jit(solution)/shard_map/slice | solution.py:271
  66.0 0.0 copy-start.1
  66.0 8.5 %shard_map.129 = f32[256,1024]{1,0:T(8,128)} custom-call(f32[256,1024]{1,0:T(8,128)} %bitcast.26, f32[32,512]{1,0:T(8,128)} %constant.192.clone.twc_ref, f32[32,512]{1,0:T(8,128)} %constant.193.clone.tws_ref, f32[256,256]{1,0:T(8,128)} %constant.190.clone.bf_ref, f32[256,256]{1,0:T(8,128)} %constant.191.clone.bb_ref, f32[1024,128]{1,0:T(8,128)} %slice.49.ph_ref, ...), custom_call_target="tpu_custom_call" | custom-call | tf_op jit(solution)/shard_map/pallas_call | solution.py:219
  74.5 1.9 %all-to-all-done = f32[32,8,1024]{2,1,0:T(8,128)} async-done(((f32[32,8,1024]{2,1,0:T(8,128)}), f32[32,8,1024]{2,1,0:T(8,128)}, u32[]{:S(2)}, u32[]{:S(2)}) %all-to-all-start) | async-done | bytes 1048608 | tf_op jit(solution)/shard_map/all_to_all | solution.py:229
  76.4 5.6 %all-to-all-start.3 = ((f32[32,8,1024]{2,1,0:T(8,128)}), f32[32,8,1024]{2,1,0:T(8,128)}, u32[]{:S(2)}, u32[]{:S(2)}) async-start(f32[32,8,1024]{2,1,0:T(8,128)} %bitcast.27), calls=%async_computation.3 | async-start | bytes 2097152 | tf_op jit(solution)/shard_map/all_to_all | solution.py:229
  82.0 0.0 copy-done.1
  82.0 0.6 copy.15
  82.6 0.4 broadcast_in_dim.44
  83.0 1.7 %slice.43.ph_ref = f32[1024,128]{1,0:T(8,128)} reshape(f32[4,32,2,4,4,32]{5,4,3,2,1,0:T(4,128)S(1)} %broadcast_in_dim.44) | data formatting | bytes 1048576 | tf_op jit(solution)/shard_map/slice | solution.py:271
  84.7 8.5 %shard_map.128 = f32[256,1024]{1,0:T(8,128)} custom-call(f32[256,1024]{1,0:T(8,128)} %bitcast.2.x_ref, f32[32,512]{1,0:T(8,128)} %constant.192.clone.twc_ref, f32[32,512]{1,0:T(8,128)} %constant.193.clone.tws_ref, f32[256,256]{1,0:T(8,128)} %constant.190.clone.bf_ref, f32[256,256]{1,0:T(8,128)} %constant.191.clone.bb_ref, f32[1024,128]{1,0:T(8,128)} %slice.43.ph_ref, ...), custom_call_target="tpu_custom_call" | custom-call | tf_op jit(solution)/shard_map/pallas_call | solution.py:219
  93.1 6.0 %all-to-all-done.3 = f32[32,8,1024]{2,1,0:T(8,128)} async-done(((f32[32,8,1024]{2,1,0:T(8,128)}), f32[32,8,1024]{2,1,0:T(8,128)}, u32[]{:S(2)}, u32[]{:S(2)}) %all-to-all-start.3) | async-done | bytes 1048608 | tf_op jit(solution)/shard_map/all_to_all | solution.py:229
  99.1 22.0 %all_to_all.20 = f32[32,8,1024]{2,1,0:T(8,128)} all-to-all(f32[32,8,1024]{2,1,0:T(8,128)} %bitcast.28), channel_id=1, replica_groups=mesh['band'=32,'seg'=4] {'band'}, dimensions={0} | all-to-all | bytes 2097152 | tf_op jit(solution)/shard_map/all_to_all | solution.py:229
  121.1 7.0 %shard_map.130 = f32[2,2,32,3072]{3,2,1,0:T(8,128)} custom-call(f32[256,1024]{1,0:T(8,128)} %bitcast.29, f32[256,1024]{1,0:T(8,128)} %bitcast.13.x1_ref, f32[512,512]{1,0:T(8,128)} %constant.194.clone.m_ref, f32[32,256]{1,0:T(8,128)} %constant.195.clone.twc_ref, f32[32,256]{1,0:T(8,128)} %constant.196.clone.tws_ref), custom_call_target="tpu_custom_call" | custom-call | tf_op jit(solution)/shard_map/pallas_call | solution.py:219
  (17 shorter events, 0.2 us)
Async XLA Ops:
  0.0 37.7 %collective-permute-start.1 = (f32[1,256,128]{2,1,0:T(8,128)}, f32[1,256,128]{2,1,0:T(8,128)S(1)}, u32[]{:S(2)}, u32[]{:S(2)}) collective-permute-start(f32[1,256,128]{2,1,0:T(8,128)} %param.14), channel_id=1, source_target_pairs={{1,0},{2,1},{3,2},{0,3},{5,4},{6,5},{7,6},{4,7},{9,8},{10,9},{11,1... | collective-permute-start | bytes 393224 | tf_op jit(solution)/shard_map/ppermute | solution.py:31
  3.1 34.6 %collective-permute-start.2 = (f32[1,256,128]{2,1,0:T(8,128)}, f32[1,256,128]{2,1,0:T(8,128)S(1)}, u32[]{:S(2)}, u32[]{:S(2)}) collective-permute-start(f32[1,256,128]{2,1,0:T(8,128)} %param.14), channel_id=1, source_target_pairs={{2,0},{3,1},{0,2},{1,3},{6,4},{7,5},{4,6},{5,7},{10,8},{11,9},{8,1... | collective-permute-start | bytes 393224 | tf_op jit(solution)/shard_map/ppermute | solution.py:31
  3.7 34.0 %collective-permute-start.3 = (f32[1,256,128]{2,1,0:T(8,128)}, f32[1,256,128]{2,1,0:T(8,128)S(1)}, u32[]{:S(2)}, u32[]{:S(2)}) collective-permute-start(f32[1,256,128]{2,1,0:T(8,128)} %param.14), channel_id=1, source_target_pairs={{3,0},{0,1},{1,2},{2,3},{7,4},{4,5},{5,6},{6,7},{11,8},{8,9},{9,10... | collective-permute-start | bytes 393224 | tf_op jit(solution)/shard_map/ppermute | solution.py:31
  5.8 14.7 %collective-permute-start = (f32[2,2,32,1024]{3,2,1,0:T(8,128)S(1)}, f32[2,2,32,1024]{3,2,1,0:T(8,128)S(1)}, u32[]{:S(2)}, u32[]{:S(2)}) collective-permute-start(f32[2,2,32,1024]{3,2,1,0:T(8,128)S(1)} %slice.54), channel_id=1, source_target_pairs={{0,1},{1,2},{2,3},{4,5},{5,6},{6,7},{8,9},{9,10},{10,11},{12,13},{... | collective-permute-start | bytes 1572872 | tf_op jit(solution)/shard_map/ppermute | solution.py:23
  20.5 0.8 copy-start.2
  28.8 9.0 %copy-start.3 = (f32[1,256,128]{2,1,0:T(8,128)S(1)}, f32[1,256,128]{2,1,0:T(8,128)}, u32[]{:S(2)}) copy-start(f32[1,256,128]{2,1,0:T(8,128)} %param.14) | copy-start | bytes 393220
  28.8 25.6 %all-to-all-start.2 = ((f32[32,8,1024]{2,1,0:T(8,128)}), f32[32,8,1024]{2,1,0:T(8,128)S(1)}, u32[]{:S(2)}, u32[]{:S(2)}) async-start(f32[32,8,1024]{2,1,0:T(8,128)} %bitcast.32), calls=%async_computation.2 | async-start | bytes 2097152 | tf_op jit(solution)/shard_map/all_to_all | solution.py:229
  54.4 6.0 %copy-start = (f32[32,8,1024]{2,1,0:T(8,128)}, f32[32,8,1024]{2,1,0:T(8,128)S(1)}, u32[]{:S(2)}) copy-start(f32[32,8,1024]{2,1,0:T(8,128)S(1)} %all-to-all-done.2) | copy-start | bytes 3145732
  54.4 22.0 %all-to-all-start = ((f32[32,8,1024]{2,1,0:T(8,128)}), f32[32,8,1024]{2,1,0:T(8,128)}, u32[]{:S(2)}, u32[]{:S(2)}) async-start(f32[32,8,1024]{2,1,0:T(8,128)} %bitcast.1), calls=%async_computation | async-start | bytes 2097152 | tf_op jit(solution)/shard_map/all_to_all | solution.py:229
  66.0 16.1 %copy-start.1 = (f32[4,32,4,4,32]{1,4,3,0,2:T(8,128)S(1)}, f32[4,32,4,4,32]{1,4,3,0,2:T(8,128)}, u32[]{:S(2)}) copy-start(f32[4,32,4,4,32]{1,4,3,0,2:T(8,128)} %get-tuple-element.10) | copy-start | bytes 786436
  76.4 22.7 %all-to-all-start.3 = ((f32[32,8,1024]{2,1,0:T(8,128)}), f32[32,8,1024]{2,1,0:T(8,128)}, u32[]{:S(2)}, u32[]{:S(2)}) async-start(f32[32,8,1024]{2,1,0:T(8,128)} %bitcast.27), calls=%async_computation.3 | async-start | bytes 2097152 | tf_op jit(solution)/shard_map/all_to_all | solution.py:229

commit v3 on v2

--- a/solution.py
+++ b/solution.py
@@ -129,7 +129,7 @@
 
 
 def column_forward_kernel(blk_ref, hist_ref, t1c, t1s, t2c, t2s, lr_ref, li_ref, pac, pas, pbc, pbs,
-                          out0_ref, out1_ref, xs_ref):
+                          out_ref, xs_ref):
     for p in range(2):
         xr, xi = [], []
         for t in range(32):
@@ -146,7 +146,7 @@
             xs_ref[k * 32:(k + 1) * 32, p * 256:p * 256 + 128] = re
             xs_ref[k * 32:(k + 1) * 32, p * 256 + 128:p * 256 + 256] = im
     dims = (((1,), (1,)), ((), ()))
-    for h, out_ref in enumerate((out0_ref, out1_ref)):
+    for h in range(2):
         x = xs_ref[512 * h:512 * (h + 1), :]
         ore = lax.dot_general(lr_ref[...], x, dims, precision=HIGHEST, preferred_element_type=F32)
         oim = lax.dot_general(li_ref[...], x, dims, precision=HIGHEST, preferred_element_type=F32)
@@ -157,14 +157,23 @@
             bs = pbs[d:d + 1, 512 * h:512 * (h + 1)]
             wc, ws = cmul(ac, as_, bc, bs)
             re, im = cmul(ore[8 * d:8 * d + 8], oim[8 * d:8 * d + 8], wc, ws)
-            out_ref[8 * d:8 * d + 8, 0:512] = re
-            out_ref[8 * d:8 * d + 8, 512:1024] = im
+            out_ref[8 * d:8 * d + 8, 1024 * h:1024 * h + 512] = re
+            out_ref[8 * d:8 * d + 8, 1024 * h + 512:1024 * h + 1024] = im
 
 
 def row_kernel(x_ref, twc_ref, tws_ref, bf_ref, bb_ref, ph_ref, ac_ref, as_ref, bc_ref, bs_ref, cc_ref, cs_ref,
                out_ref, y_ref, w_ref):
-    er = [x_ref[8 * d:8 * d + 8, 0:512] for d in range(32)]
-    ei = [x_ref[8 * d:8 * d + 8, 512:1024] for d in range(32)]
+    for h in range(2):
+        row_half(h, x_ref, twc_ref, tws_ref, bf_ref, bb_ref, ph_ref, ac_ref, as_ref, bc_ref, bs_ref, cc_ref, cs_ref,
+                 out_ref, y_ref, w_ref)
+
+
+def row_half(h, x_ref, twc_ref, tws_ref, bf_ref, bb_ref, ph_ref, ac_ref, as_ref, bc_ref, bs_ref, cc_ref, cs_ref,
+             out_ref, y_ref, w_ref):
+    base = 1024 * h
+    lanes = slice(512 * h, 512 * (h + 1))
+    er = [x_ref[8 * d:8 * d + 8, base:base + 512] for d in range(32)]
+    ei = [x_ref[8 * d:8 * d + 8, base + 512:base + 1024] for d in range(32)]
     fr, fi = fft_list(er, ei, -1)
     for g in range(32):
         a, b = cmul(fr[g], fi[g], twc_ref[g:g + 1, :], tws_ref[g:g + 1, :])
@@ -172,7 +181,7 @@
             y_ref[256 * j + 8 * g:256 * j + 8 * g + 8, 0:128] = a[:, 128 * j:128 * (j + 1)]
             y_ref[256 * j + 8 * g:256 * j + 8 * g + 8, 128:256] = b[:, 128 * j:128 * (j + 1)]
     z = jnp.dot(y_ref[...], bf_ref[...], precision=HIGHEST, preferred_element_type=F32)
-    phase = ph_ref[...]
+    phase = ph_ref[1024 * h:1024 * (h + 1), :]
     re, im = cmul(z[:, 0:128], z[:, 128:256], jnp.cos(phase), jnp.sin(phase))
     y_ref[:, 0:128] = re
     y_ref[:, 128:256] = im
@@ -185,19 +194,19 @@
         gr.append(a)
         gi.append(b)
     ur, ui = fft_list(gr, gi, 1)
-    ac = ac_ref[...]
-    as_ = as_ref[...]
+    ac = ac_ref[:, lanes]
+    as_ = as_ref[:, lanes]
     for d in range(32):
-        wc, ws = cmul(bc_ref[d:d + 1, :], bs_ref[d:d + 1, :], cc_ref[8 * d:8 * d + 8, 0:1], cs_ref[8 * d:8 * d + 8, 0:1])
+        wc, ws = cmul(bc_ref[d:d + 1, lanes], bs_ref[d:d + 1, lanes], cc_ref[8 * d:8 * d + 8, 0:1], cs_ref[8 * d:8 * d + 8, 0:1])
         wc, ws = cmul(wc, ws, ac, as_)
         re, im = cmul(ur[d], ui[d], wc, ws)
-        out_ref[8 * d:8 * d + 8, 0:512] = re
-        out_ref[8 * d:8 * d + 8, 512:1024] = im
-
-
-def column_inverse_kernel(x0_ref, x1_ref, m_ref, twc_ref, tws_ref, out_ref, s_ref):
-    lhs_re = jnp.concatenate([x0_ref[:, 0:512].T, x1_ref[:, 0:512].T], axis=0)
-    lhs_im = jnp.concatenate([x0_ref[:, 512:1024].T, x1_ref[:, 512:1024].T], axis=0)
+        out_ref[8 * d:8 * d + 8, base:base + 512] = re
+        out_ref[8 * d:8 * d + 8, base + 512:base + 1024] = im
+
+
+def column_inverse_kernel(x_ref, m_ref, twc_ref, tws_ref, out_ref, s_ref):
+    lhs_re = jnp.concatenate([x_ref[:, 0:512].T, x_ref[:, 1024:1536].T], axis=0)
+    lhs_im = jnp.concatenate([x_ref[:, 512:1024].T, x_ref[:, 1536:2048].T], axis=0)
     lhs = jnp.concatenate([lhs_re, lhs_im], axis=1)
     s_ref[...] = jnp.dot(lhs, m_ref[...], precision=HIGHEST, preferred_element_type=F32)
     er, ei = [], []
@@ -256,25 +265,20 @@
 
     t1c, t1s = lane_twiddle(-1, 128)
     lr, li = send_matrices()
-    send0, send1 = call(column_forward_kernel, [(256, 1024), (256, 1024)], [(1024, 512)],
-                        block, history, jnp.asarray(t1c), jnp.asarray(t1s), t2c, t2s,
-                        jnp.asarray(lr), jnp.asarray(li), pac, pas, pbc, pbs)
+    (send,) = call(column_forward_kernel, [(256, 2048)], [(1024, 512)],
+                   block, history, jnp.asarray(t1c), jnp.asarray(t1s), t2c, t2s,
+                   jnp.asarray(lr), jnp.asarray(li), pac, pas, pbc, pbs)
+    received = exchanged(send)
 
     twc, tws = row_twiddle(-1)
-    fwd, bwd = jnp.asarray(row_block(-1)), jnp.asarray(row_block(1))
-    back = []
-    for h, send in enumerate((send0, send1)):
-        received = exchanged(send)
-        lanes = slice(512 * h, 512 * (h + 1))
-        (sent,) = call(row_kernel, [(256, 1024)], [(1024, 256), (1024, 256)],
-                       received, jnp.asarray(twc), jnp.asarray(tws), fwd, bwd,
-                       chirp[1024 * h:1024 * (h + 1)], bac[:, lanes], bas[:, lanes],
-                       bbc[:, lanes], bbs[:, lanes], bcc, bcs)
-        back.append(exchanged(sent))
+    (sent,) = call(row_kernel, [(256, 2048)], [(1024, 256), (1024, 256)],
+                   received, jnp.asarray(twc), jnp.asarray(tws), jnp.asarray(row_block(-1)),
+                   jnp.asarray(row_block(1)), chirp, bac, bas, bbc, bbs, bcc, bcs)
+    returned = exchanged(sent)
 
     cc, cs = lane_twiddle(1, 256)
     (out,) = call(column_inverse_kernel, [(2, 2, ROWS_DEV, 3072)], [(1024, 512)],
-                  back[0], back[1], jnp.asarray(receive_matrix()), jnp.asarray(cc), jnp.asarray(cs))
+                  returned, jnp.asarray(receive_matrix()), jnp.asarray(cc), jnp.asarray(cs))
     return out[None, None]
 
 

time: 130 us -> 125 us (0.962)
  waiting for transfers between devices: 28.6 us -> 13 us
  blocking collectives: 22 us -> 33.3 us
  local copies, waits for them, and re-layouts: 13.5 us -> 24.6 us
  starting transfers between devices: 27.3 us -> 16.8 us
  Pallas kernels: 31.6 us -> 28.8 us
  other arithmetic: 5.02 us -> 6.36 us
    all_to_all x3 -> x1, waiting for transfers between devices: 24.5 us -> 9.26 us  [exchanged(): lax.all_to_all(block.reshape(32, rows // 32, width), 'band', 0, 0, tiled=...]
    all_to_all x1, blocking collectives: 22 us -> 33.3 us  [exchanged(): lax.all_to_all(block.reshape(32, rows // 32, width), 'band', 0, 0, tiled=...]
    all_to_all x3 -> x1, starting transfers between devices: 18.7 us -> 8.29 us  [exchanged(): lax.all_to_all(block.reshape(32, rows // 32, width), 'band', 0, 0, tiled=...]
    slice x7 -> x0, local copies, waits for them, and re-layouts: 7.12 us -> none  [the longest x5 5.76 us: per_device(): chirp[1024 * h:1024 * (h + 1)]]
    unnamed x15 -> x13, local copies, waits for them, and re-layouts: 1.8 us -> 7.67 us
    reshape x0 -> x1, local copies, waits for them, and re-layouts: none -> 4.54 us  [per_device(): jnp.broadcast_to(chirp[:, :, None], (8, 32, 2, 4, 4, 32)).reshape(2048, 128)]
    broadcast_in_dim x2 -> x1, local copies, waits for them, and re-layouts: 0.71 us -> 4.29 us  [per_device(): jnp.broadcast_to(chirp[:, :, None], (8, 32, 2, 4, 4, 32)).reshape(2048, 128)]
    transpose x0 -> x1, local copies, waits for them, and re-layouts: none -> 3.12 us  [per_device(): chirp = phases.reshape(32, 32, 4, 8, 4).transpose(3, 1, 2, 4, 0)]
  transfers between devices with their start and end apart: 7 -> 5, of which waited for: 4 -> 2; matrix products, arithmetic and copies ran while one was open for 14% -> 23% of each run, Pallas kernels for 19% -> 6%
where the time goes in v3:
time: 125 us; the launch traced here: 123 us
  blocking collectives  33.3 us (27%)
  Pallas kernels  28.8 us (23%)
  local copies, waits for them, and re-layouts  24.6 us (20%)
  starting transfers between devices  16.8 us (13%)
  waiting for transfers between devices  13 us (10%)
  other arithmetic  6.36 us (5%)
    all_to_all x1, blocking collectives, exchanged(): lax.all_to_all(block.reshape(32, rows // 32, width), 'band', 0, 0, tiled=...  33.3 us
    pallas_call x3, Pallas kernels, call(): pl.pallas_call(kernel, out_shape=[jax.ShapeDtypeStruct(s, F32) for s in o...  28.8 us
    all_to_all x1, waiting for transfers between devices, exchanged(): lax.all_to_all(block.reshape(32, rows // 32, width), 'band', 0, 0, tiled=...  9.26 us
    all_to_all x1, starting transfers between devices, exchanged(): lax.all_to_all(block.reshape(32, rows // 32, width), 'band', 0, 0, tiled=...  8.29 us
    unnamed x13, local copies, waits for them, and re-layouts  7.67 us
    sin x6, other arithmetic, unit(): return (jnp.cos(angle), jnp.sin(angle))  6.31 us
    ppermute x3, starting transfers between devices, gathered(): pieces.append(lax.ppermute(block, axis, route))  4.7 us
    reshape x1, local copies, waits for them, and re-layouts, per_device(): jnp.broadcast_to(chirp[:, :, None], (8, 32, 2, 4, 4, 32)).reshape(2048, 128)  4.54 us
  transfers between devices with their start and end apart: 5, of which 2 were waited for; matrix products, arithmetic and copies ran while one was open for 23% of the time, Pallas kernels for 6%

profile of v3, /device:TPU:0, one launch (start us, length us, event | category | flops | bytes accessed | tf_op | source)
XLA Modules:
  0.0 123.0 jit_solution(1366361292768667419)
XLA Ops:
  0.0 3.1 %collective-permute-start.1 = (f32[1,256,128]{2,1,0:T(8,128)}, f32[1,256,128]{2,1,0:T(8,128)S(1)}, u32[]{:S(2)}, u32[]{:S(2)}) collective-permute-start(f32[1,256,128]{2,1,0:T(8,128)} %param.14), channel_id=1, source_target_pairs={{1,0},{2,1},{3,2},{0,3},{5,4},{6,5},{7,6},{4,7},{9,8},{10,9},{11,1... | collective-permute-start | bytes 393224 | tf_op jit(solution)/shard_map/ppermute | solution.py:31
  3.1 0.6 collective-permute-start.2
  3.7 1.0 collective-permute-start.3
  4.7 1.1 slice.4
  5.8 3.8 %collective-permute-start = (f32[2,2,32,1024]{3,2,1,0:T(8,128)S(1)}, f32[2,2,32,1024]{3,2,1,0:T(8,128)S(1)}, u32[]{:S(2)}, u32[]{:S(2)}) collective-permute-start(f32[2,2,32,1024]{3,2,1,0:T(8,128)S(1)} %slice.4), channel_id=1, source_target_pairs={{0,1},{1,2},{2,3},{4,5},{5,6},{6,7},{8,9},{9,10},{10,11},{12,13},{... | collective-permute-start | bytes 1572872 | tf_op jit(solution)/shard_map/ppermute | solution.py:23
  9.6 1.6 %bitcast_dynamic-update-slice_fusion.6 = f32[8,1,256,128]{3,2,1,0:T(8,128)} fusion(f32[1,256,128]{2,1,0:T(8,128)} %param.14), kind=kLoop, calls=%fused_computation.20 | loop fusion | bytes 262144
  11.3 0.8 fusion.31
  12.0 0.8 fusion.26
  12.9 1.3 %fusion.6 = (f32[256,128]{1,0:T(8,128)}, f32[256,128]{1,0:T(8,128)}) fusion(s32[256]{0:T(256)S(1)} %get-tuple-element.21, s32[256]{0:T(256)S(1)} %get-tuple-element.22, pred[256]{0:T(512)(128)(4,1)S(1)} %compare_and_fusion), kind=kLoop, calls=%fused_computation.23 | loop fusion | flops 98304 | bytes 264448 | tf_op jit(solution)/shard_map/sin | solution.py:69
  14.2 1.2 %fusion.13 = (f32[32,1024]{1,0:T(8,128)}, f32[32,1024]{1,0:T(8,128)}) fusion(s32[1024]{0:T(1024)S(1)} %get-tuple-element.17), kind=kLoop, calls=%fused_computation.30 | loop fusion | flops 458752 | bytes 266240 | tf_op jit(solution)/shard_map/sin | solution.py:69
  15.4 1.3 %fusion.11 = (f32[32,1024]{1,0:T(8,128)}, f32[32,1024]{1,0:T(8,128)}) fusion(s32[1024]{0:T(1024)S(1)} %get-tuple-element.20, s32[32]{0:T(128)S(1)} %iota_multiply_fusion), kind=kLoop, calls=%fused_computation.28 | loop fusion | flops 458752 | bytes 266368 | tf_op jit(solution)/shard_map/sin | solution.py:69
  16.7 3.7 %collective-permute-done.hist_ref = f32[2,2,32,1024]{3,2,1,0:T(8,128)S(1)} collective-permute-done((f32[2,2,32,1024]{3,2,1,0:T(8,128)S(1)}, f32[2,2,32,1024]{3,2,1,0:T(8,128)S(1)}, u32[]{:S(2)}, u32[]{:S(2)}) %collective-permute-start) | collective-permute-done | bytes 524320 | tf_op jit(solution)/shard_map/ppermute | solution.py:23
  20.5 0.0 copy-start.2
  20.5 0.8 copy-done.2
  21.2 7.9 %shard_map.127 = f32[256,2048]{1,0:T(8,128)} custom-call(f32[2,2,32,3072]{3,2,1,0:T(8,128)} %bitcast.27, f32[2,2,32,1024]{3,2,1,0:T(8,128)} %copy-done.2, f32[32,128]{1,0:T(8,128)} %constant.186.clone.t1c, f32[32,128]{1,0:T(8,128)} %constant.187.clone.t1s, f32[32,32]{1,0:T(8,128)} %get-tuple-element.16.t2c, f32[32,32]{1,0:T(8,128)} %get-tuple-element.15.t2s, ...), custom_call_target="tpu_custom_call" | custom-call | tf_op jit(solution)/shard_map/pallas_call | solution.py:228
  29.1 0.0 copy-start.1
  29.1 8.3 %all-to-all-start = ((f32[32,8,2048]{2,1,0:T(8,128)}), f32[32,8,2048]{2,1,0:T(8,128)S(1)}, u32[]{:S(2)}, u32[]{:S(2)}) async-start(f32[32,8,2048]{2,1,0:T(8,128)} %bitcast.25), calls=%async_computation | async-start | bytes 4194304 | tf_op jit(solution)/shard_map/all_to_all | solution.py:238
  37.4 0.8 fusion.21
  38.3 0.0 collective-permute-done.1
  38.3 0.7 bitcast_dynamic-update-slice_fusion.4
  38.9 0.0 collective-permute-done.2
  38.9 0.7 bitcast_dynamic-update-slice_fusion.2
  39.6 0.0 collective-permute-done.3
  39.6 0.7 bitcast_dynamic-update-slice_fusion
  40.3 0.0 copy-done.1
  40.3 0.7 bitcast_dynamic-update-slice_fusion.7
  40.9 0.7 bitcast_dynamic-update-slice_fusion.5
  41.6 0.7 bitcast_dynamic-update-slice_fusion.3
  42.3 0.7 bitcast_dynamic-update-slice_fusion.1
  42.9 1.1 constant_dynamic-slice_fusion
  44.0 0.2 copy.14
  44.2 1.9 %reshape_squeeze_reshape_transpose.3 = f32[32,32,4,8,4]{1,0,4,3,2:T(8,128)} reshape(f32[4,1,256,128]{2,0,3,1:T(4,128)S(1)} %copy.14) | data formatting | bytes 1048576 | tf_op jit(solution)/shard_map/reshape;squeeze;reshape;transpose | solution.py:247
  46.2 3.1 %copy.15 = f32[8,32,4,4,32]{4,3,2,1,0:T(4,128)} copy(f32[8,32,4,4,32]{1,4,3,0,2:T(8,128)} %bitcast.24) | data formatting | bytes 1048576 | tf_op jit(solution)/shard_map/transpose | solution.py:247
  49.3 4.3 %broadcast_in_dim.30 = f32[8,32,2,4,4,32]{5,4,3,2,1,0:T(4,128)} broadcast(f32[8,32,4,4,32]{4,3,2,1,0:T(4,128)} %copy.15), dimensions={0,1,3,4,5} | broadcast | bytes 1572864 | tf_op jit(solution)/shard_map/broadcast_in_dim | solution.py:248
  53.6 4.5 %reshape.163.ph_ref = f32[2048,128]{1,0:T(8,128)} reshape(f32[8,32,2,4,4,32]{5,4,3,2,1,0:T(4,128)} %broadcast_in_dim.30) | data formatting | bytes 2097152 | tf_op jit(solution)/shard_map/reshape | solution.py:248
  58.1 9.3 %all-to-all-done = f32[32,8,2048]{2,1,0:T(8,128)S(1)} async-done(((f32[32,8,2048]{2,1,0:T(8,128)}), f32[32,8,2048]{2,1,0:T(8,128)S(1)}, u32[]{:S(2)}, u32[]{:S(2)}) %all-to-all-start) | async-done | bytes 2097184 | tf_op jit(solution)/shard_map/all_to_all | solution.py:238
  67.4 0.0 copy-start
  67.4 1.3 %copy-done = f32[32,8,2048]{2,1,0:T(8,128)} copy-done((f32[32,8,2048]{2,1,0:T(8,128)}, f32[32,8,2048]{2,1,0:T(8,128)S(1)}, u32[]{:S(2)}) %copy-start) | copy-done | bytes 2097176
  68.7 13.9 %shard_map.128 = f32[256,2048]{1,0:T(8,128)} custom-call(f32[256,2048]{1,0:T(8,128)} %bitcast.21, f32[32,512]{1,0:T(8,128)} %constant.190.clone.twc_ref, f32[32,512]{1,0:T(8,128)} %constant.191.clone.tws_ref, f32[256,256]{1,0:T(8,128)} %constant.192.clone.bf_ref, f32[256,256]{1,0:T(8,128)} %constant.193.clone.bb_ref, f32[2048,128]{1,0:T(8,128)} %reshape.163.ph_ref, ...), custom_call_target="tpu_custom_call" | custom-call | tf_op jit(solution)/shard_map/pallas_call | solution.py:228
  82.6 33.3 %all_to_all.10 = f32[32,8,2048]{2,1,0:T(8,128)} all-to-all(f32[32,8,2048]{2,1,0:T(8,128)} %bitcast.22), channel_id=1, replica_groups=mesh['band'=32,'seg'=4] {'band'}, dimensions={0} | all-to-all | bytes 4194304 | tf_op jit(solution)/shard_map/all_to_all | solution.py:238
  115.9 7.1 %shard_map.129 = f32[2,2,32,3072]{3,2,1,0:T(8,128)} custom-call(f32[256,2048]{1,0:T(8,128)} %bitcast.23, f32[512,512]{1,0:T(8,128)} %constant.194.clone.m_ref, f32[32,256]{1,0:T(8,128)} %constant.195.clone.twc_ref, f32[32,256]{1,0:T(8,128)} %constant.196.clone.tws_ref), custom_call_target="tpu_custom_call" | custom-call | tf_op jit(solution)/shard_map/pallas_call | solution.py:228
  (8 shorter events, 0.0 us)
Async XLA Ops:
  0.0 38.3 %collective-permute-start.1 = (f32[1,256,128]{2,1,0:T(8,128)}, f32[1,256,128]{2,1,0:T(8,128)S(1)}, u32[]{:S(2)}, u32[]{:S(2)}) collective-permute-start(f32[1,256,128]{2,1,0:T(8,128)} %param.14), channel_id=1, source_target_pairs={{1,0},{2,1},{3,2},{0,3},{5,4},{6,5},{7,6},{4,7},{9,8},{10,9},{11,1... | collective-permute-start | bytes 393224 | tf_op jit(solution)/shard_map/ppermute | solution.py:31
  3.1 35.8 %collective-permute-start.2 = (f32[1,256,128]{2,1,0:T(8,128)}, f32[1,256,128]{2,1,0:T(8,128)S(1)}, u32[]{:S(2)}, u32[]{:S(2)}) collective-permute-start(f32[1,256,128]{2,1,0:T(8,128)} %param.14), channel_id=1, source_target_pairs={{2,0},{3,1},{0,2},{1,3},{6,4},{7,5},{4,6},{5,7},{10,8},{11,9},{8,1... | collective-permute-start | bytes 393224 | tf_op jit(solution)/shard_map/ppermute | solution.py:31
  3.7 35.9 %collective-permute-start.3 = (f32[1,256,128]{2,1,0:T(8,128)}, f32[1,256,128]{2,1,0:T(8,128)S(1)}, u32[]{:S(2)}, u32[]{:S(2)}) collective-permute-start(f32[1,256,128]{2,1,0:T(8,128)} %param.14), channel_id=1, source_target_pairs={{3,0},{0,1},{1,2},{2,3},{7,4},{4,5},{5,6},{6,7},{11,8},{8,9},{9,10... | collective-permute-start | bytes 393224 | tf_op jit(solution)/shard_map/ppermute | solution.py:31
  5.8 14.7 %collective-permute-start = (f32[2,2,32,1024]{3,2,1,0:T(8,128)S(1)}, f32[2,2,32,1024]{3,2,1,0:T(8,128)S(1)}, u32[]{:S(2)}, u32[]{:S(2)}) collective-permute-start(f32[2,2,32,1024]{3,2,1,0:T(8,128)S(1)} %slice.4), channel_id=1, source_target_pairs={{0,1},{1,2},{2,3},{4,5},{5,6},{6,7},{8,9},{9,10},{10,11},{12,13},{... | collective-permute-start | bytes 1572872 | tf_op jit(solution)/shard_map/ppermute | solution.py:23
  20.5 0.8 copy-start.2
  29.1 11.2 %copy-start.1 = (f32[1,256,128]{2,1,0:T(8,128)S(1)}, f32[1,256,128]{2,1,0:T(8,128)}, u32[]{:S(2)}) copy-start(f32[1,256,128]{2,1,0:T(8,128)} %param.14) | copy-start | bytes 393220
  29.1 38.3 %all-to-all-start = ((f32[32,8,2048]{2,1,0:T(8,128)}), f32[32,8,2048]{2,1,0:T(8,128)S(1)}, u32[]{:S(2)}, u32[]{:S(2)}) async-start(f32[32,8,2048]{2,1,0:T(8,128)} %bitcast.25), calls=%async_computation | async-start | bytes 4194304 | tf_op jit(solution)/shard_map/all_to_all | solution.py:238
  67.4 1.3 %copy-start = (f32[32,8,2048]{2,1,0:T(8,128)}, f32[32,8,2048]{2,1,0:T(8,128)S(1)}, u32[]{:S(2)}) copy-start(f32[32,8,2048]{2,1,0:T(8,128)S(1)} %all-to-all-done) | copy-start | bytes 6291460

commit v4 on v3

--- a/solution.py
+++ b/solution.py
@@ -161,15 +161,12 @@
             out_ref[8 * d:8 * d + 8, 1024 * h + 512:1024 * h + 1024] = im
 
 
-def row_kernel(x_ref, twc_ref, tws_ref, bf_ref, bb_ref, ph_ref, ac_ref, as_ref, bc_ref, bs_ref, cc_ref, cs_ref,
-               out_ref, y_ref, w_ref):
+def row_kernel(x_ref, twc_ref, tws_ref, bf_ref, bb_ref, chc_ref, chs_ref, pc_ref, ps_ref, out_ref, y_ref, w_ref):
     for h in range(2):
-        row_half(h, x_ref, twc_ref, tws_ref, bf_ref, bb_ref, ph_ref, ac_ref, as_ref, bc_ref, bs_ref, cc_ref, cs_ref,
-                 out_ref, y_ref, w_ref)
-
-
-def row_half(h, x_ref, twc_ref, tws_ref, bf_ref, bb_ref, ph_ref, ac_ref, as_ref, bc_ref, bs_ref, cc_ref, cs_ref,
-             out_ref, y_ref, w_ref):
+        row_half(h, x_ref, twc_ref, tws_ref, bf_ref, bb_ref, chc_ref, chs_ref, pc_ref, ps_ref, out_ref, y_ref, w_ref)
+
+
+def row_half(h, x_ref, twc_ref, tws_ref, bf_ref, bb_ref, chc_ref, chs_ref, pc_ref, ps_ref, out_ref, y_ref, w_ref):
     base = 1024 * h
     lanes = slice(512 * h, 512 * (h + 1))
     er = [x_ref[8 * d:8 * d + 8, base:base + 512] for d in range(32)]
@@ -181,8 +178,7 @@
             y_ref[256 * j + 8 * g:256 * j + 8 * g + 8, 0:128] = a[:, 128 * j:128 * (j + 1)]
             y_ref[256 * j + 8 * g:256 * j + 8 * g + 8, 128:256] = b[:, 128 * j:128 * (j + 1)]
     z = jnp.dot(y_ref[...], bf_ref[...], precision=HIGHEST, preferred_element_type=F32)
-    phase = ph_ref[1024 * h:1024 * (h + 1), :]
-    re, im = cmul(z[:, 0:128], z[:, 128:256], jnp.cos(phase), jnp.sin(phase))
+    re, im = cmul(z[:, 0:128], z[:, 128:256], chc_ref[1024 * h:1024 * (h + 1), :], chs_ref[1024 * h:1024 * (h + 1), :])
     y_ref[:, 0:128] = re
     y_ref[:, 128:256] = im
     w_ref[...] = jnp.dot(y_ref[...], bb_ref[...], precision=HIGHEST, preferred_element_type=F32)
@@ -194,12 +190,8 @@
         gr.append(a)
         gi.append(b)
     ur, ui = fft_list(gr, gi, 1)
-    ac = ac_ref[:, lanes]
-    as_ = as_ref[:, lanes]
     for d in range(32):
-        wc, ws = cmul(bc_ref[d:d + 1, lanes], bs_ref[d:d + 1, lanes], cc_ref[8 * d:8 * d + 8, 0:1], cs_ref[8 * d:8 * d + 8, 0:1])
-        wc, ws = cmul(wc, ws, ac, as_)
-        re, im = cmul(ur[d], ui[d], wc, ws)
+        re, im = cmul(ur[d], ui[d], pc_ref[8 * d:8 * d + 8, lanes], ps_ref[8 * d:8 * d + 8, lanes])
         out_ref[8 * d:8 * d + 8, base:base + 512] = re
         out_ref[8 * d:8 * d + 8, base + 512:base + 1024] = im
 
@@ -243,9 +235,6 @@
     block = voltages[0, 0]
     band = lax.axis_index("band")
     history = passed_along(block[..., 3072 - HIST:], "seg", 1)
-    phases = gathered(chirp_phase, "seg", 1)[0]
-    chirp = phases.reshape(32, 32, 4, 8, 4).transpose(3, 1, 2, 4, 0)
-    chirp = jnp.broadcast_to(chirp[:, :, None], (8, 32, 2, 4, 4, 32)).reshape(2048, 128)
 
     i32 = jnp.int32
     lane = jnp.arange(1024, dtype=i32)[None, :]
@@ -258,10 +247,7 @@
     pbc, pbs = unit(128 * r_lane * dd, LENGTH, -1)
     kc_lane = 128 * band + ka_lane
     rl_lane = lane % 32
-    bac, bas = unit(rl_lane * (kc_lane + 32 * (q % 4)), LENGTH, 1)
-    bbc, bbs = unit(32 * dd * kc_lane, LENGTH, 1)
     rows = jnp.arange(256, dtype=i32)[:, None]
-    bcc, bcs = unit(jnp.broadcast_to(1024 * (rows // 8) * (rows % 4), (256, 128)), LENGTH, 1)
 
     t1c, t1s = lane_twiddle(-1, 128)
     lr, li = send_matrices()
@@ -270,10 +256,17 @@
                    jnp.asarray(lr), jnp.asarray(li), pac, pas, pbc, pbs)
     received = exchanged(send)
 
+    chirp_phase, send = lax.optimization_barrier((chirp_phase, send))
+    phases = gathered(chirp_phase, "seg", 1)[0]
+    chirp = phases.reshape(32, 32, 4, 8, 4).transpose(3, 1, 2, 4, 0)
+    chirp = jnp.broadcast_to(chirp[:, :, None], (8, 32, 2, 4, 4, 32)).reshape(2048, 128)
+    ch_c, ch_s = jnp.cos(chirp), jnp.sin(chirp)
+    back_c, back_s = unit((32 * (rows // 8) + lane % 32) * (kc_lane + 32 * (rows % 4)), LENGTH, 1)
+
     twc, tws = row_twiddle(-1)
     (sent,) = call(row_kernel, [(256, 2048)], [(1024, 256), (1024, 256)],
                    received, jnp.asarray(twc), jnp.asarray(tws), jnp.asarray(row_block(-1)),
-                   jnp.asarray(row_block(1)), chirp, bac, bas, bbc, bbs, bcc, bcs)
+                   jnp.asarray(row_block(1)), ch_c, ch_s, back_c, back_s)
     returned = exchanged(sent)
 
     cc, cs = lane_twiddle(1, 256)

time: 125 us -> 141 us (1.13)
  local copies, waits for them, and re-layouts: 24.6 us -> 35.1 us
  waiting for transfers between devices: 13 us -> 16.3 us
  Pallas kernels: 28.8 us -> 25.9 us
  blocking collectives: 33.3 us -> 35.9 us
  other arithmetic: 6.36 us -> 8.82 us
    sin x0 -> x5, local copies, waits for them, and re-layouts: none -> 12.4 us  [per_device(): ch_c, ch_s = (jnp.cos(chirp), jnp.sin(chirp))]
    cos x0 -> x4, local copies, waits for them, and re-layouts: none -> 10.9 us  [per_device(): ch_c, ch_s = (jnp.cos(chirp), jnp.sin(chirp))]
    all_to_all x1, waiting for transfers between devices: 9.26 us -> 0.01 us  [exchanged(): lax.all_to_all(block.reshape(32, rows // 32, width), 'band', 0, 0, tiled=...]
    ppermute x3, waiting for transfers between devices: 0.01 us -> 8.07 us  [gathered(): pieces.append(lax.ppermute(block, axis, route))]
    unnamed x13, local copies, waits for them, and re-layouts: 7.67 us -> 2.2 us
    reshape x1 -> x0, local copies, waits for them, and re-layouts: 4.54 us -> none  [per_device(): jnp.broadcast_to(chirp[:, :, None], (8, 32, 2, 4, 4, 32)).reshape(2048, 128)]
    ppermute x1, waiting for transfers between devices: 3.72 us -> 8.22 us  [passed_along(): return lax.ppermute(block, axis, route)]
    broadcast_in_dim x1 -> x2, local copies, waits for them, and re-layouts: 4.29 us -> 8.58 us  [per_device(): jnp.broadcast_to(chirp[:, :, None], (8, 32, 2, 4, 4, 32)).reshape(2048, 128)]
  transfers between devices with their start and end apart: 5 -> 5, of which waited for: 2 -> 4; matrix products, arithmetic and copies ran while one was open for 23% -> 29% of each run, Pallas kernels for 6% -> 0%
where the time goes in v4:
time: 141 us; the launch traced here: 139 us
  blocking collectives  35.9 us (25%)
  local copies, waits for them, and re-layouts  35.1 us (25%)
  Pallas kernels  25.9 us (18%)
  starting transfers between devices  17.3 us (12%)
  waiting for transfers between devices  16.3 us (12%)
  other arithmetic  8.82 us (6%)
    all_to_all x1, blocking collectives, exchanged(): lax.all_to_all(block.reshape(32, rows // 32, width), 'band', 0, 0, tiled=...  35.9 us
    pallas_call x3, Pallas kernels, call(): pl.pallas_call(kernel, out_shape=[jax.ShapeDtypeStruct(s, F32) for s in o...  25.9 us
    sin x5, local copies, waits for them, and re-layouts, per_device(): ch_c, ch_s = (jnp.cos(chirp), jnp.sin(chirp))  12.4 us
    cos x4, local copies, waits for them, and re-layouts, per_device(): ch_c, ch_s = (jnp.cos(chirp), jnp.sin(chirp))  10.9 us
    sin x4, other arithmetic, unit(): return (jnp.cos(angle), jnp.sin(angle))  8.8 us
    broadcast_in_dim x2, local copies, waits for them, and re-layouts, per_device(): jnp.broadcast_to(chirp[:, :, None], (8, 32, 2, 4, 4, 32)).reshape(2048, 128)  8.58 us
    ppermute x1, waiting for transfers between devices, passed_along(): return lax.ppermute(block, axis, route)  8.22 us
    all_to_all x1, starting transfers between devices, exchanged(): lax.all_to_all(block.reshape(32, rows // 32, width), 'band', 0, 0, tiled=...  8.17 us
  transfers between devices with their start and end apart: 5, of which 4 were waited for; matrix products, arithmetic and copies ran while one was open for 29% of the time, Pallas kernels for 0%

profile of v4, /device:TPU:0, one launch (start us, length us, event | category | flops | bytes accessed | tf_op | source)
XLA Modules:
  0.0 139.4 jit_solution(14848136431297380553)
XLA Ops:
  0.0 1.1 slice.4
  1.1 3.6 %collective-permute-start = (f32[2,2,32,1024]{3,2,1,0:T(8,128)S(1)}, f32[2,2,32,1024]{3,2,1,0:T(8,128)S(1)}, u32[]{:S(2)}, u32[]{:S(2)}) collective-permute-start(f32[2,2,32,1024]{3,2,1,0:T(8,128)S(1)} %slice.4), channel_id=1, source_target_pairs={{0,1},{1,2},{2,3},{4,5},{5,6},{6,7},{8,9},{9,10},{10,11},{12,13},{... | collective-permute-start | bytes 1572872 | tf_op jit(solution)/shard_map/ppermute | solution.py:23
  4.7 0.8 fusion.24
  5.5 0.9 fusion.19
  6.4 1.2 fusion.11
  7.6 8.2 %collective-permute-done.hist_ref = f32[2,2,32,1024]{3,2,1,0:T(8,128)S(1)} collective-permute-done((f32[2,2,32,1024]{3,2,1,0:T(8,128)S(1)}, f32[2,2,32,1024]{3,2,1,0:T(8,128)S(1)}, u32[]{:S(2)}, u32[]{:S(2)}) %collective-permute-start) | collective-permute-done | bytes 524320 | tf_op jit(solution)/shard_map/ppermute | solution.py:23
  15.8 0.0 copy-start.2
  15.8 0.8 copy-done.2
  16.6 7.9 %shard_map.127 = f32[256,2048]{1,0:T(8,128)} custom-call(f32[2,2,32,3072]{3,2,1,0:T(8,128)} %bitcast.31, f32[2,2,32,1024]{3,2,1,0:T(8,128)} %copy-done.2, f32[32,128]{1,0:T(8,128)} %constant.168.clone.t1c, f32[32,128]{1,0:T(8,128)} %constant.169.clone.t1s, f32[32,32]{1,0:T(8,128)} %get-tuple-element.16.t2c, f32[32,32]{1,0:T(8,128)} %get-tuple-element.15.t2s, ...), custom_call_target="tpu_custom_call" | custom-call | tf_op jit(solution)/shard_map/pallas_call | solution.py:220
  24.5 8.2 %all-to-all-start = ((f32[32,8,2048]{2,1,0:T(8,128)}), f32[32,8,2048]{2,1,0:T(8,128)S(1)}, u32[]{:S(2)}, u32[]{:S(2)}) async-start(f32[32,8,2048]{2,1,0:T(8,128)} %bitcast.29), calls=%async_computation | async-start | bytes 4194304 | tf_op jit(solution)/shard_map/all_to_all | solution.py:230
  32.7 0.0 copy-start.1
  32.7 5.9 %fusion.3 = (f32[256,1024]{1,0:T(8,128)}, f32[256,1024]{1,0:T(8,128)}) fusion(s32[256]{0:T(256)S(1)} %get-tuple-element.21, s32[1024]{0:T(1024)S(1)} %get-tuple-element.20, s32[1024]{0:T(1024)S(1)} %get-tuple-element.19, s32[256]{0:T(256)S(1)} %get-tuple-element.22), kind=kLoop, calls=%fused_computation.6 | loop fusion | flops 4194304 | bytes 2107392 | tf_op jit(solution)/shard_map/sin | solution.py:69
  38.6 0.0 copy-done.1
  38.6 3.9 %collective-permute-start.1 = (f32[1,256,128]{2,1,0:T(8,128)S(1)}, f32[1,256,128]{2,1,0:T(8,128)S(1)}, u32[]{:S(2)}, u32[]{:S(2)}) collective-permute-start(f32[1,256,128]{2,1,0:T(8,128)S(1)} %copy-done.1), channel_id=1, source_target_pairs={{1,0},{2,1},{3,2},{0,3},{5,4},{6,5},{7,6},{4,7},{9,8},{10,9},{11,1... | collective-permute-start | bytes 393224 | tf_op jit(solution)/shard_map/ppermute | solution.py:31
  42.5 0.6 collective-permute-start.2
  43.2 1.0 collective-permute-start.3
  44.1 4.4 %collective-permute-done.1 = f32[1,256,128]{2,1,0:T(8,128)S(1)} collective-permute-done((f32[1,256,128]{2,1,0:T(8,128)S(1)}, f32[1,256,128]{2,1,0:T(8,128)S(1)}, u32[]{:S(2)}, u32[]{:S(2)}) %collective-permute-start.1) | collective-permute-done | bytes 131104 | tf_op jit(solution)/shard_map/ppermute | solution.py:31
  48.5 1.9 %collective-permute-done.2 = f32[1,256,128]{2,1,0:T(8,128)S(1)} collective-permute-done((f32[1,256,128]{2,1,0:T(8,128)S(1)}, f32[1,256,128]{2,1,0:T(8,128)S(1)}, u32[]{:S(2)}, u32[]{:S(2)}) %collective-permute-start.2) | collective-permute-done | bytes 131104 | tf_op jit(solution)/shard_map/ppermute | solution.py:31
  50.4 1.8 %collective-permute-done.3 = f32[1,256,128]{2,1,0:T(8,128)S(1)} collective-permute-done((f32[1,256,128]{2,1,0:T(8,128)S(1)}, f32[1,256,128]{2,1,0:T(8,128)S(1)}, u32[]{:S(2)}, u32[]{:S(2)}) %collective-permute-start.3) | collective-permute-done | bytes 131104 | tf_op jit(solution)/shard_map/ppermute | solution.py:31
  52.3 2.6 %dynamic-slice_sine_fusion = (f32[4,1,256,128]{3,2,1,0:T(8,128)S(1)}, f32[4,1,256,128]{3,2,1,0:T(8,128)}) fusion(f32[8,1,256,128]{3,2,1,0:T(8,128)S(1)} %bitcast_dynamic-update-slice_fusion.1, s32[]{:T(128)S(6)} %select_n.106), kind=kLoop, calls=%fused_computation.8 | loop fusion | bytes 1572868 | tf_op jit(solution)/shard_map/sin | solution.py:263
  54.9 1.3 copy.16
  56.2 1.9 %cos.25 = f32[32,32,4,8,4]{1,0,4,3,2:T(8,128)} reshape(f32[4,1,256,128]{2,0,3,1:T(4,128)S(1)} %copy.16) | data formatting | bytes 1048576 | tf_op jit(solution)/shard_map/cos | solution.py:263
  58.1 3.1 %copy.17 = f32[8,32,4,4,32]{4,3,2,1,0:T(4,128)} copy(f32[8,32,4,4,32]{1,4,3,0,2:T(8,128)} %bitcast.27) | data formatting | bytes 1048576 | tf_op jit(solution)/shard_map/cos | solution.py:263
  61.2 4.3 %broadcast_in_dim.6 = f32[8,32,2,4,4,32]{5,4,3,2,1,0:T(4,128)} broadcast(f32[8,32,4,4,32]{4,3,2,1,0:T(4,128)} %copy.17), dimensions={0,1,3,4,5} | broadcast | bytes 1572864 | tf_op jit(solution)/shard_map/broadcast_in_dim | solution.py:262
  65.5 4.5 %cos.27.chc_ref = f32[2048,128]{1,0:T(8,128)} reshape(f32[8,32,2,4,4,32]{5,4,3,2,1,0:T(4,128)} %broadcast_in_dim.6) | data formatting | bytes 2097152 | tf_op jit(solution)/shard_map/cos | solution.py:263
  70.1 0.2 copy.18
  70.3 1.9 %sin.25 = f32[32,32,4,8,4]{1,0,4,3,2:T(8,128)} reshape(f32[4,1,256,128]{2,0,3,1:T(4,128)S(1)} %copy.18) | data formatting | bytes 1048576 | tf_op jit(solution)/shard_map/sin | solution.py:263
  72.2 3.1 %copy.19 = f32[8,32,4,4,32]{4,3,2,1,0:T(4,128)} copy(f32[8,32,4,4,32]{1,4,3,0,2:T(8,128)} %bitcast.28) | data formatting | bytes 1048576 | tf_op jit(solution)/shard_map/sin | solution.py:263
  75.3 4.3 %broadcast_in_dim.7 = f32[8,32,2,4,4,32]{5,4,3,2,1,0:T(4,128)} broadcast(f32[8,32,4,4,32]{4,3,2,1,0:T(4,128)} %copy.19), dimensions={0,1,3,4,5} | broadcast | bytes 1572864 | tf_op jit(solution)/shard_map/broadcast_in_dim | solution.py:262
  79.6 4.5 %sin.27.chs_ref = f32[2048,128]{1,0:T(8,128)} reshape(f32[8,32,2,4,4,32]{5,4,3,2,1,0:T(4,128)} %broadcast_in_dim.7) | data formatting | bytes 2097152 | tf_op jit(solution)/shard_map/sin | solution.py:263
  84.2 0.0 all-to-all-done
  84.2 0.0 copy-start
  84.2 1.3 copy-done
  85.5 10.9 %shard_map.128 = f32[256,2048]{1,0:T(8,128)} custom-call(f32[256,2048]{1,0:T(8,128)} %bitcast.24, f32[32,512]{1,0:T(8,128)} %constant.172.clone.twc_ref, f32[32,512]{1,0:T(8,128)} %constant.173.clone.tws_ref, f32[256,256]{1,0:T(8,128)} %constant.174.clone.bf_ref, f32[256,256]{1,0:T(8,128)} %constant.175.clone.bb_ref, f32[2048,128]{1,0:T(8,128)} %cos.27.chc_ref, ...), custom_call_target="tpu_custom_call" | custom-call | tf_op jit(solution)/shard_map/pallas_call | solution.py:220
  96.4 35.9 %all_to_all.10 = f32[32,8,2048]{2,1,0:T(8,128)} all-to-all(f32[32,8,2048]{2,1,0:T(8,128)} %bitcast.25), channel_id=1, replica_groups=mesh['band'=32,'seg'=4] {'band'}, dimensions={0} | all-to-all | bytes 4194304 | tf_op jit(solution)/shard_map/all_to_all | solution.py:230
  132.4 7.1 %shard_map.129 = f32[2,2,32,3072]{3,2,1,0:T(8,128)} custom-call(f32[256,2048]{1,0:T(8,128)} %bitcast.26, f32[512,512]{1,0:T(8,128)} %constant.176.clone.m_ref, f32[32,256]{1,0:T(8,128)} %constant.177.clone.twc_ref, f32[32,256]{1,0:T(8,128)} %constant.178.clone.tws_ref), custom_call_target="tpu_custom_call" | custom-call | tf_op jit(solution)/shard_map/pallas_call | solution.py:220
  (13 shorter events, 0.1 us)
Async XLA Ops:
  1.1 14.7 %collective-permute-start = (f32[2,2,32,1024]{3,2,1,0:T(8,128)S(1)}, f32[2,2,32,1024]{3,2,1,0:T(8,128)S(1)}, u32[]{:S(2)}, u32[]{:S(2)}) collective-permute-start(f32[2,2,32,1024]{3,2,1,0:T(8,128)S(1)} %slice.4), channel_id=1, source_target_pairs={{0,1},{1,2},{2,3},{4,5},{5,6},{6,7},{8,9},{9,10},{10,11},{12,13},{... | collective-permute-start | bytes 1572872 | tf_op jit(solution)/shard_map/ppermute | solution.py:23
  15.8 0.8 copy-start.2
  24.5 59.7 %all-to-all-start = ((f32[32,8,2048]{2,1,0:T(8,128)}), f32[32,8,2048]{2,1,0:T(8,128)S(1)}, u32[]{:S(2)}, u32[]{:S(2)}) async-start(f32[32,8,2048]{2,1,0:T(8,128)} %bitcast.29), calls=%async_computation | async-start | bytes 4194304 | tf_op jit(solution)/shard_map/all_to_all | solution.py:230
  32.7 6.0 %copy-start.1 = (f32[1,256,128]{2,1,0:T(8,128)S(1)}, f32[1,256,128]{2,1,0:T(8,128)}, u32[]{:S(2)}) copy-start(f32[1,256,128]{2,1,0:T(8,128)} %param.14) | copy-start | bytes 393220
  38.6 9.9 %collective-permute-start.1 = (f32[1,256,128]{2,1,0:T(8,128)S(1)}, f32[1,256,128]{2,1,0:T(8,128)S(1)}, u32[]{:S(2)}, u32[]{:S(2)}) collective-permute-start(f32[1,256,128]{2,1,0:T(8,128)S(1)} %copy-done.1), channel_id=1, source_target_pairs={{1,0},{2,1},{3,2},{0,3},{5,4},{6,5},{7,6},{4,7},{9,8},{10,9},{11,1... | collective-permute-start | bytes 393224 | tf_op jit(solution)/shard_map/ppermute | solution.py:31
  42.5 7.9 %collective-permute-start.2 = (f32[1,256,128]{2,1,0:T(8,128)S(1)}, f32[1,256,128]{2,1,0:T(8,128)S(1)}, u32[]{:S(2)}, u32[]{:S(2)}) collective-permute-start(f32[1,256,128]{2,1,0:T(8,128)S(1)} %copy-done.1), channel_id=1, source_target_pairs={{2,0},{3,1},{0,2},{1,3},{6,4},{7,5},{4,6},{5,7},{10,8},{11,9},{8,1... | collective-permute-start | bytes 393224 | tf_op jit(solution)/shard_map/ppermute | solution.py:31
  43.2 9.1 %collective-permute-start.3 = (f32[1,256,128]{2,1,0:T(8,128)S(1)}, f32[1,256,128]{2,1,0:T(8,128)S(1)}, u32[]{:S(2)}, u32[]{:S(2)}) collective-permute-start(f32[1,256,128]{2,1,0:T(8,128)S(1)} %copy-done.1), channel_id=1, source_target_pairs={{3,0},{0,1},{1,2},{2,3},{7,4},{4,5},{5,6},{6,7},{11,8},{8,9},{9,10... | collective-permute-start | bytes 393224 | tf_op jit(solution)/shard_map/ppermute | solution.py:31
  84.2 1.3 copy-start

commit v5 on v4

--- a/solution.py
+++ b/solution.py
@@ -231,6 +231,11 @@
     return out.reshape(rows, width)
 
 
+def arranged(table):
+    table = table.reshape(32, 32, 4, 8, 4).transpose(3, 1, 2, 4, 0)
+    return jnp.broadcast_to(table[:, :, None], (8, 32, 2, 4, 4, 32)).reshape(2048, 128)
+
+
 def per_device(voltages, chirp_phase):
     block = voltages[0, 0]
     band = lax.axis_index("band")
@@ -257,10 +262,7 @@
     received = exchanged(send)
 
     chirp_phase, send = lax.optimization_barrier((chirp_phase, send))
-    phases = gathered(chirp_phase, "seg", 1)[0]
-    chirp = phases.reshape(32, 32, 4, 8, 4).transpose(3, 1, 2, 4, 0)
-    chirp = jnp.broadcast_to(chirp[:, :, None], (8, 32, 2, 4, 4, 32)).reshape(2048, 128)
-    ch_c, ch_s = jnp.cos(chirp), jnp.sin(chirp)
+    ch_c, ch_s = [arranged(gathered(f(chirp_phase), "seg", 1)[0]) for f in (jnp.cos, jnp.sin)]
     back_c, back_s = unit((32 * (rows // 8) + lane % 32) * (kc_lane + 32 * (rows % 4)), LENGTH, 1)
 
     twc, tws = row_twiddle(-1)

time: 141 us -> 136 us (0.965)
  waiting for transfers between devices: 16.3 us -> 8.29 us
  starting transfers between devices: 17.3 us -> 22.3 us
  local copies, waits for them, and re-layouts: 35.1 us -> 31.9 us
  other arithmetic: 8.82 us -> 10.3 us
    sin x5 -> x1, local copies, waits for them, and re-layouts: 12.4 us -> 0.46 us  [per_device(): f(chirp_phase)]
    cos x4 -> x0, local copies, waits for them, and re-layouts: 10.9 us -> none  [per_device(): ch_c, ch_s = (jnp.cos(chirp), jnp.sin(chirp))]
    reshape x0 -> x2, local copies, waits for them, and re-layouts: none -> 9.07 us  [arranged(): jnp.broadcast_to(table[:, :, None], (8, 32, 2, 4, 4, 32)).reshape(2048, 128)]
    ppermute x3 -> x6, waiting for transfers between devices: 8.07 us -> 0.02 us  [gathered(): pieces.append(lax.ppermute(block, axis, route))]
    transpose x0 -> x2, local copies, waits for them, and re-layouts: none -> 6.26 us  [arranged(): table = table.reshape(32, 32, 4, 8, 4).transpose(3, 1, 2, 4, 0)]
    ppermute x3 -> x6, starting transfers between devices: 5.52 us -> 10.4 us  [gathered(): pieces.append(lax.ppermute(block, axis, route))]
    another operation x0 -> x2, local copies, waits for them, and re-layouts: none -> 3.87 us  [arranged(): table = table.reshape(32, 32, 4, 8, 4).transpose(3, 1, 2, 4, 0)]
    concatenate x0 -> x2, other arithmetic: none -> 1.6 us  [gathered(): ordered = jnp.roll(ahead, lax.axis_index(axis), axis=0)]
  transfers between devices with their start and end apart: 5 -> 8, of which waited for: 4 -> 1; matrix products, arithmetic and copies ran while one was open for 29% -> 29% of each run, Pallas kernels for 0% -> 0%
where the time goes in v5:
time: 136 us; the launch traced here: 135 us
  blocking collectives  36.1 us (27%)
  local copies, waits for them, and re-layouts  31.9 us (23%)
  Pallas kernels  25.9 us (19%)
  starting transfers between devices  22.3 us (16%)
  other arithmetic  10.3 us (8%)
  waiting for transfers between devices  8.29 us (6%)
    all_to_all x1, blocking collectives, exchanged(): lax.all_to_all(block.reshape(32, rows // 32, width), 'band', 0, 0, tiled=...  36.1 us
    pallas_call x3, Pallas kernels, call(): pl.pallas_call(kernel, out_shape=[jax.ShapeDtypeStruct(s, F32) for s in o...  25.9 us
    ppermute x6, starting transfers between devices, gathered(): pieces.append(lax.ppermute(block, axis, route))  10.4 us
    reshape x2, local copies, waits for them, and re-layouts, arranged(): jnp.broadcast_to(table[:, :, None], (8, 32, 2, 4, 4, 32)).reshape(2048, 128)  9.07 us
    sin x4, other arithmetic, unit(): return (jnp.cos(angle), jnp.sin(angle))  8.71 us
    broadcast_in_dim x2, local copies, waits for them, and re-layouts, arranged(): jnp.broadcast_to(table[:, :, None], (8, 32, 2, 4, 4, 32)).reshape(2048, 128)  8.55 us
    all_to_all x1, starting transfers between devices, exchanged(): lax.all_to_all(block.reshape(32, rows // 32, width), 'band', 0, 0, tiled=...  8.3 us
    ppermute x1, waiting for transfers between devices, passed_along(): return lax.ppermute(block, axis, route)  8.28 us
  transfers between devices with their start and end apart: 8, of which 1 were waited for; matrix products, arithmetic and copies ran while one was open for 29% of the time, Pallas kernels for 0%

profile of v5, /device:TPU:0, one launch (start us, length us, event | category | flops | bytes accessed | tf_op | source)
XLA Modules:
  0.0 134.8 jit_solution(13057361763108663837)
XLA Ops:
  0.0 1.1 slice.4
  1.1 3.6 %collective-permute-start = (f32[2,2,32,1024]{3,2,1,0:T(8,128)S(1)}, f32[2,2,32,1024]{3,2,1,0:T(8,128)S(1)}, u32[]{:S(2)}, u32[]{:S(2)}) collective-permute-start(f32[2,2,32,1024]{3,2,1,0:T(8,128)S(1)} %slice.4), channel_id=1, source_target_pairs={{0,1},{1,2},{2,3},{4,5},{5,6},{6,7},{8,9},{9,10},{10,11},{12,13},{... | collective-permute-start | bytes 1572872 | tf_op jit(solution)/shard_map/ppermute | solution.py:23
  4.7 0.8 fusion.38
  5.5 0.8 fusion.33
  6.3 1.2 fusion.25
  7.6 8.3 %collective-permute-done.hist_ref = f32[2,2,32,1024]{3,2,1,0:T(8,128)S(1)} collective-permute-done((f32[2,2,32,1024]{3,2,1,0:T(8,128)S(1)}, f32[2,2,32,1024]{3,2,1,0:T(8,128)S(1)}, u32[]{:S(2)}, u32[]{:S(2)}) %collective-permute-start) | collective-permute-done | bytes 524320 | tf_op jit(solution)/shard_map/ppermute | solution.py:23
  15.8 0.0 copy-start.1
  15.8 0.8 copy-done.1
  16.6 7.9 %shard_map.127 = f32[256,2048]{1,0:T(8,128)} custom-call(f32[2,2,32,3072]{3,2,1,0:T(8,128)} %bitcast.27, f32[2,2,32,1024]{3,2,1,0:T(8,128)} %copy-done.1, f32[32,128]{1,0:T(8,128)} %constant.169.clone.t1c, f32[32,128]{1,0:T(8,128)} %constant.170.clone.t1s, f32[32,32]{1,0:T(8,128)} %get-tuple-element.17.t2c, f32[32,32]{1,0:T(8,128)} %get-tuple-element.16.t2s, ...), custom_call_target="tpu_custom_call" | custom-call | tf_op jit(solution)/shard_map/pallas_call | solution.py:220
  24.5 0.0 copy-start.2
  24.5 8.3 %all-to-all-start = ((f32[32,8,2048]{2,1,0:T(8,128)}), f32[32,8,2048]{2,1,0:T(8,128)S(1)}, u32[]{:S(2)}, u32[]{:S(2)}) async-start(f32[32,8,2048]{2,1,0:T(8,128)} %bitcast.25), calls=%async_computation | async-start | bytes 4194304 | tf_op jit(solution)/shard_map/all_to_all | solution.py:230
  32.8 0.0 copy-done.2
  32.8 0.5 fusion.48
  33.3 4.2 %collective-permute-start.5 = (f32[1,256,128]{2,1,0:T(8,128)S(1)}, f32[1,256,128]{2,1,0:T(8,128)S(1)}, u32[]{:S(2)}, u32[]{:S(2)}) collective-permute-start(f32[1,256,128]{2,1,0:T(8,128)S(1)} %get-tuple-element.8), channel_id=1, source_target_pairs={{2,0},{3,1},{0,2},{1,3},{6,4},{7,5},{4,6},{5,7},{10,8},{11,9},{8,1... | collective-permute-start | bytes 393224 | tf_op jit(solution)/shard_map/ppermute | solution.py:31
  37.5 0.7 collective-permute-start.6
  38.1 2.6 %collective-permute-start.4 = (f32[1,256,128]{2,1,0:T(8,128)S(1)}, f32[1,256,128]{2,1,0:T(8,128)S(1)}, u32[]{:S(2)}, u32[]{:S(2)}) collective-permute-start(f32[1,256,128]{2,1,0:T(8,128)S(1)} %get-tuple-element.8), channel_id=1, source_target_pairs={{1,0},{2,1},{3,2},{0,3},{5,4},{6,5},{7,6},{4,7},{9,8},{10,9},{11,1... | collective-permute-start | bytes 393224 | tf_op jit(solution)/shard_map/ppermute | solution.py:31
  40.7 0.0 collective-permute-start.1
  40.7 1.5 %collective-permute-start.2 = (f32[1,256,128]{2,1,0:T(8,128)S(1)}, f32[1,256,128]{2,1,0:T(8,128)S(1)}, u32[]{:S(2)}, u32[]{:S(2)}) collective-permute-start(f32[1,256,128]{2,1,0:T(8,128)S(1)} %get-tuple-element.9), channel_id=1, source_target_pairs={{2,0},{3,1},{0,2},{1,3},{6,4},{7,5},{4,6},{5,7},{10,8},{11,9},{8,1... | collective-permute-start | bytes 393224 | tf_op jit(solution)/shard_map/ppermute | solution.py:31
  42.2 0.0 collective-permute-done.5
  42.2 1.4 %collective-permute-start.3 = (f32[1,256,128]{2,1,0:T(8,128)S(1)}, f32[1,256,128]{2,1,0:T(8,128)}, u32[]{:S(2)}, u32[]{:S(2)}) collective-permute-start(f32[1,256,128]{2,1,0:T(8,128)S(1)} %get-tuple-element.9), channel_id=1, source_target_pairs={{3,0},{0,1},{1,2},{2,3},{7,4},{4,5},{5,6},{6,7},{11,8},{8,9},{9,10... | collective-permute-start | bytes 393224 | tf_op jit(solution)/shard_map/ppermute | solution.py:31
  43.7 5.9 %fusion.3 = (f32[256,1024]{1,0:T(8,128)}, f32[256,1024]{1,0:T(8,128)}) fusion(s32[256]{0:T(256)S(1)} %get-tuple-element.22, s32[1024]{0:T(1024)S(1)} %get-tuple-element.21, s32[1024]{0:T(1024)S(1)} %get-tuple-element.20, s32[256]{0:T(256)S(1)} %get-tuple-element.23), kind=kLoop, calls=%fused_computation.22 | loop fusion | flops 4194304 | bytes 2107392 | tf_op jit(solution)/shard_map/sin | solution.py:69
  49.6 0.0 collective-permute-done.6
  49.6 0.0 collective-permute-done.4
  49.6 0.3 fusion.8
  49.9 0.2 copy.16
  50.1 1.9 %reshape_squeeze_reshape_transpose.7 = f32[32,32,4,8,4]{1,0,4,3,2:T(8,128)} reshape(f32[4,1,256,128]{2,0,3,1:T(4,128)S(1)} %copy.16) | data formatting | bytes 1048576 | tf_op jit(solution)/shard_map/reshape;squeeze;reshape;transpose | solution.py:235
  52.1 3.1 %copy.17 = f32[8,32,4,4,32]{4,3,2,1,0:T(4,128)} copy(f32[8,32,4,4,32]{1,4,3,0,2:T(8,128)} %bitcast.23) | data formatting | bytes 1048576 | tf_op jit(solution)/shard_map/transpose | solution.py:235
  55.2 4.3 %broadcast_in_dim.7 = f32[8,32,2,4,4,32]{5,4,3,2,1,0:T(4,128)} broadcast(f32[8,32,4,4,32]{4,3,2,1,0:T(4,128)} %copy.17), dimensions={0,1,3,4,5} | broadcast | bytes 1572864 | tf_op jit(solution)/shard_map/broadcast_in_dim | solution.py:236
  59.5 4.5 %reshape.161.chs_ref = f32[2048,128]{1,0:T(8,128)} reshape(f32[8,32,2,4,4,32]{5,4,3,2,1,0:T(4,128)} %broadcast_in_dim.7) | data formatting | bytes 2097152 | tf_op jit(solution)/shard_map/reshape | solution.py:236
  64.0 0.0 collective-permute-done.1
  64.0 0.0 collective-permute-done.2
  64.0 0.0 collective-permute-done.3
  64.0 1.3 fusion.15
  65.3 0.2 copy.14
  65.5 1.9 %reshape_squeeze_reshape_transpose.6 = f32[32,32,4,8,4]{1,0,4,3,2:T(8,128)} reshape(f32[4,1,256,128]{2,0,3,1:T(4,128)S(1)} %copy.14) | data formatting | bytes 1048576 | tf_op jit(solution)/shard_map/reshape;squeeze;reshape;transpose | solution.py:235
  67.5 3.1 %copy.15 = f32[8,32,4,4,32]{4,3,2,1,0:T(4,128)} copy(f32[8,32,4,4,32]{1,4,3,0,2:T(8,128)} %bitcast.24) | data formatting | bytes 1048576 | tf_op jit(solution)/shard_map/transpose | solution.py:235
  70.6 4.3 %broadcast_in_dim.6 = f32[8,32,2,4,4,32]{5,4,3,2,1,0:T(4,128)} broadcast(f32[8,32,4,4,32]{4,3,2,1,0:T(4,128)} %copy.15), dimensions={0,1,3,4,5} | broadcast | bytes 1572864 | tf_op jit(solution)/shard_map/broadcast_in_dim | solution.py:236
  74.9 4.5 %reshape.160.chc_ref = f32[2048,128]{1,0:T(8,128)} reshape(f32[8,32,2,4,4,32]{5,4,3,2,1,0:T(4,128)} %broadcast_in_dim.6) | data formatting | bytes 2097152 | tf_op jit(solution)/shard_map/reshape | solution.py:236
  79.4 0.0 all-to-all-done
  79.4 0.0 copy-start
  79.4 1.3 copy-done
  80.7 10.9 %shard_map.128 = f32[256,2048]{1,0:T(8,128)} custom-call(f32[256,2048]{1,0:T(8,128)} %bitcast.20, f32[32,512]{1,0:T(8,128)} %constant.173.clone.twc_ref, f32[32,512]{1,0:T(8,128)} %constant.174.clone.tws_ref, f32[256,256]{1,0:T(8,128)} %constant.175.clone.bf_ref, f32[256,256]{1,0:T(8,128)} %constant.176.clone.bb_ref, f32[2048,128]{1,0:T(8,128)} %reshape.160.chc_ref, ...), custom_call_target="tpu_custom_call" | custom-call | tf_op jit(solution)/shard_map/pallas_call | solution.py:220
  91.7 36.1 %all_to_all.10 = f32[32,8,2048]{2,1,0:T(8,128)} all-to-all(f32[32,8,2048]{2,1,0:T(8,128)} %bitcast.21), channel_id=1, replica_groups=mesh['band'=32,'seg'=4] {'band'}, dimensions={0} | all-to-all | bytes 4194304 | tf_op jit(solution)/shard_map/all_to_all | solution.py:230
  127.7 7.1 %shard_map.129 = f32[2,2,32,3072]{3,2,1,0:T(8,128)} custom-call(f32[256,2048]{1,0:T(8,128)} %bitcast.22, f32[512,512]{1,0:T(8,128)} %constant.177.clone.m_ref, f32[32,256]{1,0:T(8,128)} %constant.178.clone.twc_ref, f32[32,256]{1,0:T(8,128)} %constant.179.clone.tws_ref), custom_call_target="tpu_custom_call" | custom-call | tf_op jit(solution)/shard_map/pallas_call | solution.py:220
  (5 shorter events, 0.0 us)
Async XLA Ops:
  1.1 14.7 %collective-permute-start = (f32[2,2,32,1024]{3,2,1,0:T(8,128)S(1)}, f32[2,2,32,1024]{3,2,1,0:T(8,128)S(1)}, u32[]{:S(2)}, u32[]{:S(2)}) collective-permute-start(f32[2,2,32,1024]{3,2,1,0:T(8,128)S(1)} %slice.4), channel_id=1, source_target_pairs={{0,1},{1,2},{2,3},{4,5},{5,6},{6,7},{8,9},{9,10},{10,11},{12,13},{... | collective-permute-start | bytes 1572872 | tf_op jit(solution)/shard_map/ppermute | solution.py:23
  15.8 0.8 copy-start.1
  24.5 8.3 %copy-start.2 = (f32[1,256,128]{2,1,0:T(8,128)S(1)}, f32[1,256,128]{2,1,0:T(8,128)}, u32[]{:S(2)}) copy-start(f32[1,256,128]{2,1,0:T(8,128)} %param.16) | copy-start | bytes 393220
  24.5 54.9 %all-to-all-start = ((f32[32,8,2048]{2,1,0:T(8,128)}), f32[32,8,2048]{2,1,0:T(8,128)S(1)}, u32[]{:S(2)}, u32[]{:S(2)}) async-start(f32[32,8,2048]{2,1,0:T(8,128)} %bitcast.25), calls=%async_computation | async-start | bytes 4194304 | tf_op jit(solution)/shard_map/all_to_all | solution.py:230
  33.3 9.0 %collective-permute-start.5 = (f32[1,256,128]{2,1,0:T(8,128)S(1)}, f32[1,256,128]{2,1,0:T(8,128)S(1)}, u32[]{:S(2)}, u32[]{:S(2)}) collective-permute-start(f32[1,256,128]{2,1,0:T(8,128)S(1)} %get-tuple-element.8), channel_id=1, source_target_pairs={{2,0},{3,1},{0,2},{1,3},{6,4},{7,5},{4,6},{5,7},{10,8},{11,9},{8,1... | collective-permute-start | bytes 393224 | tf_op jit(solution)/shard_map/ppermute | solution.py:31
  37.5 12.1 %collective-permute-start.6 = (f32[1,256,128]{2,1,0:T(8,128)S(1)}, f32[1,256,128]{2,1,0:T(8,128)S(1)}, u32[]{:S(2)}, u32[]{:S(2)}) collective-permute-start(f32[1,256,128]{2,1,0:T(8,128)S(1)} %get-tuple-element.8), channel_id=1, source_target_pairs={{3,0},{0,1},{1,2},{2,3},{7,4},{4,5},{5,6},{6,7},{11,8},{8,9},{9,10... | collective-permute-start | bytes 393224 | tf_op jit(solution)/shard_map/ppermute | solution.py:31
  38.1 11.4 %collective-permute-start.4 = (f32[1,256,128]{2,1,0:T(8,128)S(1)}, f32[1,256,128]{2,1,0:T(8,128)S(1)}, u32[]{:S(2)}, u32[]{:S(2)}) collective-permute-start(f32[1,256,128]{2,1,0:T(8,128)S(1)} %get-tuple-element.8), channel_id=1, source_target_pairs={{1,0},{2,1},{3,2},{0,3},{5,4},{6,5},{7,6},{4,7},{9,8},{10,9},{11,1... | collective-permute-start | bytes 393224 | tf_op jit(solution)/shard_map/ppermute | solution.py:31
  40.7 23.3 %collective-permute-start.1 = (f32[1,256,128]{2,1,0:T(8,128)S(1)}, f32[1,256,128]{2,1,0:T(8,128)S(1)}, u32[]{:S(2)}, u32[]{:S(2)}) collective-permute-start(f32[1,256,128]{2,1,0:T(8,128)S(1)} %get-tuple-element.9), channel_id=1, source_target_pairs={{1,0},{2,1},{3,2},{0,3},{5,4},{6,5},{7,6},{4,7},{9,8},{10,9},{11,1... | collective-permute-start | bytes 393224 | tf_op jit(solution)/shard_map/ppermute | solution.py:31
  40.7 23.3 %collective-permute-start.2 = (f32[1,256,128]{2,1,0:T(8,128)S(1)}, f32[1,256,128]{2,1,0:T(8,128)S(1)}, u32[]{:S(2)}, u32[]{:S(2)}) collective-permute-start(f32[1,256,128]{2,1,0:T(8,128)S(1)} %get-tuple-element.9), channel_id=1, source_target_pairs={{2,0},{3,1},{0,2},{1,3},{6,4},{7,5},{4,6},{5,7},{10,8},{11,9},{8,1... | collective-permute-start | bytes 393224 | tf_op jit(solution)/shard_map/ppermute | solution.py:31
  42.2 21.8 %collective-permute-start.3 = (f32[1,256,128]{2,1,0:T(8,128)S(1)}, f32[1,256,128]{2,1,0:T(8,128)}, u32[]{:S(2)}, u32[]{:S(2)}) collective-permute-start(f32[1,256,128]{2,1,0:T(8,128)S(1)} %get-tuple-element.9), channel_id=1, source_target_pairs={{3,0},{0,1},{1,2},{2,3},{7,4},{4,5},{5,6},{6,7},{11,8},{8,9},{9,10... | collective-permute-start | bytes 393224 | tf_op jit(solution)/shard_map/ppermute | solution.py:31
  79.4 1.3 copy-start

commit v6 on v5

--- a/solution.py
+++ b/solution.py
@@ -64,6 +64,29 @@
     return outr, outi
 
 
+BF16 = jnp.bfloat16
+
+
+def split(x):
+    hi = x.astype(BF16)
+    return hi, (x - hi.astype(F32)).astype(BF16)
+
+
+def dot3(a, b_hi, b_lo, dims=(((1,), (0,)), ((), ())), a_first=True):
+    a_hi, a_lo = split(a)
+    def one(x, y):
+        if a_first:
+            return lax.dot_general(x, y, dims, preferred_element_type=F32)
+        return lax.dot_general(y, x, dims, preferred_element_type=F32)
+    return one(a_hi, b_hi) + (one(a_lo, b_hi) + one(a_hi, b_lo))
+
+
+def halves(m):
+    hi = m.astype(BF16)
+    lo = (m - hi.astype(np.float32)).astype(BF16)
+    return jnp.asarray(hi), jnp.asarray(lo)
+
+
 def unit(m, n, sign):
     angle = (m % n).astype(F32) * F32(sign * 2.0 * math.pi / n)
     return jnp.cos(angle), jnp.sin(angle)
@@ -128,7 +151,7 @@
     return ar * br - ai * bi, ar * bi + ai * br
 
 
-def column_forward_kernel(blk_ref, hist_ref, t1c, t1s, t2c, t2s, lr_ref, li_ref, pac, pas, pbc, pbs,
+def column_forward_kernel(blk_ref, hist_ref, t1c, t1s, t2c, t2s, lrh, lrl, lih, lil, pac, pas, pbc, pbs,
                           out_ref, xs_ref):
     for p in range(2):
         xr, xi = [], []
@@ -148,8 +171,8 @@
     dims = (((1,), (1,)), ((), ()))
     for h in range(2):
         x = xs_ref[512 * h:512 * (h + 1), :]
-        ore = lax.dot_general(lr_ref[...], x, dims, precision=HIGHEST, preferred_element_type=F32)
-        oim = lax.dot_general(li_ref[...], x, dims, precision=HIGHEST, preferred_element_type=F32)
+        ore = dot3(x, lrh[...], lrl[...], dims, a_first=False)
+        oim = dot3(x, lih[...], lil[...], dims, a_first=False)
         ac = pac[:, 512 * h:512 * (h + 1)]
         as_ = pas[:, 512 * h:512 * (h + 1)]
         for d in range(32):
@@ -161,12 +184,12 @@
             out_ref[8 * d:8 * d + 8, 1024 * h + 512:1024 * h + 1024] = im
 
 
-def row_kernel(x_ref, twc_ref, tws_ref, bf_ref, bb_ref, chc_ref, chs_ref, pc_ref, ps_ref, out_ref, y_ref, w_ref):
+def row_kernel(x_ref, twc_ref, tws_ref, bfh, bfl, bbh, bbl, ph_ref, pc_ref, ps_ref, out_ref, y_ref, w_ref):
     for h in range(2):
-        row_half(h, x_ref, twc_ref, tws_ref, bf_ref, bb_ref, chc_ref, chs_ref, pc_ref, ps_ref, out_ref, y_ref, w_ref)
-
-
-def row_half(h, x_ref, twc_ref, tws_ref, bf_ref, bb_ref, chc_ref, chs_ref, pc_ref, ps_ref, out_ref, y_ref, w_ref):
+        row_half(h, x_ref, twc_ref, tws_ref, bfh, bfl, bbh, bbl, ph_ref, pc_ref, ps_ref, out_ref, y_ref, w_ref)
+
+
+def row_half(h, x_ref, twc_ref, tws_ref, bfh, bfl, bbh, bbl, ph_ref, pc_ref, ps_ref, out_ref, y_ref, w_ref):
     base = 1024 * h
     lanes = slice(512 * h, 512 * (h + 1))
     er = [x_ref[8 * d:8 * d + 8, base:base + 512] for d in range(32)]
@@ -177,11 +200,12 @@
         for j in range(4):
             y_ref[256 * j + 8 * g:256 * j + 8 * g + 8, 0:128] = a[:, 128 * j:128 * (j + 1)]
             y_ref[256 * j + 8 * g:256 * j + 8 * g + 8, 128:256] = b[:, 128 * j:128 * (j + 1)]
-    z = jnp.dot(y_ref[...], bf_ref[...], precision=HIGHEST, preferred_element_type=F32)
-    re, im = cmul(z[:, 0:128], z[:, 128:256], chc_ref[1024 * h:1024 * (h + 1), :], chs_ref[1024 * h:1024 * (h + 1), :])
+    z = dot3(y_ref[...], bfh[...], bfl[...])
+    phase = ph_ref[1024 * h:1024 * (h + 1), :]
+    re, im = cmul(z[:, 0:128], z[:, 128:256], jnp.cos(phase), jnp.sin(phase))
     y_ref[:, 0:128] = re
     y_ref[:, 128:256] = im
-    w_ref[...] = jnp.dot(y_ref[...], bb_ref[...], precision=HIGHEST, preferred_element_type=F32)
+    w_ref[...] = dot3(y_ref[...], bbh[...], bbl[...])
     gr, gi = [], []
     for g in range(32):
         a = jnp.concatenate([w_ref[256 * j + 8 * g:256 * j + 8 * g + 8, 0:128] for j in range(4)], axis=1)
@@ -196,11 +220,11 @@
         out_ref[8 * d:8 * d + 8, base + 512:base + 1024] = im
 
 
-def column_inverse_kernel(x_ref, m_ref, twc_ref, tws_ref, out_ref, s_ref):
+def column_inverse_kernel(x_ref, mh_ref, ml_ref, twc_ref, tws_ref, out_ref, s_ref):
     lhs_re = jnp.concatenate([x_ref[:, 0:512].T, x_ref[:, 1024:1536].T], axis=0)
     lhs_im = jnp.concatenate([x_ref[:, 512:1024].T, x_ref[:, 1536:2048].T], axis=0)
     lhs = jnp.concatenate([lhs_re, lhs_im], axis=1)
-    s_ref[...] = jnp.dot(lhs, m_ref[...], precision=HIGHEST, preferred_element_type=F32)
+    s_ref[...] = dot3(lhs, mh_ref[...], ml_ref[...])
     er, ei = [], []
     for k in range(32):
         rows = slice(32 * k, 32 * (k + 1))
@@ -258,22 +282,22 @@
     lr, li = send_matrices()
     (send,) = call(column_forward_kernel, [(256, 2048)], [(1024, 512)],
                    block, history, jnp.asarray(t1c), jnp.asarray(t1s), t2c, t2s,
-                   jnp.asarray(lr), jnp.asarray(li), pac, pas, pbc, pbs)
+                   *halves(lr), *halves(li), pac, pas, pbc, pbs)
     received = exchanged(send)
 
     chirp_phase, send = lax.optimization_barrier((chirp_phase, send))
-    ch_c, ch_s = [arranged(gathered(f(chirp_phase), "seg", 1)[0]) for f in (jnp.cos, jnp.sin)]
+    chirp = arranged(gathered(chirp_phase, "seg", 1)[0])
     back_c, back_s = unit((32 * (rows // 8) + lane % 32) * (kc_lane + 32 * (rows % 4)), LENGTH, 1)
 
     twc, tws = row_twiddle(-1)
     (sent,) = call(row_kernel, [(256, 2048)], [(1024, 256), (1024, 256)],
-                   received, jnp.asarray(twc), jnp.asarray(tws), jnp.asarray(row_block(-1)),
-                   jnp.asarray(row_block(1)), ch_c, ch_s, back_c, back_s)
+                   received, jnp.asarray(twc), jnp.asarray(tws), *halves(row_block(-1)),
+                   *halves(row_block(1)), chirp, back_c, back_s)
     returned = exchanged(sent)
 
     cc, cs = lane_twiddle(1, 256)
     (out,) = call(column_inverse_kernel, [(2, 2, ROWS_DEV, 3072)], [(1024, 512)],
-                  returned, jnp.asarray(receive_matrix()), jnp.asarray(cc), jnp.asarray(cs))
+                  returned, *halves(receive_matrix()), jnp.asarray(cc), jnp.asarray(cs))
     return out[None, None]
 
 

time: 136 us -> 117 us (0.86)
  local copies, waits for them, and re-layouts: 31.9 us -> 13.9 us
  waiting for transfers between devices: 8.29 us -> 16.2 us
  starting transfers between devices: 22.3 us -> 17.4 us
  Pallas kernels: 25.9 us -> 22.7 us
  other arithmetic: 10.3 us -> 8.79 us
    ppermute x6 -> x3, waiting for transfers between devices: 0.02 us -> 7.99 us  [gathered(): pieces.append(lax.ppermute(block, axis, route))]
    broadcast_in_dim x2 -> x1, local copies, waits for them, and re-layouts: 8.55 us -> 2.68 us  [arranged(): jnp.broadcast_to(table[:, :, None], (8, 32, 2, 4, 4, 32)).reshape(2048, 128)]
    ppermute x6 -> x3, starting transfers between devices: 10.4 us -> 5.52 us  [gathered(): pieces.append(lax.ppermute(block, axis, route))]
    reshape x2 -> x1, local copies, waits for them, and re-layouts: 9.07 us -> 4.54 us  [arranged(): jnp.broadcast_to(table[:, :, None], (8, 32, 2, 4, 4, 32)).reshape(2048, 128)]
    transpose x2 -> x1, local copies, waits for them, and re-layouts: 6.26 us -> 2.48 us  [arranged(): table = table.reshape(32, 32, 4, 8, 4).transpose(3, 1, 2, 4, 0)]
    pallas_call x3, Pallas kernels: 25.9 us -> 22.7 us  [call(): pl.pallas_call(kernel, out_shape=[jax.ShapeDtypeStruct(s, F32) for s in o...]
    another operation x2 -> x1, local copies, waits for them, and re-layouts: 3.87 us -> 1.93 us  [arranged(): table = table.reshape(32, 32, 4, 8, 4).transpose(3, 1, 2, 4, 0)]
    concatenate x2 -> x0, other arithmetic: 1.6 us -> none  [gathered(): ordered = jnp.roll(ahead, lax.axis_index(axis), axis=0)]
  transfers between devices with their start and end apart: 8 -> 5, of which waited for: 1 -> 4; matrix products, arithmetic and copies ran while one was open for 29% -> 18% of each run, Pallas kernels for 0% -> 0%
where the time goes in v6:
time: 117 us; the launch traced here: 115 us
  blocking collectives  35.9 us (31%)
  Pallas kernels  22.7 us (19%)
  starting transfers between devices  17.4 us (15%)
  waiting for transfers between devices  16.2 us (14%)
  local copies, waits for them, and re-layouts  13.9 us (12%)
  other arithmetic  8.79 us (8%)
    all_to_all x1, blocking collectives, exchanged(): lax.all_to_all(block.reshape(32, rows // 32, width), 'band', 0, 0, tiled=...  35.9 us
    pallas_call x3, Pallas kernels, call(): pl.pallas_call(kernel, out_shape=[jax.ShapeDtypeStruct(s, F32) for s in o...  22.7 us
    sin x4, other arithmetic, unit(): return (jnp.cos(angle), jnp.sin(angle))  8.76 us
    all_to_all x1, starting transfers between devices, exchanged(): lax.all_to_all(block.reshape(32, rows // 32, width), 'band', 0, 0, tiled=...  8.3 us
    ppermute x1, waiting for transfers between devices, passed_along(): return lax.ppermute(block, axis, route)  8.22 us
    ppermute x3, waiting for transfers between devices, gathered(): pieces.append(lax.ppermute(block, axis, route))  7.99 us
    ppermute x3, starting transfers between devices, gathered(): pieces.append(lax.ppermute(block, axis, route))  5.52 us
    reshape x1, local copies, waits for them, and re-layouts, arranged(): jnp.broadcast_to(table[:, :, None], (8, 32, 2, 4, 4, 32)).reshape(2048, 128)  4.54 us
  transfers between devices with their start and end apart: 5, of which 4 were waited for; matrix products, arithmetic and copies ran while one was open for 18% of the time, Pallas kernels for 0%

profile of v6, /device:TPU:0, one launch (start us, length us, event | category | flops | bytes accessed | tf_op | source)
XLA Modules:
  0.0 115.1 jit_solution(17543594726811322462)
XLA Ops:
  0.0 1.1 slice.4
  1.1 3.6 %collective-permute-start = (f32[2,2,32,1024]{3,2,1,0:T(8,128)S(1)}, f32[2,2,32,1024]{3,2,1,0:T(8,128)S(1)}, u32[]{:S(2)}, u32[]{:S(2)}) collective-permute-start(f32[2,2,32,1024]{3,2,1,0:T(8,128)S(1)} %slice.4), channel_id=1, source_target_pairs={{0,1},{1,2},{2,3},{4,5},{5,6},{6,7},{8,9},{9,10},{10,11},{12,13},{... | collective-permute-start | bytes 1572872 | tf_op jit(solution)/shard_map/ppermute | solution.py:23
  4.7 0.8 fusion.24
  5.5 0.8 fusion.19
  6.4 1.2 %fusion.11 = (f32[32,1024]{1,0:T(8,128)}, f32[32,1024]{1,0:T(8,128)}) fusion(s32[1024]{0:T(1024)S(1)} %get-tuple-element.15), kind=kLoop, calls=%fused_computation.25 | loop fusion | flops 458752 | bytes 266240 | tf_op jit(solution)/shard_map/sin | solution.py:92
  7.6 8.2 %collective-permute-done.hist_ref = f32[2,2,32,1024]{3,2,1,0:T(8,128)S(1)} collective-permute-done((f32[2,2,32,1024]{3,2,1,0:T(8,128)S(1)}, f32[2,2,32,1024]{3,2,1,0:T(8,128)S(1)}, u32[]{:S(2)}, u32[]{:S(2)}) %collective-permute-start) | collective-permute-done | bytes 524320 | tf_op jit(solution)/shard_map/ppermute | solution.py:23
  15.8 0.0 copy-start.1
  15.8 0.8 copy-done.1
  16.6 6.2 %shard_map.172 = f32[256,2048]{1,0:T(8,128)} custom-call(f32[2,2,32,3072]{3,2,1,0:T(8,128)} %bitcast.26, f32[2,2,32,1024]{3,2,1,0:T(8,128)} %copy-done.1, f32[32,128]{1,0:T(8,128)} %constant.178.clone.t1c, f32[32,128]{1,0:T(8,128)} %constant.179.clone.t1s, f32[32,32]{1,0:T(8,128)} %get-tuple-element.14.t2c, f32[32,32]{1,0:T(8,128)} %get-tuple-element.13.t2s, ...), custom_call_target="tpu_custom_call" | custom-call | tf_op jit(solution)/shard_map/pallas_call | solution.py:244
  22.8 8.3 %all-to-all-start = ((f32[32,8,2048]{2,1,0:T(8,128)}), f32[32,8,2048]{2,1,0:T(8,128)}, u32[]{:S(2)}, u32[]{:S(2)}) async-start(f32[32,8,2048]{2,1,0:T(8,128)} %bitcast.23), calls=%async_computation | async-start | bytes 4194304 | tf_op jit(solution)/shard_map/all_to_all | solution.py:254
  31.1 0.0 copy-start
  31.1 5.9 %fusion.3 = (f32[256,1024]{1,0:T(8,128)}, f32[256,1024]{1,0:T(8,128)}) fusion(s32[256]{0:T(256)S(1)} %get-tuple-element.19, s32[1024]{0:T(1024)S(1)} %get-tuple-element.18, s32[1024]{0:T(1024)S(1)} %get-tuple-element.17, s32[256]{0:T(256)S(1)} %get-tuple-element.20), kind=kLoop, calls=%fused_computation.6 | loop fusion | flops 4194304 | bytes 2107392 | tf_op jit(solution)/shard_map/sin | solution.py:92
  37.0 0.0 copy-done
  37.0 3.9 %collective-permute-start.1 = (f32[1,256,128]{2,1,0:T(8,128)S(1)}, f32[1,256,128]{2,1,0:T(8,128)S(1)}, u32[]{:S(2)}, u32[]{:S(2)}) collective-permute-start(f32[1,256,128]{2,1,0:T(8,128)S(1)} %copy-done), channel_id=1, source_target_pairs={{1,0},{2,1},{3,2},{0,3},{5,4},{6,5},{7,6},{4,7},{9,8},{10,9},{11,1... | collective-permute-start | bytes 393224 | tf_op jit(solution)/shard_map/ppermute | solution.py:31
  40.9 0.6 collective-permute-start.2
  41.6 1.0 collective-permute-start.3
  42.6 4.3 %collective-permute-done.1 = f32[1,256,128]{2,1,0:T(8,128)S(1)} collective-permute-done((f32[1,256,128]{2,1,0:T(8,128)S(1)}, f32[1,256,128]{2,1,0:T(8,128)S(1)}, u32[]{:S(2)}, u32[]{:S(2)}) %collective-permute-start.1) | collective-permute-done | bytes 131104 | tf_op jit(solution)/shard_map/ppermute | solution.py:31
  46.9 2.0 %collective-permute-done.2 = f32[1,256,128]{2,1,0:T(8,128)S(1)} collective-permute-done((f32[1,256,128]{2,1,0:T(8,128)S(1)}, f32[1,256,128]{2,1,0:T(8,128)S(1)}, u32[]{:S(2)}, u32[]{:S(2)}) %collective-permute-start.2) | collective-permute-done | bytes 131104 | tf_op jit(solution)/shard_map/ppermute | solution.py:31
  48.9 1.7 %collective-permute-done.3 = f32[1,256,128]{2,1,0:T(8,128)S(1)} collective-permute-done((f32[1,256,128]{2,1,0:T(8,128)S(1)}, f32[1,256,128]{2,1,0:T(8,128)S(1)}, u32[]{:S(2)}, u32[]{:S(2)}) %collective-permute-start.3) | collective-permute-done | bytes 131104 | tf_op jit(solution)/shard_map/ppermute | solution.py:31
  50.7 0.2 copy.19
  51.0 1.9 %reshape_squeeze_reshape_transpose.3 = f32[32,32,4,8,4]{1,0,4,3,2:T(8,128)} reshape(f32[4,1,256,128]{2,0,3,1:T(4,128)S(1)} %copy.19) | data formatting | bytes 1048576 | tf_op jit(solution)/shard_map/reshape;squeeze;reshape;transpose | solution.py:259
  52.9 2.5 %copy.20 = f32[8,32,4,4,32]{4,3,2,1,0:T(4,128)S(1)} copy(f32[8,32,4,4,32]{1,4,3,0,2:T(8,128)} %bitcast.22) | data formatting | bytes 1048576 | tf_op jit(solution)/shard_map/transpose | solution.py:259
  55.4 2.7 %broadcast_in_dim.4 = f32[8,32,2,4,4,32]{5,4,3,2,1,0:T(4,128)} broadcast(f32[8,32,4,4,32]{4,3,2,1,0:T(4,128)S(1)} %copy.20), dimensions={0,1,3,4,5} | broadcast | bytes 1572864 | tf_op jit(solution)/shard_map/broadcast_in_dim | solution.py:260
  58.1 4.5 %reshape.156.ph_ref = f32[2048,128]{1,0:T(8,128)} reshape(f32[8,32,2,4,4,32]{5,4,3,2,1,0:T(4,128)} %broadcast_in_dim.4) | data formatting | bytes 2097152 | tf_op jit(solution)/shard_map/reshape | solution.py:260
  62.6 0.0 all-to-all-done
  62.6 11.2 %shard_map.173 = f32[256,2048]{1,0:T(8,128)} custom-call(f32[256,2048]{1,0:T(8,128)} %bitcast.2.x_ref, f32[32,512]{1,0:T(8,128)} %constant.184.clone.twc_ref, f32[32,512]{1,0:T(8,128)} %constant.185.clone.tws_ref, bf16[256,256]{1,0:T(8,128)(2,1)} %constant.186.clone.bfh, bf16[256,256]{1,0:T(8,128)(2,1)} %constant.187.clone.bfl, ...), custom_call_target="tpu_custom_call" | custom-call | tf_op jit(solution)/shard_map/pallas_call | solution.py:244
  73.8 35.9 %all_to_all.10 = f32[32,8,2048]{2,1,0:T(8,128)} all-to-all(f32[32,8,2048]{2,1,0:T(8,128)} %bitcast.24), channel_id=1, replica_groups=mesh['band'=32,'seg'=4] {'band'}, dimensions={0} | all-to-all | bytes 4194304 | tf_op jit(solution)/shard_map/all_to_all | solution.py:254
  109.7 5.4 %shard_map.174 = f32[2,2,32,3072]{3,2,1,0:T(8,128)} custom-call(f32[256,2048]{1,0:T(8,128)} %bitcast.21, bf16[512,512]{1,0:T(8,128)(2,1)} %constant.190.clone.mh_ref, bf16[512,512]{1,0:T(8,128)(2,1)} %constant.191.clone.ml_ref, f32[32,256]{1,0:T(8,128)} %constant.192.clone.twc_ref, f32[32,256]{1,0:T(8,128)} %constant.193.clone.tws_ref), custom_call_target="tpu_custom_call" | custom-call | tf_op jit(solution)/shard_map/pallas_call | solution.py:244
  (14 shorter events, 0.2 us)
Async XLA Ops:
  1.1 14.7 %collective-permute-start = (f32[2,2,32,1024]{3,2,1,0:T(8,128)S(1)}, f32[2,2,32,1024]{3,2,1,0:T(8,128)S(1)}, u32[]{:S(2)}, u32[]{:S(2)}) collective-permute-start(f32[2,2,32,1024]{3,2,1,0:T(8,128)S(1)} %slice.4), channel_id=1, source_target_pairs={{0,1},{1,2},{2,3},{4,5},{5,6},{6,7},{8,9},{9,10},{10,11},{12,13},{... | collective-permute-start | bytes 1572872 | tf_op jit(solution)/shard_map/ppermute | solution.py:23
  15.8 0.8 copy-start.1
  22.8 39.8 %all-to-all-start = ((f32[32,8,2048]{2,1,0:T(8,128)}), f32[32,8,2048]{2,1,0:T(8,128)}, u32[]{:S(2)}, u32[]{:S(2)}) async-start(f32[32,8,2048]{2,1,0:T(8,128)} %bitcast.23), calls=%async_computation | async-start | bytes 4194304 | tf_op jit(solution)/shard_map/all_to_all | solution.py:254
  31.1 5.9 %copy-start = (f32[1,256,128]{2,1,0:T(8,128)S(1)}, f32[1,256,128]{2,1,0:T(8,128)}, u32[]{:S(2)}) copy-start(f32[1,256,128]{2,1,0:T(8,128)} %param.19) | copy-start | bytes 393220
  37.0 9.8 %collective-permute-start.1 = (f32[1,256,128]{2,1,0:T(8,128)S(1)}, f32[1,256,128]{2,1,0:T(8,128)S(1)}, u32[]{:S(2)}, u32[]{:S(2)}) collective-permute-start(f32[1,256,128]{2,1,0:T(8,128)S(1)} %copy-done), channel_id=1, source_target_pairs={{1,0},{2,1},{3,2},{0,3},{5,4},{6,5},{7,6},{4,7},{9,8},{10,9},{11,1... | collective-permute-start | bytes 393224 | tf_op jit(solution)/shard_map/ppermute | solution.py:31
  40.9 7.9 %collective-permute-start.2 = (f32[1,256,128]{2,1,0:T(8,128)S(1)}, f32[1,256,128]{2,1,0:T(8,128)S(1)}, u32[]{:S(2)}, u32[]{:S(2)}) collective-permute-start(f32[1,256,128]{2,1,0:T(8,128)S(1)} %copy-done), channel_id=1, source_target_pairs={{2,0},{3,1},{0,2},{1,3},{6,4},{7,5},{4,6},{5,7},{10,8},{11,9},{8,1... | collective-permute-start | bytes 393224 | tf_op jit(solution)/shard_map/ppermute | solution.py:31
  41.6 9.0 %collective-permute-start.3 = (f32[1,256,128]{2,1,0:T(8,128)S(1)}, f32[1,256,128]{2,1,0:T(8,128)S(1)}, u32[]{:S(2)}, u32[]{:S(2)}) collective-permute-start(f32[1,256,128]{2,1,0:T(8,128)S(1)} %copy-done), channel_id=1, source_target_pairs={{3,0},{0,1},{1,2},{2,3},{7,4},{4,5},{5,6},{6,7},{11,8},{8,9},{9,10... | collective-permute-start | bytes 393224 | tf_op jit(solution)/shard_map/ppermute | solution.py:31

commit v7 on v6

--- a/solution.py
+++ b/solution.py
@@ -184,12 +184,12 @@
             out_ref[8 * d:8 * d + 8, 1024 * h + 512:1024 * h + 1024] = im
 
 
-def row_kernel(x_ref, twc_ref, tws_ref, bfh, bfl, bbh, bbl, ph_ref, pc_ref, ps_ref, out_ref, y_ref, w_ref):
+def row_kernel(x_ref, twc_ref, tws_ref, bfh, bfl, bbh, bbl, chc_ref, chs_ref, pc_ref, ps_ref, out_ref, y_ref, w_ref):
     for h in range(2):
-        row_half(h, x_ref, twc_ref, tws_ref, bfh, bfl, bbh, bbl, ph_ref, pc_ref, ps_ref, out_ref, y_ref, w_ref)
-
-
-def row_half(h, x_ref, twc_ref, tws_ref, bfh, bfl, bbh, bbl, ph_ref, pc_ref, ps_ref, out_ref, y_ref, w_ref):
+        row_half(h, x_ref, twc_ref, tws_ref, bfh, bfl, bbh, bbl, chc_ref, chs_ref, pc_ref, ps_ref, out_ref, y_ref, w_ref)
+
+
+def row_half(h, x_ref, twc_ref, tws_ref, bfh, bfl, bbh, bbl, chc_ref, chs_ref, pc_ref, ps_ref, out_ref, y_ref, w_ref):
     base = 1024 * h
     lanes = slice(512 * h, 512 * (h + 1))
     er = [x_ref[8 * d:8 * d + 8, base:base + 512] for d in range(32)]
@@ -197,20 +197,28 @@
     fr, fi = fft_list(er, ei, -1)
     for g in range(32):
         a, b = cmul(fr[g], fi[g], twc_ref[g:g + 1, :], tws_ref[g:g + 1, :])
-        for j in range(4):
-            y_ref[256 * j + 8 * g:256 * j + 8 * g + 8, 0:128] = a[:, 128 * j:128 * (j + 1)]
-            y_ref[256 * j + 8 * g:256 * j + 8 * g + 8, 128:256] = b[:, 128 * j:128 * (j + 1)]
+        for p in range(2):
+            for j in range(4):
+                at = 512 * p + 128 * j + 4 * g
+                y_ref[at:at + 4, 0:128] = a[4 * p:4 * p + 4, 128 * j:128 * (j + 1)]
+                y_ref[at:at + 4, 128:256] = b[4 * p:4 * p + 4, 128 * j:128 * (j + 1)]
     z = dot3(y_ref[...], bfh[...], bfl[...])
-    phase = ph_ref[1024 * h:1024 * (h + 1), :]
-    re, im = cmul(z[:, 0:128], z[:, 128:256], jnp.cos(phase), jnp.sin(phase))
-    y_ref[:, 0:128] = re
-    y_ref[:, 128:256] = im
+    c = chc_ref[512 * h:512 * (h + 1), :]
+    s = chs_ref[512 * h:512 * (h + 1), :]
+    for p in range(2):
+        rows = slice(512 * p, 512 * (p + 1))
+        re, im = cmul(z[rows, 0:128], z[rows, 128:256], c, s)
+        y_ref[rows, 0:128] = re
+        y_ref[rows, 128:256] = im
     w_ref[...] = dot3(y_ref[...], bbh[...], bbl[...])
     gr, gi = [], []
     for g in range(32):
-        a = jnp.concatenate([w_ref[256 * j + 8 * g:256 * j + 8 * g + 8, 0:128] for j in range(4)], axis=1)
-        b = jnp.concatenate([w_ref[256 * j + 8 * g:256 * j + 8 * g + 8, 128:256] for j in range(4)], axis=1)
-        a, b = cmul(a, b, twc_ref[g:g + 1, :], -tws_ref[g:g + 1, :])
+        pa, pb = [], []
+        for j in range(4):
+            lo, hi = 128 * j + 4 * g, 512 + 128 * j + 4 * g
+            pa.append(jnp.concatenate([w_ref[lo:lo + 4, 0:128], w_ref[hi:hi + 4, 0:128]], axis=0))
+            pb.append(jnp.concatenate([w_ref[lo:lo + 4, 128:256], w_ref[hi:hi + 4, 128:256]], axis=0))
+        a, b = cmul(jnp.concatenate(pa, axis=1), jnp.concatenate(pb, axis=1), twc_ref[g:g + 1, :], -tws_ref[g:g + 1, :])
         gr.append(a)
         gi.append(b)
     ur, ui = fft_list(gr, gi, 1)
@@ -256,8 +264,7 @@
 
 
 def arranged(table):
-    table = table.reshape(32, 32, 4, 8, 4).transpose(3, 1, 2, 4, 0)
-    return jnp.broadcast_to(table[:, :, None], (8, 32, 2, 4, 4, 32)).reshape(2048, 128)
+    return table.reshape(32, 32, 4, 8, 4).transpose(3, 1, 2, 4, 0).reshape(1024, 128)
 
 
 def per_device(voltages, chirp_phase):
@@ -286,13 +293,14 @@
     received = exchanged(send)
 
     chirp_phase, send = lax.optimization_barrier((chirp_phase, send))
-    chirp = arranged(gathered(chirp_phase, "seg", 1)[0])
+    phases = gathered(chirp_phase, "seg", 1)[0]
+    ch_c, ch_s = arranged(jnp.cos(phases)), arranged(jnp.sin(phases))
     back_c, back_s = unit((32 * (rows // 8) + lane % 32) * (kc_lane + 32 * (rows % 4)), LENGTH, 1)
 
     twc, tws = row_twiddle(-1)
     (sent,) = call(row_kernel, [(256, 2048)], [(1024, 256), (1024, 256)],
                    received, jnp.asarray(twc), jnp.asarray(tws), *halves(row_block(-1)),
-                   *halves(row_block(1)), chirp, back_c, back_s)
+                   *halves(row_block(1)), ch_c, ch_s, back_c, back_s)
     returned = exchanged(sent)
 
     cc, cs = lane_twiddle(1, 256)

time: 117 us -> 113 us (0.966)
  Pallas kernels: 22.7 us -> 19.6 us
  waiting for transfers between devices: 16.2 us -> 13.3 us
  local copies, waits for them, and re-layouts: 13.9 us -> 15.6 us
  starting transfers between devices: 17.4 us -> 18.6 us
    pallas_call x3, Pallas kernels: 22.7 us -> 19.6 us  [call(): pl.pallas_call(kernel, out_shape=[jax.ShapeDtypeStruct(s, F32) for s in o...]
    ppermute x3, waiting for transfers between devices: 7.99 us -> 5.01 us  [gathered(): pieces.append(lax.ppermute(block, axis, route))]
    sin x0 -> x3, local copies, waits for them, and re-layouts: none -> 2.69 us  [per_device(): ch_c, ch_s = (arranged(jnp.cos(phases)), arranged(jnp.sin(phases)))]
    broadcast_in_dim x1 -> x0, local copies, waits for them, and re-layouts: 2.68 us -> none  [arranged(): jnp.broadcast_to(table[:, :, None], (8, 32, 2, 4, 4, 32)).reshape(2048, 128)]
    another operation x1 -> x0, local copies, waits for them, and re-layouts: 1.93 us -> none  [arranged(): table = table.reshape(32, 32, 4, 8, 4).transpose(3, 1, 2, 4, 0)]
    reshape x1 -> x2, local copies, waits for them, and re-layouts: 4.54 us -> 6.1 us  [arranged(): table.reshape(32, 32, 4, 8, 4).transpose(3, 1, 2, 4, 0).reshape(1024, 128)]
    transpose x1 -> x2, local copies, waits for them, and re-layouts: 2.48 us -> 4.04 us  [arranged(): table.reshape(32, 32, 4, 8, 4).transpose(3, 1, 2, 4, 0).reshape(1024, 128)]
    ppermute x3, starting transfers between devices: 5.52 us -> 6.73 us  [gathered(): pieces.append(lax.ppermute(block, axis, route))]
  transfers between devices with their start and end apart: 5 -> 5, of which waited for: 4 -> 3; matrix products, arithmetic and copies ran while one was open for 18% -> 20% of each run, Pallas kernels for 0% -> 0%
where the time goes in v7:
time: 113 us; the launch traced here: 112 us
  blocking collectives  35.9 us (32%)
  Pallas kernels  19.6 us (17%)
  starting transfers between devices  18.6 us (16%)
  local copies, waits for them, and re-layouts  15.6 us (14%)
  waiting for transfers between devices  13.3 us (12%)
  other arithmetic  8.7 us (8%)
    all_to_all x1, blocking collectives, exchanged(): lax.all_to_all(block.reshape(32, rows // 32, width), 'band', 0, 0, tiled=...  35.9 us
    pallas_call x3, Pallas kernels, call(): pl.pallas_call(kernel, out_shape=[jax.ShapeDtypeStruct(s, F32) for s in o...  19.6 us
    sin x4, other arithmetic, unit(): return (jnp.cos(angle), jnp.sin(angle))  8.67 us
    all_to_all x1, starting transfers between devices, exchanged(): lax.all_to_all(block.reshape(32, rows // 32, width), 'band', 0, 0, tiled=...  8.29 us
    ppermute x1, waiting for transfers between devices, passed_along(): return lax.ppermute(block, axis, route)  8.24 us
    ppermute x3, starting transfers between devices, gathered(): pieces.append(lax.ppermute(block, axis, route))  6.73 us
    reshape x2, local copies, waits for them, and re-layouts, arranged(): table.reshape(32, 32, 4, 8, 4).transpose(3, 1, 2, 4, 0).reshape(1024, 128)  6.1 us
    ppermute x3, waiting for transfers between devices, gathered(): pieces.append(lax.ppermute(block, axis, route))  5.01 us
  transfers between devices with their start and end apart: 5, of which 3 were waited for; matrix products, arithmetic and copies ran while one was open for 20% of the time, Pallas kernels for 0%

profile of v7, /device:TPU:0, one launch (start us, length us, event | category | flops | bytes accessed | tf_op | source)
XLA Modules:
  0.0 111.9 jit_solution(4971949865252833193)
XLA Ops:
  0.0 1.1 slice.4
  1.1 3.6 %collective-permute-start = (f32[2,2,32,1024]{3,2,1,0:T(8,128)S(1)}, f32[2,2,32,1024]{3,2,1,0:T(8,128)S(1)}, u32[]{:S(2)}, u32[]{:S(2)}) collective-permute-start(f32[2,2,32,1024]{3,2,1,0:T(8,128)S(1)} %slice.4), channel_id=1, source_target_pairs={{0,1},{1,2},{2,3},{4,5},{5,6},{6,7},{8,9},{9,10},{10,11},{12,13},{... | collective-permute-start | bytes 1572872 | tf_op jit(solution)/shard_map/ppermute | solution.py:23
  4.7 0.8 fusion.24
  5.5 0.8 fusion.19
  6.3 1.2 %fusion.11 = (f32[32,1024]{1,0:T(8,128)}, f32[32,1024]{1,0:T(8,128)}) fusion(s32[1024]{0:T(1024)S(1)} %get-tuple-element.17), kind=kLoop, calls=%fused_computation.27 | loop fusion | flops 458752 | bytes 266240 | tf_op jit(solution)/shard_map/sin | solution.py:92
  7.6 8.2 %collective-permute-done.hist_ref = f32[2,2,32,1024]{3,2,1,0:T(8,128)S(1)} collective-permute-done((f32[2,2,32,1024]{3,2,1,0:T(8,128)S(1)}, f32[2,2,32,1024]{3,2,1,0:T(8,128)S(1)}, u32[]{:S(2)}, u32[]{:S(2)}) %collective-permute-start) | collective-permute-done | bytes 524320 | tf_op jit(solution)/shard_map/ppermute | solution.py:23
  15.8 0.0 copy-start.1
  15.8 0.8 copy-done.1
  16.6 6.2 %shard_map.172 = f32[256,2048]{1,0:T(8,128)} custom-call(f32[2,2,32,3072]{3,2,1,0:T(8,128)} %bitcast.30, f32[2,2,32,1024]{3,2,1,0:T(8,128)} %copy-done.1, f32[32,128]{1,0:T(8,128)} %constant.178.clone.t1c, f32[32,128]{1,0:T(8,128)} %constant.179.clone.t1s, f32[32,32]{1,0:T(8,128)} %get-tuple-element.16.t2c, f32[32,32]{1,0:T(8,128)} %get-tuple-element.15.t2s, ...), custom_call_target="tpu_custom_call" | custom-call | tf_op jit(solution)/shard_map/pallas_call | solution.py:252
  22.8 8.3 %all-to-all-start = ((f32[32,8,2048]{2,1,0:T(8,128)}), f32[32,8,2048]{2,1,0:T(8,128)}, u32[]{:S(2)}, u32[]{:S(2)}) async-start(f32[32,8,2048]{2,1,0:T(8,128)} %bitcast.27), calls=%async_computation | async-start | bytes 4194304 | tf_op jit(solution)/shard_map/all_to_all | solution.py:262
  31.1 0.0 copy-start
  31.1 5.8 %fusion.3 = (f32[256,1024]{1,0:T(8,128)}, f32[256,1024]{1,0:T(8,128)}) fusion(s32[256]{0:T(256)S(1)} %get-tuple-element.21, s32[1024]{0:T(1024)S(1)} %get-tuple-element.20, s32[1024]{0:T(1024)S(1)} %get-tuple-element.19, s32[256]{0:T(256)S(1)} %get-tuple-element.22), kind=kLoop, calls=%fused_computation.6 | loop fusion | flops 4194304 | bytes 2107392 | tf_op jit(solution)/shard_map/sin | solution.py:92
  37.0 0.0 copy-done
  37.0 2.5 %collective-permute-start.3 = (f32[1,256,128]{2,1,0:T(8,128)S(1)}, f32[1,256,128]{2,1,0:T(8,128)S(1)}, u32[]{:S(2)}, u32[]{:S(2)}) collective-permute-start(f32[1,256,128]{2,1,0:T(8,128)S(1)} %copy-done), channel_id=1, source_target_pairs={{3,0},{0,1},{1,2},{2,3},{7,4},{4,5},{5,6},{6,7},{11,8},{8,9},{9,10... | collective-permute-start | bytes 393224 | tf_op jit(solution)/shard_map/ppermute | solution.py:31
  39.4 2.9 %collective-permute-start.2 = (f32[1,256,128]{2,1,0:T(8,128)S(1)}, f32[1,256,128]{2,1,0:T(8,128)S(1)}, u32[]{:S(2)}, u32[]{:S(2)}) collective-permute-start(f32[1,256,128]{2,1,0:T(8,128)S(1)} %copy-done), channel_id=1, source_target_pairs={{2,0},{3,1},{0,2},{1,3},{6,4},{7,5},{4,6},{5,7},{10,8},{11,9},{8,1... | collective-permute-start | bytes 393224 | tf_op jit(solution)/shard_map/ppermute | solution.py:31
  42.3 1.3 %collective-permute-start.1 = (f32[1,256,128]{2,1,0:T(8,128)S(1)}, f32[1,256,128]{2,1,0:T(8,128)S(1)}, u32[]{:S(2)}, u32[]{:S(2)}) collective-permute-start(f32[1,256,128]{2,1,0:T(8,128)S(1)} %copy-done), channel_id=1, source_target_pairs={{1,0},{2,1},{3,2},{0,3},{5,4},{6,5},{7,6},{4,7},{9,8},{10,9},{11,1... | collective-permute-start | bytes 393224 | tf_op jit(solution)/shard_map/ppermute | solution.py:31
  43.7 4.5 %collective-permute-done.1 = f32[1,256,128]{2,1,0:T(8,128)S(1)} collective-permute-done((f32[1,256,128]{2,1,0:T(8,128)S(1)}, f32[1,256,128]{2,1,0:T(8,128)S(1)}, u32[]{:S(2)}, u32[]{:S(2)}) %collective-permute-start.1) | collective-permute-done | bytes 131104 | tf_op jit(solution)/shard_map/ppermute | solution.py:31
  48.2 0.5 collective-permute-done.2
  48.7 0.0 collective-permute-done.3
  48.9 1.9 %dynamic-slice_sine_fusion = (f32[4,1,256,128]{3,2,1,0:T(8,128)S(1)}, f32[4,1,256,128]{3,2,1,0:T(8,128)S(1)}) fusion(f32[8,1,256,128]{3,2,1,0:T(8,128)S(1)} %bitcast_dynamic-update-slice_fusion.1, s32[]{:T(128)S(6)} %select_n.106), kind=kLoop, calls=%fused_computation.8 | loop fusion | bytes 1572868 | tf_op jit(solution)/shard_map/sin | solution.py:297
  50.7 0.2 copy.23
  51.0 0.2 copy.21
  51.2 0.6 cos.23
  51.8 2.0 %copy.22 = f32[8,32,4,4,32]{4,3,2,1,0:T(4,128)} copy(f32[8,32,4,4,32]{1,4,3,0,2:T(8,128)S(1)} %bitcast.25) | data formatting | bytes 1048576 | tf_op jit(solution)/shard_map/transpose | solution.py:267
  53.8 3.1 %reshape.164.chc_ref = f32[1024,128]{1,0:T(8,128)} reshape(f32[8,32,4,4,32]{4,3,2,1,0:T(4,128)} %copy.22) | data formatting | bytes 1048576 | tf_op jit(solution)/shard_map/reshape | solution.py:267
  56.9 0.6 sin.23
  57.5 2.0 %copy.24 = f32[8,32,4,4,32]{4,3,2,1,0:T(4,128)} copy(f32[8,32,4,4,32]{1,4,3,0,2:T(8,128)S(1)} %bitcast.26) | data formatting | bytes 1048576 | tf_op jit(solution)/shard_map/transpose | solution.py:267
  59.5 3.0 %reshape.165.chs_ref = f32[1024,128]{1,0:T(8,128)} reshape(f32[8,32,4,4,32]{4,3,2,1,0:T(4,128)} %copy.24) | data formatting | bytes 1048576 | tf_op jit(solution)/shard_map/reshape | solution.py:267
  62.5 0.0 all-to-all-done
  62.5 8.1 %shard_map.173 = f32[256,2048]{1,0:T(8,128)} custom-call(f32[256,2048]{1,0:T(8,128)} %bitcast.2.x_ref, f32[32,512]{1,0:T(8,128)} %constant.184.clone.twc_ref, f32[32,512]{1,0:T(8,128)} %constant.185.clone.tws_ref, bf16[256,256]{1,0:T(8,128)(2,1)} %constant.186.clone.bfh, bf16[256,256]{1,0:T(8,128)(2,1)} %constant.187.clone.bfl, ...), custom_call_target="tpu_custom_call" | custom-call | tf_op jit(solution)/shard_map/pallas_call | solution.py:252
  70.6 35.9 %all_to_all.10 = f32[32,8,2048]{2,1,0:T(8,128)} all-to-all(f32[32,8,2048]{2,1,0:T(8,128)} %bitcast.28), channel_id=1, replica_groups=mesh['band'=32,'seg'=4] {'band'}, dimensions={0} | all-to-all | bytes 4194304 | tf_op jit(solution)/shard_map/all_to_all | solution.py:262
  106.5 5.4 %shard_map.174 = f32[2,2,32,3072]{3,2,1,0:T(8,128)} custom-call(f32[256,2048]{1,0:T(8,128)} %bitcast.24, bf16[512,512]{1,0:T(8,128)(2,1)} %constant.190.clone.mh_ref, bf16[512,512]{1,0:T(8,128)(2,1)} %constant.191.clone.ml_ref, f32[32,256]{1,0:T(8,128)} %constant.192.clone.twc_ref, f32[32,256]{1,0:T(8,128)} %constant.193.clone.tws_ref), custom_call_target="tpu_custom_call" | custom-call | tf_op jit(solution)/shard_map/pallas_call | solution.py:252
  (13 shorter events, 0.1 us)
Async XLA Ops:
  1.1 14.7 %collective-permute-start = (f32[2,2,32,1024]{3,2,1,0:T(8,128)S(1)}, f32[2,2,32,1024]{3,2,1,0:T(8,128)S(1)}, u32[]{:S(2)}, u32[]{:S(2)}) collective-permute-start(f32[2,2,32,1024]{3,2,1,0:T(8,128)S(1)} %slice.4), channel_id=1, source_target_pairs={{0,1},{1,2},{2,3},{4,5},{5,6},{6,7},{8,9},{9,10},{10,11},{12,13},{... | collective-permute-start | bytes 1572872 | tf_op jit(solution)/shard_map/ppermute | solution.py:23
  15.8 0.8 copy-start.1
  22.8 39.8 %all-to-all-start = ((f32[32,8,2048]{2,1,0:T(8,128)}), f32[32,8,2048]{2,1,0:T(8,128)}, u32[]{:S(2)}, u32[]{:S(2)}) async-start(f32[32,8,2048]{2,1,0:T(8,128)} %bitcast.27), calls=%async_computation | async-start | bytes 4194304 | tf_op jit(solution)/shard_map/all_to_all | solution.py:262
  31.1 5.9 %copy-start = (f32[1,256,128]{2,1,0:T(8,128)S(1)}, f32[1,256,128]{2,1,0:T(8,128)}, u32[]{:S(2)}) copy-start(f32[1,256,128]{2,1,0:T(8,128)} %param.19) | copy-start | bytes 393220
  37.0 11.8 %collective-permute-start.3 = (f32[1,256,128]{2,1,0:T(8,128)S(1)}, f32[1,256,128]{2,1,0:T(8,128)S(1)}, u32[]{:S(2)}, u32[]{:S(2)}) collective-permute-start(f32[1,256,128]{2,1,0:T(8,128)S(1)} %copy-done), channel_id=1, source_target_pairs={{3,0},{0,1},{1,2},{2,3},{7,4},{4,5},{5,6},{6,7},{11,8},{8,9},{9,10... | collective-permute-start | bytes 393224 | tf_op jit(solution)/shard_map/ppermute | solution.py:31
  39.4 9.3 %collective-permute-start.2 = (f32[1,256,128]{2,1,0:T(8,128)S(1)}, f32[1,256,128]{2,1,0:T(8,128)S(1)}, u32[]{:S(2)}, u32[]{:S(2)}) collective-permute-start(f32[1,256,128]{2,1,0:T(8,128)S(1)} %copy-done), channel_id=1, source_target_pairs={{2,0},{3,1},{0,2},{1,3},{6,4},{7,5},{4,6},{5,7},{10,8},{11,9},{8,1... | collective-permute-start | bytes 393224 | tf_op jit(solution)/shard_map/ppermute | solution.py:31
  42.3 5.8 %collective-permute-start.1 = (f32[1,256,128]{2,1,0:T(8,128)S(1)}, f32[1,256,128]{2,1,0:T(8,128)S(1)}, u32[]{:S(2)}, u32[]{:S(2)}) collective-permute-start(f32[1,256,128]{2,1,0:T(8,128)S(1)} %copy-done), channel_id=1, source_target_pairs={{1,0},{2,1},{3,2},{0,3},{5,4},{6,5},{7,6},{4,7},{9,8},{10,9},{11,1... | collective-permute-start | bytes 393224 | tf_op jit(solution)/shard_map/ppermute | solution.py:31

commit v8 on v7

--- a/solution.py
+++ b/solution.py
@@ -151,14 +151,14 @@
     return ar * br - ai * bi, ar * bi + ai * br
 
 
-def column_forward_kernel(blk_ref, hist_ref, t1c, t1s, t2c, t2s, lrh, lrl, lih, lil, pac, pas, pbc, pbs,
+def column_forward_kernel(blk_ref, hist0_ref, hist1_ref, t1c, t1s, t2c, t2s, lrh, lrl, lih, lil, pac, pas, pbc, pbs,
                           out_ref, xs_ref):
-    for p in range(2):
+    for p, hist_ref in enumerate((hist0_ref, hist1_ref)):
         xr, xi = [], []
         for t in range(32):
             if t < 8:
-                xr.append(hist_ref[p, 0, :, t * 128:(t + 1) * 128])
-                xi.append(hist_ref[p, 1, :, t * 128:(t + 1) * 128])
+                xr.append(hist_ref[0, :, t * 128:(t + 1) * 128])
+                xi.append(hist_ref[1, :, t * 128:(t + 1) * 128])
             else:
                 xr.append(blk_ref[p, 0, :, (t - 8) * 128:(t - 7) * 128])
                 xi.append(blk_ref[p, 1, :, (t - 8) * 128:(t - 7) * 128])
@@ -270,7 +270,7 @@
 def per_device(voltages, chirp_phase):
     block = voltages[0, 0]
     band = lax.axis_index("band")
-    history = passed_along(block[..., 3072 - HIST:], "seg", 1)
+    history = [passed_along(block[p, :, :, 3072 - HIST:], "seg", 1) for p in range(2)]
 
     i32 = jnp.int32
     lane = jnp.arange(1024, dtype=i32)[None, :]
@@ -285,17 +285,19 @@
     rl_lane = lane % 32
     rows = jnp.arange(256, dtype=i32)[:, None]
 
+    back_c, back_s = unit((32 * (rows // 8) + lane % 32) * (kc_lane + 32 * (rows % 4)), LENGTH, 1)
+    back_c, back_s, history = lax.optimization_barrier((back_c, back_s, history))
+
     t1c, t1s = lane_twiddle(-1, 128)
     lr, li = send_matrices()
     (send,) = call(column_forward_kernel, [(256, 2048)], [(1024, 512)],
-                   block, history, jnp.asarray(t1c), jnp.asarray(t1s), t2c, t2s,
+                   block, *history, jnp.asarray(t1c), jnp.asarray(t1s), t2c, t2s,
                    *halves(lr), *halves(li), pac, pas, pbc, pbs)
     received = exchanged(send)
 
     chirp_phase, send = lax.optimization_barrier((chirp_phase, send))
     phases = gathered(chirp_phase, "seg", 1)[0]
     ch_c, ch_s = arranged(jnp.cos(phases)), arranged(jnp.sin(phases))
-    back_c, back_s = unit((32 * (rows // 8) + lane % 32) * (kc_lane + 32 * (rows % 4)), LENGTH, 1)
 
     twc, tws = row_twiddle(-1)
     (sent,) = call(row_kernel, [(256, 2048)], [(1024, 256), (1024, 256)],

time: 113 us -> 111 us (0.982)
  waiting for transfers between devices: 13.3 us -> 10.4 us
  blocking collectives: 35.9 us -> 33.3 us
  starting transfers between devices: 18.6 us -> 21.1 us
    ppermute x1 -> x2, waiting for transfers between devices: 8.24 us -> 0.01 us  [passed_along(): return lax.ppermute(block, axis, route)]
    all_to_all x1, waiting for transfers between devices: 0.01 us -> 5.43 us  [exchanged(): lax.all_to_all(block.reshape(32, rows // 32, width), 'band', 0, 0, tiled=...]
    ppermute x1 -> x2, starting transfers between devices: 3.6 us -> 7.06 us  [passed_along(): return lax.ppermute(block, axis, route)]
    all_to_all x1, blocking collectives: 35.9 us -> 33.3 us  [exchanged(): lax.all_to_all(block.reshape(32, rows // 32, width), 'band', 0, 0, tiled=...]
    ppermute x3, starting transfers between devices: 6.73 us -> 5.59 us  [gathered(): pieces.append(lax.ppermute(block, axis, route))]
  transfers between devices with their start and end apart: 5 -> 6, of which waited for: 3 -> 3; matrix products, arithmetic and copies ran while one was open for 20% -> 21% of each run, Pallas kernels for 0% -> 0%
where the time goes in v8:
time: 111 us; the launch traced here: 109 us
  blocking collectives  33.3 us (30%)
  starting transfers between devices  21.1 us (19%)
  Pallas kernels  19.6 us (18%)
  local copies, waits for them, and re-layouts  15.7 us (14%)
  waiting for transfers between devices  10.4 us (9%)
  other arithmetic  8.73 us (8%)
    all_to_all x1, blocking collectives, exchanged(): lax.all_to_all(block.reshape(32, rows // 32, width), 'band', 0, 0, tiled=...  33.3 us
    pallas_call x3, Pallas kernels, call(): pl.pallas_call(kernel, out_shape=[jax.ShapeDtypeStruct(s, F32) for s in o...  19.6 us
    sin x4, other arithmetic, unit(): return (jnp.cos(angle), jnp.sin(angle))  8.7 us
    all_to_all x1, starting transfers between devices, exchanged(): lax.all_to_all(block.reshape(32, rows // 32, width), 'band', 0, 0, tiled=...  8.43 us
    ppermute x2, starting transfers between devices, passed_along(): return lax.ppermute(block, axis, route)  7.06 us
    reshape x2, local copies, waits for them, and re-layouts, arranged(): table.reshape(32, 32, 4, 8, 4).transpose(3, 1, 2, 4, 0).reshape(1024, 128)  6.14 us
    ppermute x3, starting transfers between devices, gathered(): pieces.append(lax.ppermute(block, axis, route))  5.59 us
    all_to_all x1, waiting for transfers between devices, exchanged(): lax.all_to_all(block.reshape(32, rows // 32, width), 'band', 0, 0, tiled=...  5.43 us
  transfers between devices with their start and end apart: 6, of which 3 were waited for; matrix products, arithmetic and copies ran while one was open for 21% of the time, Pallas kernels for 0%

profile of v8, /device:TPU:0, one launch (start us, length us, event | category | flops | bytes accessed | tf_op | source)
XLA Modules:
  0.0 109.1 jit_solution(14517959895642154364)
XLA Ops:
  0.0 1.1 slice_bitcast_fusion
  1.1 3.6 %collective-permute-start.1 = (f32[2,32,1024]{2,1,0:T(8,128)S(1)}, f32[2,32,1024]{2,1,0:T(8,128)S(1)}, u32[]{:S(2)}, u32[]{:S(2)}) collective-permute-start(f32[2,32,1024]{2,1,0:T(8,128)S(1)} %get-tuple-element.15), channel_id=1, source_target_pairs={{0,1},{1,2},{2,3},{4,5},{5,6},{6,7},{8,9},{9,10},{10,11},{12,13},{... | collective-permute-start | bytes 786440 | tf_op jit(solution)/shard_map/ppermute | solution.py:23
  4.7 3.5 %collective-permute-start = (f32[2,32,1024]{2,1,0:T(8,128)S(1)}, f32[2,32,1024]{2,1,0:T(8,128)S(1)}, u32[]{:S(2)}, u32[]{:S(2)}) collective-permute-start(f32[2,32,1024]{2,1,0:T(8,128)S(1)} %get-tuple-element.16), channel_id=1, source_target_pairs={{0,1},{1,2},{2,3},{4,5},{5,6},{6,7},{8,9},{9,10},{10,11},{12,13},{... | collective-permute-start | bytes 786440 | tf_op jit(solution)/shard_map/ppermute | solution.py:23
  8.2 0.8 fusion.24
  9.0 1.3 %fusion.11 = (f32[32,1024]{1,0:T(8,128)}, f32[32,1024]{1,0:T(8,128)}) fusion(s32[1024]{0:T(1024)S(1)} %get-tuple-element.31), kind=kLoop, calls=%fused_computation.29 | loop fusion | flops 458752 | bytes 266240 | tf_op jit(solution)/shard_map/sin | solution.py:92
  10.2 0.8 fusion.19
  11.1 5.9 %fusion.3 = (f32[256,1024]{1,0:T(8,128)}, f32[256,1024]{1,0:T(8,128)}) fusion(s32[256]{0:T(256)S(1)} %get-tuple-element.29, s32[1024]{0:T(1024)S(1)} %get-tuple-element.28, s32[1024]{0:T(1024)S(1)} %get-tuple-element.27, s32[256]{0:T(256)S(1)} %get-tuple-element.30), kind=kLoop, calls=%fused_computation.6 | loop fusion | flops 4194304 | bytes 2107392 | tf_op jit(solution)/shard_map/sin | solution.py:92
  16.9 0.0 collective-permute-done.1.hist1_ref
  16.9 0.0 copy-start.1
  16.9 0.0 collective-permute-done.hist0_ref
  16.9 0.0 copy-start.2
  16.9 0.7 copy-done.1
  17.6 0.1 copy-done.2
  17.7 6.2 %shard_map.172 = f32[256,2048]{1,0:T(8,128)} custom-call(f32[2,2,32,3072]{3,2,1,0:T(8,128)} %bitcast.34, f32[2,32,1024]{2,1,0:T(8,128)} %copy-done.2, f32[2,32,1024]{2,1,0:T(8,128)} %copy-done.1, f32[32,128]{1,0:T(8,128)} %constant.178.clone.t1c, f32[32,128]{1,0:T(8,128)} %constant.179.clone.t1s, f32[32,32]{1,0:T(8,128)} %get-tuple-element.26.t2c, ...), custom_call_target="tpu_custom_call" | custom-call | tf_op jit(solution)/shard_map/pallas_call | solution.py:252
  23.9 0.0 copy-start
  23.9 8.4 %all-to-all-start = ((f32[32,8,2048]{2,1,0:T(8,128)}), f32[32,8,2048]{2,1,0:T(8,128)}, u32[]{:S(2)}, u32[]{:S(2)}) async-start(f32[32,8,2048]{2,1,0:T(8,128)} %bitcast.31), calls=%async_computation | async-start | bytes 4194304 | tf_op jit(solution)/shard_map/all_to_all | solution.py:262
  32.4 0.0 copy-done
  32.4 1.3 %collective-permute-start.4 = (f32[1,256,128]{2,1,0:T(8,128)S(1)}, f32[1,256,128]{2,1,0:T(8,128)S(1)}, u32[]{:S(2)}, u32[]{:S(2)}) collective-permute-start(f32[1,256,128]{2,1,0:T(8,128)S(1)} %copy-done), channel_id=1, source_target_pairs={{3,0},{0,1},{1,2},{2,3},{7,4},{4,5},{5,6},{6,7},{11,8},{8,9},{9,10... | collective-permute-start | bytes 393224 | tf_op jit(solution)/shard_map/ppermute | solution.py:31
  33.7 2.9 %collective-permute-start.3 = (f32[1,256,128]{2,1,0:T(8,128)S(1)}, f32[1,256,128]{2,1,0:T(8,128)S(1)}, u32[]{:S(2)}, u32[]{:S(2)}) collective-permute-start(f32[1,256,128]{2,1,0:T(8,128)S(1)} %copy-done), channel_id=1, source_target_pairs={{2,0},{3,1},{0,2},{1,3},{6,4},{7,5},{4,6},{5,7},{10,8},{11,9},{8,1... | collective-permute-start | bytes 393224 | tf_op jit(solution)/shard_map/ppermute | solution.py:31
  36.6 1.3 %collective-permute-start.2 = (f32[1,256,128]{2,1,0:T(8,128)S(1)}, f32[1,256,128]{2,1,0:T(8,128)S(1)}, u32[]{:S(2)}, u32[]{:S(2)}) collective-permute-start(f32[1,256,128]{2,1,0:T(8,128)S(1)} %copy-done), channel_id=1, source_target_pairs={{1,0},{2,1},{3,2},{0,3},{5,4},{6,5},{7,6},{4,7},{9,8},{10,9},{11,1... | collective-permute-start | bytes 393224 | tf_op jit(solution)/shard_map/ppermute | solution.py:31
  38.0 4.7 %collective-permute-done.2 = f32[1,256,128]{2,1,0:T(8,128)S(1)} collective-permute-done((f32[1,256,128]{2,1,0:T(8,128)S(1)}, f32[1,256,128]{2,1,0:T(8,128)S(1)}, u32[]{:S(2)}, u32[]{:S(2)}) %collective-permute-start.2) | collective-permute-done | bytes 131104 | tf_op jit(solution)/shard_map/ppermute | solution.py:31
  42.7 0.3 collective-permute-done.3
  43.0 0.0 collective-permute-done.4
  43.1 1.9 %dynamic-slice_sine_fusion = (f32[4,1,256,128]{3,2,1,0:T(8,128)S(1)}, f32[4,1,256,128]{3,2,1,0:T(8,128)S(1)}) fusion(f32[8,1,256,128]{3,2,1,0:T(8,128)S(1)} %bitcast_dynamic-update-slice_fusion.1, s32[]{:T(128)S(6)} %select_n.110), kind=kLoop, calls=%fused_computation.8 | loop fusion | bytes 1572868 | tf_op jit(solution)/shard_map/sin | solution.py:300
  45.0 0.2 copy.23
  45.2 0.2 copy.21
  45.5 0.6 cos.24
  46.1 2.0 %copy.22 = f32[8,32,4,4,32]{4,3,2,1,0:T(4,128)} copy(f32[8,32,4,4,32]{1,4,3,0,2:T(8,128)S(1)} %bitcast.29) | data formatting | bytes 1048576 | tf_op jit(solution)/shard_map/transpose | solution.py:267
  48.1 3.1 %reshape.164.chc_ref = f32[1024,128]{1,0:T(8,128)} reshape(f32[8,32,4,4,32]{4,3,2,1,0:T(4,128)} %copy.22) | data formatting | bytes 1048576 | tf_op jit(solution)/shard_map/reshape | solution.py:267
  51.2 0.6 sin.24
  51.8 2.0 %copy.24 = f32[8,32,4,4,32]{4,3,2,1,0:T(4,128)} copy(f32[8,32,4,4,32]{1,4,3,0,2:T(8,128)S(1)} %bitcast.30) | data formatting | bytes 1048576 | tf_op jit(solution)/shard_map/transpose | solution.py:267
  53.8 3.1 %reshape.165.chs_ref = f32[1024,128]{1,0:T(8,128)} reshape(f32[8,32,4,4,32]{4,3,2,1,0:T(4,128)} %copy.24) | data formatting | bytes 1048576 | tf_op jit(solution)/shard_map/reshape | solution.py:267
  56.9 5.4 %all-to-all-done = f32[32,8,2048]{2,1,0:T(8,128)} async-done(((f32[32,8,2048]{2,1,0:T(8,128)}), f32[32,8,2048]{2,1,0:T(8,128)}, u32[]{:S(2)}, u32[]{:S(2)}) %all-to-all-start) | async-done | bytes 2097184 | tf_op jit(solution)/shard_map/all_to_all | solution.py:262
  62.3 8.1 %shard_map.173 = f32[256,2048]{1,0:T(8,128)} custom-call(f32[256,2048]{1,0:T(8,128)} %bitcast.4.x_ref, f32[32,512]{1,0:T(8,128)} %constant.184.clone.twc_ref, f32[32,512]{1,0:T(8,128)} %constant.185.clone.tws_ref, bf16[256,256]{1,0:T(8,128)(2,1)} %constant.186.clone.bfh, bf16[256,256]{1,0:T(8,128)(2,1)} %constant.187.clone.bfl, ...), custom_call_target="tpu_custom_call" | custom-call | tf_op jit(solution)/shard_map/pallas_call | solution.py:252
  70.4 33.3 %all_to_all.10 = f32[32,8,2048]{2,1,0:T(8,128)} all-to-all(f32[32,8,2048]{2,1,0:T(8,128)} %bitcast.32), channel_id=1, replica_groups=mesh['band'=32,'seg'=4] {'band'}, dimensions={0} | all-to-all | bytes 4194304 | tf_op jit(solution)/shard_map/all_to_all | solution.py:262
  103.7 5.4 %shard_map.174 = f32[2,2,32,3072]{3,2,1,0:T(8,128)} custom-call(f32[256,2048]{1,0:T(8,128)} %bitcast.28, bf16[512,512]{1,0:T(8,128)(2,1)} %constant.190.clone.mh_ref, bf16[512,512]{1,0:T(8,128)(2,1)} %constant.191.clone.ml_ref, f32[32,256]{1,0:T(8,128)} %constant.192.clone.twc_ref, f32[32,256]{1,0:T(8,128)} %constant.193.clone.tws_ref), custom_call_target="tpu_custom_call" | custom-call | tf_op jit(solution)/shard_map/pallas_call | solution.py:252
  (13 shorter events, 0.1 us)
Async XLA Ops:
  1.1 15.9 %collective-permute-start.1 = (f32[2,32,1024]{2,1,0:T(8,128)S(1)}, f32[2,32,1024]{2,1,0:T(8,128)S(1)}, u32[]{:S(2)}, u32[]{:S(2)}) collective-permute-start(f32[2,32,1024]{2,1,0:T(8,128)S(1)} %get-tuple-element.15), channel_id=1, source_target_pairs={{0,1},{1,2},{2,3},{4,5},{5,6},{6,7},{8,9},{9,10},{10,11},{12,13},{... | collective-permute-start | bytes 786440 | tf_op jit(solution)/shard_map/ppermute | solution.py:23
  4.7 12.3 %collective-permute-start = (f32[2,32,1024]{2,1,0:T(8,128)S(1)}, f32[2,32,1024]{2,1,0:T(8,128)S(1)}, u32[]{:S(2)}, u32[]{:S(2)}) collective-permute-start(f32[2,32,1024]{2,1,0:T(8,128)S(1)} %get-tuple-element.16), channel_id=1, source_target_pairs={{0,1},{1,2},{2,3},{4,5},{5,6},{6,7},{8,9},{9,10},{10,11},{12,13},{... | collective-permute-start | bytes 786440 | tf_op jit(solution)/shard_map/ppermute | solution.py:23
  16.9 0.7 copy-start.1
  16.9 0.8 copy-start.2
  23.9 8.5 %copy-start = (f32[1,256,128]{2,1,0:T(8,128)S(1)}, f32[1,256,128]{2,1,0:T(8,128)}, u32[]{:S(2)}) copy-start(f32[1,256,128]{2,1,0:T(8,128)} %param.19) | copy-start | bytes 393220
  23.9 38.4 %all-to-all-start = ((f32[32,8,2048]{2,1,0:T(8,128)}), f32[32,8,2048]{2,1,0:T(8,128)}, u32[]{:S(2)}, u32[]{:S(2)}) async-start(f32[32,8,2048]{2,1,0:T(8,128)} %bitcast.31), calls=%async_computation | async-start | bytes 4194304 | tf_op jit(solution)/shard_map/all_to_all | solution.py:262
  32.4 10.6 %collective-permute-start.4 = (f32[1,256,128]{2,1,0:T(8,128)S(1)}, f32[1,256,128]{2,1,0:T(8,128)S(1)}, u32[]{:S(2)}, u32[]{:S(2)}) collective-permute-start(f32[1,256,128]{2,1,0:T(8,128)S(1)} %copy-done), channel_id=1, source_target_pairs={{3,0},{0,1},{1,2},{2,3},{7,4},{4,5},{5,6},{6,7},{11,8},{8,9},{9,10... | collective-permute-start | bytes 393224 | tf_op jit(solution)/shard_map/ppermute | solution.py:31
  33.7 9.3 %collective-permute-start.3 = (f32[1,256,128]{2,1,0:T(8,128)S(1)}, f32[1,256,128]{2,1,0:T(8,128)S(1)}, u32[]{:S(2)}, u32[]{:S(2)}) collective-permute-start(f32[1,256,128]{2,1,0:T(8,128)S(1)} %copy-done), channel_id=1, source_target_pairs={{2,0},{3,1},{0,2},{1,3},{6,4},{7,5},{4,6},{5,7},{10,8},{11,9},{8,1... | collective-permute-start | bytes 393224 | tf_op jit(solution)/shard_map/ppermute | solution.py:31
  36.6 6.0 %collective-permute-start.2 = (f32[1,256,128]{2,1,0:T(8,128)S(1)}, f32[1,256,128]{2,1,0:T(8,128)S(1)}, u32[]{:S(2)}, u32[]{:S(2)}) collective-permute-start(f32[1,256,128]{2,1,0:T(8,128)S(1)} %copy-done), channel_id=1, source_target_pairs={{1,0},{2,1},{3,2},{0,3},{5,4},{6,5},{7,6},{4,7},{9,8},{10,9},{11,1... | collective-permute-start | bytes 393224 | tf_op jit(solution)/shard_map/ppermute | solution.py:31

commit v9 on v8

--- a/solution.py
+++ b/solution.py
@@ -184,12 +184,14 @@
             out_ref[8 * d:8 * d + 8, 1024 * h + 512:1024 * h + 1024] = im
 
 
-def row_kernel(x_ref, twc_ref, tws_ref, bfh, bfl, bbh, bbl, chc_ref, chs_ref, pc_ref, ps_ref, out_ref, y_ref, w_ref):
+def row_kernel(x_ref, twc_ref, tws_ref, bfh, bfl, bbh, bbl, chc_ref, chs_ref, ac_ref, as_ref, bc_ref, bs_ref,
+               cc_ref, cs_ref, out_ref, y_ref, w_ref):
+    tw_refs = (ac_ref, as_ref, bc_ref, bs_ref, cc_ref, cs_ref)
     for h in range(2):
-        row_half(h, x_ref, twc_ref, tws_ref, bfh, bfl, bbh, bbl, chc_ref, chs_ref, pc_ref, ps_ref, out_ref, y_ref, w_ref)
-
-
-def row_half(h, x_ref, twc_ref, tws_ref, bfh, bfl, bbh, bbl, chc_ref, chs_ref, pc_ref, ps_ref, out_ref, y_ref, w_ref):
+        row_half(h, x_ref, twc_ref, tws_ref, bfh, bfl, bbh, bbl, chc_ref, chs_ref, tw_refs, out_ref, y_ref, w_ref)
+
+
+def row_half(h, x_ref, twc_ref, tws_ref, bfh, bfl, bbh, bbl, chc_ref, chs_ref, tw_refs, out_ref, y_ref, w_ref):
     base = 1024 * h
     lanes = slice(512 * h, 512 * (h + 1))
     er = [x_ref[8 * d:8 * d + 8, base:base + 512] for d in range(32)]
@@ -222,8 +224,13 @@
         gr.append(a)
         gi.append(b)
     ur, ui = fft_list(gr, gi, 1)
+    ac_ref, as_ref, bc_ref, bs_ref, cc_ref, cs_ref = tw_refs
+    ac = ac_ref[:, lanes]
+    as_ = as_ref[:, lanes]
     for d in range(32):
-        re, im = cmul(ur[d], ui[d], pc_ref[8 * d:8 * d + 8, lanes], ps_ref[8 * d:8 * d + 8, lanes])
+        wc, ws = cmul(bc_ref[d:d + 1, lanes], bs_ref[d:d + 1, lanes], cc_ref[8 * d:8 * d + 8, 0:1], cs_ref[8 * d:8 * d + 8, 0:1])
+        wc, ws = cmul(wc, ws, ac, as_)
+        re, im = cmul(ur[d], ui[d], wc, ws)
         out_ref[8 * d:8 * d + 8, base:base + 512] = re
         out_ref[8 * d:8 * d + 8, base + 512:base + 1024] = im
 
@@ -285,8 +292,9 @@
     rl_lane = lane % 32
     rows = jnp.arange(256, dtype=i32)[:, None]
 
-    back_c, back_s = unit((32 * (rows // 8) + lane % 32) * (kc_lane + 32 * (rows % 4)), LENGTH, 1)
-    back_c, back_s, history = lax.optimization_barrier((back_c, back_s, history))
+    bac, bas = unit(rl_lane * (kc_lane + 32 * (q % 4)), LENGTH, 1)
+    bbc, bbs = unit(32 * dd * kc_lane, LENGTH, 1)
+    bcc, bcs = unit(jnp.broadcast_to(1024 * (rows // 8) * (rows % 4), (256, 128)), LENGTH, 1)
 
     t1c, t1s = lane_twiddle(-1, 128)
     lr, li = send_matrices()
@@ -302,7 +310,7 @@
     twc, tws = row_twiddle(-1)
     (sent,) = call(row_kernel, [(256, 2048)], [(1024, 256), (1024, 256)],
                    received, jnp.asarray(twc), jnp.asarray(tws), *halves(row_block(-1)),
-                   *halves(row_block(1)), ch_c, ch_s, back_c, back_s)
+                   *halves(row_block(1)), ch_c, ch_s, bac, bas, bbc, bbs, bcc, bcs)
     returned = exchanged(sent)
 
     cc, cs = lane_twiddle(1, 256)

time: 111 us -> 118 us (1.063)
  local copies, waits for them, and re-layouts: 15.7 us -> 23.3 us
  blocking collectives: 33.3 us -> 35.9 us
  other arithmetic: 8.73 us -> 6.36 us
    all_to_all x1, waiting for transfers between devices: 5.43 us -> 0.01 us  [exchanged(): lax.all_to_all(block.reshape(32, rows // 32, width), 'band', 0, 0, tiled=...]
    ppermute x3, waiting for transfers between devices: 5.01 us -> 8.07 us  [gathered(): pieces.append(lax.ppermute(block, axis, route))]
    all_to_all x1, blocking collectives: 33.3 us -> 35.9 us  [exchanged(): lax.all_to_all(block.reshape(32, rows // 32, width), 'band', 0, 0, tiled=...]
    sin x4 -> x6, other arithmetic: 8.7 us -> 6.31 us  [unit(): return (jnp.cos(angle), jnp.sin(angle))]
    cos x2, local copies, waits for them, and re-layouts: 0.82 us -> 3.17 us  [per_device(): ch_c, ch_s = (arranged(jnp.cos(phases)), arranged(jnp.sin(phases)))]
    ppermute x2, waiting for transfers between devices: 0.01 us -> 2.09 us  [passed_along(): return lax.ppermute(block, axis, route)]
    transpose x2, local copies, waits for them, and re-layouts: 4.06 us -> 6.13 us  [arranged(): table.reshape(32, 32, 4, 8, 4).transpose(3, 1, 2, 4, 0).reshape(1024, 128)]
    sin x3, local copies, waits for them, and re-layouts: 2.69 us -> 4.74 us  [per_device(): ch_c, ch_s = (arranged(jnp.cos(phases)), arranged(jnp.sin(phases)))]
  transfers between devices with their start and end apart: 6 -> 6, of which waited for: 3 -> 4; matrix products, arithmetic and copies ran while one was open for 21% -> 23% of each run, Pallas kernels for 0% -> 0%
where the time goes in v9:
time: 118 us; the launch traced here: 116 us
  blocking collectives  35.9 us (30%)
  local copies, waits for them, and re-layouts  23.3 us (20%)
  starting transfers between devices  20.9 us (18%)
  Pallas kernels  19.3 us (16%)
  waiting for transfers between devices  10.2 us (9%)
  other arithmetic  6.36 us (5%)
    all_to_all x1, blocking collectives, exchanged(): lax.all_to_all(block.reshape(32, rows // 32, width), 'band', 0, 0, tiled=...  35.9 us
    pallas_call x3, Pallas kernels, call(): pl.pallas_call(kernel, out_shape=[jax.ShapeDtypeStruct(s, F32) for s in o...  19.3 us
    all_to_all x1, starting transfers between devices, exchanged(): lax.all_to_all(block.reshape(32, rows // 32, width), 'band', 0, 0, tiled=...  8.3 us
    ppermute x3, waiting for transfers between devices, gathered(): pieces.append(lax.ppermute(block, axis, route))  8.07 us
    ppermute x2, starting transfers between devices, passed_along(): return lax.ppermute(block, axis, route)  7.06 us
    sin x6, other arithmetic, unit(): return (jnp.cos(angle), jnp.sin(angle))  6.31 us
    transpose x2, local copies, waits for them, and re-layouts, arranged(): table.reshape(32, 32, 4, 8, 4).transpose(3, 1, 2, 4, 0).reshape(1024, 128)  6.13 us
    reshape x2, local copies, waits for them, and re-layouts, arranged(): table.reshape(32, 32, 4, 8, 4).transpose(3, 1, 2, 4, 0).reshape(1024, 128)  6.11 us
  transfers between devices with their start and end apart: 6, of which 4 were waited for; matrix products, arithmetic and copies ran while one was open for 23% of the time, Pallas kernels for 0%

profile of v9, /device:TPU:0, one launch (start us, length us, event | category | flops | bytes accessed | tf_op | source)
XLA Modules:
  0.0 116.1 jit_solution(6495408517038718819)
XLA Ops:
  0.0 1.1 slice_bitcast_fusion
  1.1 3.6 %collective-permute-start = (f32[2,32,1024]{2,1,0:T(8,128)S(1)}, f32[2,32,1024]{2,1,0:T(8,128)S(1)}, u32[]{:S(2)}, u32[]{:S(2)}) collective-permute-start(f32[2,32,1024]{2,1,0:T(8,128)S(1)} %get-tuple-element.8), channel_id=1, source_target_pairs={{0,1},{1,2},{2,3},{4,5},{5,6},{6,7},{8,9},{9,10},{10,11},{12,13},{... | collective-permute-start | bytes 786440 | tf_op jit(solution)/shard_map/ppermute | solution.py:23
  4.7 3.5 %collective-permute-start.1 = (f32[2,32,1024]{2,1,0:T(8,128)S(1)}, f32[2,32,1024]{2,1,0:T(8,128)S(1)}, u32[]{:S(2)}, u32[]{:S(2)}) collective-permute-start(f32[2,32,1024]{2,1,0:T(8,128)S(1)} %get-tuple-element.7), channel_id=1, source_target_pairs={{0,1},{1,2},{2,3},{4,5},{5,6},{6,7},{8,9},{9,10},{10,11},{12,13},{... | collective-permute-start | bytes 786440 | tf_op jit(solution)/shard_map/ppermute | solution.py:23
  8.2 1.2 %fusion.13 = (f32[32,1024]{1,0:T(8,128)}, f32[32,1024]{1,0:T(8,128)}) fusion(s32[1024]{0:T(1024)S(1)} %get-tuple-element.23), kind=kLoop, calls=%fused_computation.34 | loop fusion | flops 458752 | bytes 266240 | tf_op jit(solution)/shard_map/sin | solution.py:92
  9.5 0.8 fusion.31
  10.2 0.8 fusion.26
  11.1 1.3 %fusion.6 = (f32[256,128]{1,0:T(8,128)}, f32[256,128]{1,0:T(8,128)}) fusion(s32[256]{0:T(256)S(1)} %get-tuple-element.27, s32[256]{0:T(256)S(1)} %get-tuple-element.28, pred[256]{0:T(512)(128)(4,1)S(1)} %compare_and_fusion), kind=kLoop, calls=%fused_computation.27 | loop fusion | flops 98304 | bytes 264448 | tf_op jit(solution)/shard_map/sin | solution.py:92
  12.4 1.3 %fusion.11 = (f32[32,1024]{1,0:T(8,128)}, f32[32,1024]{1,0:T(8,128)}) fusion(s32[1024]{0:T(1024)S(1)} %get-tuple-element.26, s32[32]{0:T(128)S(1)} %iota_multiply_fusion), kind=kLoop, calls=%fused_computation.32 | loop fusion | flops 458752 | bytes 266368 | tf_op jit(solution)/shard_map/sin | solution.py:92
  13.7 0.0 collective-permute-done.hist0_ref
  13.7 0.0 copy-start.2
  13.7 2.1 %collective-permute-done.1.hist1_ref = f32[2,32,1024]{2,1,0:T(8,128)S(1)} collective-permute-done((f32[2,32,1024]{2,1,0:T(8,128)S(1)}, f32[2,32,1024]{2,1,0:T(8,128)S(1)}, u32[]{:S(2)}, u32[]{:S(2)}) %collective-permute-start.1) | collective-permute-done | bytes 262176 | tf_op jit(solution)/shard_map/ppermute | solution.py:23
  15.8 0.0 copy-start.3
  15.8 0.0 copy-done.2
  15.8 0.7 copy-done.3
  16.5 6.2 %shard_map.172 = f32[256,2048]{1,0:T(8,128)} custom-call(f32[2,2,32,3072]{3,2,1,0:T(8,128)} %bitcast.35, f32[2,32,1024]{2,1,0:T(8,128)} %copy-done.2, f32[2,32,1024]{2,1,0:T(8,128)} %copy-done.3, f32[32,128]{1,0:T(8,128)} %constant.196.clone.t1c, f32[32,128]{1,0:T(8,128)} %constant.197.clone.t1s, f32[32,32]{1,0:T(8,128)} %get-tuple-element.22.t2c, ...), custom_call_target="tpu_custom_call" | custom-call | tf_op jit(solution)/shard_map/pallas_call | solution.py:259
  22.7 0.0 copy-start.1
  22.7 8.3 %all-to-all-start = ((f32[32,8,2048]{2,1,0:T(8,128)}), f32[32,8,2048]{2,1,0:T(8,128)S(1)}, u32[]{:S(2)}, u32[]{:S(2)}) async-start(f32[32,8,2048]{2,1,0:T(8,128)} %bitcast.33), calls=%async_computation | async-start | bytes 4194304 | tf_op jit(solution)/shard_map/all_to_all | solution.py:269
  31.0 0.8 fusion.21
  31.8 0.0 copy-done.1
  31.8 3.9 %collective-permute-start.2 = (f32[1,256,128]{2,1,0:T(8,128)S(1)}, f32[1,256,128]{2,1,0:T(8,128)S(1)}, u32[]{:S(2)}, u32[]{:S(2)}) collective-permute-start(f32[1,256,128]{2,1,0:T(8,128)S(1)} %copy-done.1), channel_id=1, source_target_pairs={{1,0},{2,1},{3,2},{0,3},{5,4},{6,5},{7,6},{4,7},{9,8},{10,9},{11,1... | collective-permute-start | bytes 393224 | tf_op jit(solution)/shard_map/ppermute | solution.py:31
  35.7 0.6 collective-permute-start.3
  36.4 1.0 collective-permute-start.4
  37.4 4.4 %collective-permute-done.2 = f32[1,256,128]{2,1,0:T(8,128)S(1)} collective-permute-done((f32[1,256,128]{2,1,0:T(8,128)S(1)}, f32[1,256,128]{2,1,0:T(8,128)S(1)}, u32[]{:S(2)}, u32[]{:S(2)}) %collective-permute-start.2) | collective-permute-done | bytes 131104 | tf_op jit(solution)/shard_map/ppermute | solution.py:31
  41.8 1.9 %collective-permute-done.3 = f32[1,256,128]{2,1,0:T(8,128)S(1)} collective-permute-done((f32[1,256,128]{2,1,0:T(8,128)S(1)}, f32[1,256,128]{2,1,0:T(8,128)S(1)}, u32[]{:S(2)}, u32[]{:S(2)}) %collective-permute-start.3) | collective-permute-done | bytes 131104 | tf_op jit(solution)/shard_map/ppermute | solution.py:31
  43.7 1.8 %collective-permute-done.4 = f32[1,256,128]{2,1,0:T(8,128)S(1)} collective-permute-done((f32[1,256,128]{2,1,0:T(8,128)S(1)}, f32[1,256,128]{2,1,0:T(8,128)S(1)}, u32[]{:S(2)}, u32[]{:S(2)}) %collective-permute-start.4) | collective-permute-done | bytes 131104 | tf_op jit(solution)/shard_map/ppermute | solution.py:31
  45.5 2.6 %dynamic-slice_sine_fusion = (f32[4,1,256,128]{3,2,1,0:T(8,128)S(1)}, f32[4,1,256,128]{3,2,1,0:T(8,128)}) fusion(f32[8,1,256,128]{3,2,1,0:T(8,128)S(1)} %bitcast_dynamic-update-slice_fusion.1, s32[]{:T(128)S(6)} %select_n.127), kind=kLoop, calls=%fused_computation | loop fusion | bytes 1572868 | tf_op jit(solution)/shard_map/sin | solution.py:308
  48.1 1.3 %copy.21 = f32[4,1,256,128]{2,0,3,1:T(4,128)S(1)} copy(f32[4,1,256,128]{3,2,1,0:T(8,128)} %get-tuple-element.10) | data formatting | bytes 1048576 | tf_op jit(solution)/shard_map/cos | solution.py:308
  49.4 1.9 %cos.29 = f32[32,32,4,8,4]{1,0,4,3,2:T(8,128)} reshape(f32[4,1,256,128]{2,0,3,1:T(4,128)S(1)} %copy.21) | data formatting | bytes 1048576 | tf_op jit(solution)/shard_map/cos | solution.py:308
  51.3 3.1 %copy.22 = f32[8,32,4,4,32]{4,3,2,1,0:T(4,128)} copy(f32[8,32,4,4,32]{1,4,3,0,2:T(8,128)} %bitcast.31) | data formatting | bytes 1048576 | tf_op jit(solution)/shard_map/transpose | solution.py:274
  54.4 3.1 %reshape.171.chc_ref = f32[1024,128]{1,0:T(8,128)} reshape(f32[8,32,4,4,32]{4,3,2,1,0:T(4,128)} %copy.22) | data formatting | bytes 1048576 | tf_op jit(solution)/shard_map/reshape | solution.py:274
  57.4 0.2 copy.23
  57.7 1.9 %sin.29 = f32[32,32,4,8,4]{1,0,4,3,2:T(8,128)} reshape(f32[4,1,256,128]{2,0,3,1:T(4,128)S(1)} %copy.23) | data formatting | bytes 1048576 | tf_op jit(solution)/shard_map/sin | solution.py:308
  59.6 3.1 %copy.24 = f32[8,32,4,4,32]{4,3,2,1,0:T(4,128)} copy(f32[8,32,4,4,32]{1,4,3,0,2:T(8,128)} %bitcast.32) | data formatting | bytes 1048576 | tf_op jit(solution)/shard_map/transpose | solution.py:274
  62.7 3.1 %reshape.172.chs_ref = f32[1024,128]{1,0:T(8,128)} reshape(f32[8,32,4,4,32]{4,3,2,1,0:T(4,128)} %copy.24) | data formatting | bytes 1048576 | tf_op jit(solution)/shard_map/reshape | solution.py:274
  65.7 0.0 all-to-all-done
  65.7 0.0 copy-start
  65.7 1.3 %copy-done = f32[32,8,2048]{2,1,0:T(8,128)} copy-done((f32[32,8,2048]{2,1,0:T(8,128)}, f32[32,8,2048]{2,1,0:T(8,128)S(1)}, u32[]{:S(2)}) %copy-start) | copy-done | bytes 2097176
  67.0 7.8 %shard_map.173 = f32[256,2048]{1,0:T(8,128)} custom-call(f32[256,2048]{1,0:T(8,128)} %bitcast.28, f32[32,512]{1,0:T(8,128)} %constant.202.clone.twc_ref, f32[32,512]{1,0:T(8,128)} %constant.203.clone.tws_ref, bf16[256,256]{1,0:T(8,128)(2,1)} %constant.204.clone.bfh, bf16[256,256]{1,0:T(8,128)(2,1)} %constant.205.clone.bfl, ...), custom_call_target="tpu_custom_call" | custom-call | tf_op jit(solution)/shard_map/pallas_call | solution.py:259
  74.8 35.9 %all_to_all.10 = f32[32,8,2048]{2,1,0:T(8,128)} all-to-all(f32[32,8,2048]{2,1,0:T(8,128)} %bitcast.29), channel_id=1, replica_groups=mesh['band'=32,'seg'=4] {'band'}, dimensions={0} | all-to-all | bytes 4194304 | tf_op jit(solution)/shard_map/all_to_all | solution.py:269
  110.7 5.4 %shard_map.174 = f32[2,2,32,3072]{3,2,1,0:T(8,128)} custom-call(f32[256,2048]{1,0:T(8,128)} %bitcast.30, bf16[512,512]{1,0:T(8,128)(2,1)} %constant.208.clone.mh_ref, bf16[512,512]{1,0:T(8,128)(2,1)} %constant.209.clone.ml_ref, f32[32,256]{1,0:T(8,128)} %constant.210.clone.twc_ref, f32[32,256]{1,0:T(8,128)} %constant.211.clone.tws_ref), custom_call_target="tpu_custom_call" | custom-call | tf_op jit(solution)/shard_map/pallas_call | solution.py:259
  (16 shorter events, 0.1 us)
Async XLA Ops:
  1.1 12.6 %collective-permute-start = (f32[2,32,1024]{2,1,0:T(8,128)S(1)}, f32[2,32,1024]{2,1,0:T(8,128)S(1)}, u32[]{:S(2)}, u32[]{:S(2)}) collective-permute-start(f32[2,32,1024]{2,1,0:T(8,128)S(1)} %get-tuple-element.8), channel_id=1, source_target_pairs={{0,1},{1,2},{2,3},{4,5},{5,6},{6,7},{8,9},{9,10},{10,11},{12,13},{... | collective-permute-start | bytes 786440 | tf_op jit(solution)/shard_map/ppermute | solution.py:23
  4.7 11.1 %collective-permute-start.1 = (f32[2,32,1024]{2,1,0:T(8,128)S(1)}, f32[2,32,1024]{2,1,0:T(8,128)S(1)}, u32[]{:S(2)}, u32[]{:S(2)}) collective-permute-start(f32[2,32,1024]{2,1,0:T(8,128)S(1)} %get-tuple-element.7), channel_id=1, source_target_pairs={{0,1},{1,2},{2,3},{4,5},{5,6},{6,7},{8,9},{9,10},{10,11},{12,13},{... | collective-permute-start | bytes 786440 | tf_op jit(solution)/shard_map/ppermute | solution.py:23
  13.7 2.1 %copy-start.2 = (f32[2,32,1024]{2,1,0:T(8,128)}, f32[2,32,1024]{2,1,0:T(8,128)S(1)}, u32[]{:S(2)}) copy-start(f32[2,32,1024]{2,1,0:T(8,128)S(1)} %collective-permute-done.hist0_ref) | copy-start | bytes 786436
  15.8 0.7 copy-start.3
  22.7 9.1 %copy-start.1 = (f32[1,256,128]{2,1,0:T(8,128)S(1)}, f32[1,256,128]{2,1,0:T(8,128)}, u32[]{:S(2)}) copy-start(f32[1,256,128]{2,1,0:T(8,128)} %param.19) | copy-start | bytes 393220
  22.7 43.0 %all-to-all-start = ((f32[32,8,2048]{2,1,0:T(8,128)}), f32[32,8,2048]{2,1,0:T(8,128)S(1)}, u32[]{:S(2)}, u32[]{:S(2)}) async-start(f32[32,8,2048]{2,1,0:T(8,128)} %bitcast.33), calls=%async_computation | async-start | bytes 4194304 | tf_op jit(solution)/shard_map/all_to_all | solution.py:269
  31.8 9.9 %collective-permute-start.2 = (f32[1,256,128]{2,1,0:T(8,128)S(1)}, f32[1,256,128]{2,1,0:T(8,128)S(1)}, u32[]{:S(2)}, u32[]{:S(2)}) collective-permute-start(f32[1,256,128]{2,1,0:T(8,128)S(1)} %copy-done.1), channel_id=1, source_target_pairs={{1,0},{2,1},{3,2},{0,3},{5,4},{6,5},{7,6},{4,7},{9,8},{10,9},{11,1... | collective-permute-start | bytes 393224 | tf_op jit(solution)/shard_map/ppermute | solution.py:31
  35.7 7.9 %collective-permute-start.3 = (f32[1,256,128]{2,1,0:T(8,128)S(1)}, f32[1,256,128]{2,1,0:T(8,128)S(1)}, u32[]{:S(2)}, u32[]{:S(2)}) collective-permute-start(f32[1,256,128]{2,1,0:T(8,128)S(1)} %copy-done.1), channel_id=1, source_target_pairs={{2,0},{3,1},{0,2},{1,3},{6,4},{7,5},{4,6},{5,7},{10,8},{11,9},{8,1... | collective-permute-start | bytes 393224 | tf_op jit(solution)/shard_map/ppermute | solution.py:31
  36.4 9.1 %collective-permute-start.4 = (f32[1,256,128]{2,1,0:T(8,128)S(1)}, f32[1,256,128]{2,1,0:T(8,128)S(1)}, u32[]{:S(2)}, u32[]{:S(2)}) collective-permute-start(f32[1,256,128]{2,1,0:T(8,128)S(1)} %copy-done.1), channel_id=1, source_target_pairs={{3,0},{0,1},{1,2},{2,3},{7,4},{4,5},{5,6},{6,7},{11,8},{8,9},{9,10... | collective-permute-start | bytes 393224 | tf_op jit(solution)/shard_map/ppermute | solution.py:31
  65.7 1.3 %copy-start = (f32[32,8,2048]{2,1,0:T(8,128)}, f32[32,8,2048]{2,1,0:T(8,128)S(1)}, u32[]{:S(2)}) copy-start(f32[32,8,2048]{2,1,0:T(8,128)S(1)} %all-to-all-done) | copy-start | bytes 6291460

commit v10 on v7

--- a/solution.py
+++ b/solution.py
@@ -285,6 +285,9 @@
     rl_lane = lane % 32
     rows = jnp.arange(256, dtype=i32)[:, None]
 
+    back_c, back_s = unit((32 * (rows // 8) + lane % 32) * (kc_lane + 32 * (rows % 4)), LENGTH, 1)
+    back_c, back_s, history = lax.optimization_barrier((back_c, back_s, history))
+
     t1c, t1s = lane_twiddle(-1, 128)
     lr, li = send_matrices()
     (send,) = call(column_forward_kernel, [(256, 2048)], [(1024, 512)],
@@ -295,7 +298,6 @@
     chirp_phase, send = lax.optimization_barrier((chirp_phase, send))
     phases = gathered(chirp_phase, "seg", 1)[0]
     ch_c, ch_s = arranged(jnp.cos(phases)), arranged(jnp.sin(phases))
-    back_c, back_s = unit((32 * (rows // 8) + lane % 32) * (kc_lane + 32 * (rows % 4)), LENGTH, 1)
 
     twc, tws = row_twiddle(-1)
     (sent,) = call(row_kernel, [(256, 2048)], [(1024, 256), (1024, 256)],

time: 113 us -> 109 us (0.965)
  blocking collectives: 35.9 us -> 33.3 us
  waiting for transfers between devices: 13.3 us -> 11.7 us
    ppermute x1, waiting for transfers between devices: 8.24 us -> 2.4 us  [passed_along(): return lax.ppermute(block, axis, route)]
    all_to_all x1, waiting for transfers between devices: 0.01 us -> 4.29 us  [exchanged(): lax.all_to_all(block.reshape(32, rows // 32, width), 'band', 0, 0, tiled=...]
    all_to_all x1, blocking collectives: 35.9 us -> 33.3 us  [exchanged(): lax.all_to_all(block.reshape(32, rows // 32, width), 'band', 0, 0, tiled=...]
  transfers between devices with their start and end apart: 5 -> 5, of which waited for: 3 -> 4; matrix products, arithmetic and copies ran while one was open for 20% -> 21% of each run, Pallas kernels for 0% -> 0%
where the time goes in v10:
time: 109 us; the launch traced here: 108 us
  blocking collectives  33.3 us (31%)
  Pallas kernels  19.6 us (18%)
  starting transfers between devices  18.8 us (17%)
  local copies, waits for them, and re-layouts  15.6 us (14%)
  waiting for transfers between devices  11.7 us (11%)
  other arithmetic  8.69 us (8%)
    all_to_all x1, blocking collectives, exchanged(): lax.all_to_all(block.reshape(32, rows // 32, width), 'band', 0, 0, tiled=...  33.3 us
    pallas_call x3, Pallas kernels, call(): pl.pallas_call(kernel, out_shape=[jax.ShapeDtypeStruct(s, F32) for s in o...  19.6 us
    sin x4, other arithmetic, unit(): return (jnp.cos(angle), jnp.sin(angle))  8.67 us
    all_to_all x1, starting transfers between devices, exchanged(): lax.all_to_all(block.reshape(32, rows // 32, width), 'band', 0, 0, tiled=...  8.42 us
    ppermute x3, starting transfers between devices, gathered(): pieces.append(lax.ppermute(block, axis, route))  6.8 us
    reshape x2, local copies, waits for them, and re-layouts, arranged(): table.reshape(32, 32, 4, 8, 4).transpose(3, 1, 2, 4, 0).reshape(1024, 128)  6.1 us
    ppermute x3, waiting for transfers between devices, gathered(): pieces.append(lax.ppermute(block, axis, route))  5.01 us
    all_to_all x1, waiting for transfers between devices, exchanged(): lax.all_to_all(block.reshape(32, rows // 32, width), 'band', 0, 0, tiled=...  4.29 us
  transfers between devices with their start and end apart: 5, of which 4 were waited for; matrix products, arithmetic and copies ran while one was open for 21% of the time, Pallas kernels for 0%

profile of v10, /device:TPU:0, one launch (start us, length us, event | category | flops | bytes accessed | tf_op | source)
XLA Modules:
  0.0 108.0 jit_solution(16380806252080898371)
XLA Ops:
  0.0 1.1 slice.4
  1.1 3.6 %collective-permute-start = (f32[2,2,32,1024]{3,2,1,0:T(8,128)S(1)}, f32[2,2,32,1024]{3,2,1,0:T(8,128)S(1)}, u32[]{:S(2)}, u32[]{:S(2)}) collective-permute-start(f32[2,2,32,1024]{3,2,1,0:T(8,128)S(1)} %slice.4), channel_id=1, source_target_pairs={{0,1},{1,2},{2,3},{4,5},{5,6},{6,7},{8,9},{9,10},{10,11},{12,13},{... | collective-permute-start | bytes 1572872 | tf_op jit(solution)/shard_map/ppermute | solution.py:23
  4.7 0.8 fusion.24
  5.5 0.8 fusion.19
  6.3 1.3 %fusion.11 = (f32[32,1024]{1,0:T(8,128)}, f32[32,1024]{1,0:T(8,128)}) fusion(s32[1024]{0:T(1024)S(1)} %get-tuple-element.27), kind=kLoop, calls=%fused_computation.27 | loop fusion | flops 458752 | bytes 266240 | tf_op jit(solution)/shard_map/sin | solution.py:92
  7.6 5.8 %fusion.3 = (f32[256,1024]{1,0:T(8,128)}, f32[256,1024]{1,0:T(8,128)}) fusion(s32[256]{0:T(256)S(1)} %get-tuple-element.25, s32[1024]{0:T(1024)S(1)} %get-tuple-element.24, s32[1024]{0:T(1024)S(1)} %get-tuple-element.23, s32[256]{0:T(256)S(1)} %get-tuple-element.26), kind=kLoop, calls=%fused_computation.6 | loop fusion | flops 4194304 | bytes 2107392 | tf_op jit(solution)/shard_map/sin | solution.py:92
  13.4 2.4 %collective-permute-done.hist_ref = f32[2,2,32,1024]{3,2,1,0:T(8,128)S(1)} collective-permute-done((f32[2,2,32,1024]{3,2,1,0:T(8,128)S(1)}, f32[2,2,32,1024]{3,2,1,0:T(8,128)S(1)}, u32[]{:S(2)}, u32[]{:S(2)}) %collective-permute-start) | collective-permute-done | bytes 524320 | tf_op jit(solution)/shard_map/ppermute | solution.py:23
  15.8 0.0 copy-start.1
  15.8 0.8 copy-done.1
  16.6 6.2 %shard_map.172 = f32[256,2048]{1,0:T(8,128)} custom-call(f32[2,2,32,3072]{3,2,1,0:T(8,128)} %bitcast.30, f32[2,2,32,1024]{3,2,1,0:T(8,128)} %copy-done.1, f32[32,128]{1,0:T(8,128)} %constant.178.clone.t1c, f32[32,128]{1,0:T(8,128)} %constant.179.clone.t1s, f32[32,32]{1,0:T(8,128)} %get-tuple-element.22.t2c, f32[32,32]{1,0:T(8,128)} %get-tuple-element.21.t2s, ...), custom_call_target="tpu_custom_call" | custom-call | tf_op jit(solution)/shard_map/pallas_call | solution.py:252
  22.8 0.0 copy-start
  22.8 8.4 %all-to-all-start = ((f32[32,8,2048]{2,1,0:T(8,128)}), f32[32,8,2048]{2,1,0:T(8,128)}, u32[]{:S(2)}, u32[]{:S(2)}) async-start(f32[32,8,2048]{2,1,0:T(8,128)} %bitcast.27), calls=%async_computation | async-start | bytes 4194304 | tf_op jit(solution)/shard_map/all_to_all | solution.py:262
  31.3 0.0 copy-done
  31.3 2.5 %collective-permute-start.3 = (f32[1,256,128]{2,1,0:T(8,128)S(1)}, f32[1,256,128]{2,1,0:T(8,128)S(1)}, u32[]{:S(2)}, u32[]{:S(2)}) collective-permute-start(f32[1,256,128]{2,1,0:T(8,128)S(1)} %copy-done), channel_id=1, source_target_pairs={{3,0},{0,1},{1,2},{2,3},{7,4},{4,5},{5,6},{6,7},{11,8},{8,9},{9,10... | collective-permute-start | bytes 393224 | tf_op jit(solution)/shard_map/ppermute | solution.py:31
  33.8 2.9 %collective-permute-start.2 = (f32[1,256,128]{2,1,0:T(8,128)S(1)}, f32[1,256,128]{2,1,0:T(8,128)S(1)}, u32[]{:S(2)}, u32[]{:S(2)}) collective-permute-start(f32[1,256,128]{2,1,0:T(8,128)S(1)} %copy-done), channel_id=1, source_target_pairs={{2,0},{3,1},{0,2},{1,3},{6,4},{7,5},{4,6},{5,7},{10,8},{11,9},{8,1... | collective-permute-start | bytes 393224 | tf_op jit(solution)/shard_map/ppermute | solution.py:31
  36.7 1.3 %collective-permute-start.1 = (f32[1,256,128]{2,1,0:T(8,128)S(1)}, f32[1,256,128]{2,1,0:T(8,128)S(1)}, u32[]{:S(2)}, u32[]{:S(2)}) collective-permute-start(f32[1,256,128]{2,1,0:T(8,128)S(1)} %copy-done), channel_id=1, source_target_pairs={{1,0},{2,1},{3,2},{0,3},{5,4},{6,5},{7,6},{4,7},{9,8},{10,9},{11,1... | collective-permute-start | bytes 393224 | tf_op jit(solution)/shard_map/ppermute | solution.py:31
  38.1 4.5 %collective-permute-done.1 = f32[1,256,128]{2,1,0:T(8,128)S(1)} collective-permute-done((f32[1,256,128]{2,1,0:T(8,128)S(1)}, f32[1,256,128]{2,1,0:T(8,128)S(1)}, u32[]{:S(2)}, u32[]{:S(2)}) %collective-permute-start.1) | collective-permute-done | bytes 131104 | tf_op jit(solution)/shard_map/ppermute | solution.py:31
  42.6 0.5 collective-permute-done.2
  43.1 0.0 collective-permute-done.3
  43.2 1.9 %dynamic-slice_sine_fusion = (f32[4,1,256,128]{3,2,1,0:T(8,128)S(1)}, f32[4,1,256,128]{3,2,1,0:T(8,128)S(1)}) fusion(f32[8,1,256,128]{3,2,1,0:T(8,128)S(1)} %bitcast_dynamic-update-slice_fusion.1, s32[]{:T(128)S(6)} %select_n.110), kind=kLoop, calls=%fused_computation.8 | loop fusion | bytes 1572868 | tf_op jit(solution)/shard_map/sin | solution.py:300
  45.1 0.2 copy.23
  45.3 0.2 copy.21
  45.6 0.6 cos.24
  46.2 2.0 %copy.22 = f32[8,32,4,4,32]{4,3,2,1,0:T(4,128)} copy(f32[8,32,4,4,32]{1,4,3,0,2:T(8,128)S(1)} %bitcast.25) | data formatting | bytes 1048576 | tf_op jit(solution)/shard_map/transpose | solution.py:267
  48.2 3.1 %reshape.164.chc_ref = f32[1024,128]{1,0:T(8,128)} reshape(f32[8,32,4,4,32]{4,3,2,1,0:T(4,128)} %copy.22) | data formatting | bytes 1048576 | tf_op jit(solution)/shard_map/reshape | solution.py:267
  51.3 0.6 sin.24
  51.9 2.0 %copy.24 = f32[8,32,4,4,32]{4,3,2,1,0:T(4,128)} copy(f32[8,32,4,4,32]{1,4,3,0,2:T(8,128)S(1)} %bitcast.26) | data formatting | bytes 1048576 | tf_op jit(solution)/shard_map/transpose | solution.py:267
  53.9 3.0 %reshape.165.chs_ref = f32[1024,128]{1,0:T(8,128)} reshape(f32[8,32,4,4,32]{4,3,2,1,0:T(4,128)} %copy.24) | data formatting | bytes 1048576 | tf_op jit(solution)/shard_map/reshape | solution.py:267
  56.9 4.3 %all-to-all-done = f32[32,8,2048]{2,1,0:T(8,128)} async-done(((f32[32,8,2048]{2,1,0:T(8,128)}), f32[32,8,2048]{2,1,0:T(8,128)}, u32[]{:S(2)}, u32[]{:S(2)}) %all-to-all-start) | async-done | bytes 2097184 | tf_op jit(solution)/shard_map/all_to_all | solution.py:262
  61.2 8.1 %shard_map.173 = f32[256,2048]{1,0:T(8,128)} custom-call(f32[256,2048]{1,0:T(8,128)} %bitcast.2.x_ref, f32[32,512]{1,0:T(8,128)} %constant.184.clone.twc_ref, f32[32,512]{1,0:T(8,128)} %constant.185.clone.tws_ref, bf16[256,256]{1,0:T(8,128)(2,1)} %constant.186.clone.bfh, bf16[256,256]{1,0:T(8,128)(2,1)} %constant.187.clone.bfl, ...), custom_call_target="tpu_custom_call" | custom-call | tf_op jit(solution)/shard_map/pallas_call | solution.py:252
  69.3 33.3 %all_to_all.10 = f32[32,8,2048]{2,1,0:T(8,128)} all-to-all(f32[32,8,2048]{2,1,0:T(8,128)} %bitcast.28), channel_id=1, replica_groups=mesh['band'=32,'seg'=4] {'band'}, dimensions={0} | all-to-all | bytes 4194304 | tf_op jit(solution)/shard_map/all_to_all | solution.py:262
  102.6 5.4 %shard_map.174 = f32[2,2,32,3072]{3,2,1,0:T(8,128)} custom-call(f32[256,2048]{1,0:T(8,128)} %bitcast.24, bf16[512,512]{1,0:T(8,128)(2,1)} %constant.190.clone.mh_ref, bf16[512,512]{1,0:T(8,128)(2,1)} %constant.191.clone.ml_ref, f32[32,256]{1,0:T(8,128)} %constant.192.clone.twc_ref, f32[32,256]{1,0:T(8,128)} %constant.193.clone.tws_ref), custom_call_target="tpu_custom_call" | custom-call | tf_op jit(solution)/shard_map/pallas_call | solution.py:252
  (13 shorter events, 0.1 us)
Async XLA Ops:
  1.1 14.7 %collective-permute-start = (f32[2,2,32,1024]{3,2,1,0:T(8,128)S(1)}, f32[2,2,32,1024]{3,2,1,0:T(8,128)S(1)}, u32[]{:S(2)}, u32[]{:S(2)}) collective-permute-start(f32[2,2,32,1024]{3,2,1,0:T(8,128)S(1)} %slice.4), channel_id=1, source_target_pairs={{0,1},{1,2},{2,3},{4,5},{5,6},{6,7},{8,9},{9,10},{10,11},{12,13},{... | collective-permute-start | bytes 1572872 | tf_op jit(solution)/shard_map/ppermute | solution.py:23
  15.8 0.8 copy-start.1
  22.8 8.5 %copy-start = (f32[1,256,128]{2,1,0:T(8,128)S(1)}, f32[1,256,128]{2,1,0:T(8,128)}, u32[]{:S(2)}) copy-start(f32[1,256,128]{2,1,0:T(8,128)} %param.19) | copy-start | bytes 393220
  22.8 38.4 %all-to-all-start = ((f32[32,8,2048]{2,1,0:T(8,128)}), f32[32,8,2048]{2,1,0:T(8,128)}, u32[]{:S(2)}, u32[]{:S(2)}) async-start(f32[32,8,2048]{2,1,0:T(8,128)} %bitcast.27), calls=%async_computation | async-start | bytes 4194304 | tf_op jit(solution)/shard_map/all_to_all | solution.py:262
  31.3 11.9 %collective-permute-start.3 = (f32[1,256,128]{2,1,0:T(8,128)S(1)}, f32[1,256,128]{2,1,0:T(8,128)S(1)}, u32[]{:S(2)}, u32[]{:S(2)}) collective-permute-start(f32[1,256,128]{2,1,0:T(8,128)S(1)} %copy-done), channel_id=1, source_target_pairs={{3,0},{0,1},{1,2},{2,3},{7,4},{4,5},{5,6},{6,7},{11,8},{8,9},{9,10... | collective-permute-start | bytes 393224 | tf_op jit(solution)/shard_map/ppermute | solution.py:31
  33.8 9.3 %collective-permute-start.2 = (f32[1,256,128]{2,1,0:T(8,128)S(1)}, f32[1,256,128]{2,1,0:T(8,128)S(1)}, u32[]{:S(2)}, u32[]{:S(2)}) collective-permute-start(f32[1,256,128]{2,1,0:T(8,128)S(1)} %copy-done), channel_id=1, source_target_pairs={{2,0},{3,1},{0,2},{1,3},{6,4},{7,5},{4,6},{5,7},{10,8},{11,9},{8,1... | collective-permute-start | bytes 393224 | tf_op jit(solution)/shard_map/ppermute | solution.py:31
  36.7 5.9 %collective-permute-start.1 = (f32[1,256,128]{2,1,0:T(8,128)S(1)}, f32[1,256,128]{2,1,0:T(8,128)S(1)}, u32[]{:S(2)}, u32[]{:S(2)}) collective-permute-start(f32[1,256,128]{2,1,0:T(8,128)S(1)} %copy-done), channel_id=1, source_target_pairs={{1,0},{2,1},{3,2},{0,3},{5,4},{6,5},{7,6},{4,7},{9,8},{10,9},{11,1... | collective-permute-start | bytes 393224 | tf_op jit(solution)/shard_map/ppermute | solution.py:31

commit v11 on v10

--- a/solution.py
+++ b/solution.py
@@ -138,6 +138,29 @@
                    np.where(riout[None, :] == 0, c, s),
                    np.where(riout[None, :] == 0, -s, c))
     return (val * same / LENGTH).astype(np.float32)
+
+
+def built_send_matrices(index):
+    row, col = index[:256][:, None], index[None, :]
+    pp, k2 = (row // 4) % 2, 4 * (row // 8) + row % 4
+    pin, riin, lane = col // 256, (col // 128) % 2, col % 128
+    c, s = unit(k2 * lane, 128, -1)
+    same = (pp == pin).astype(F32)
+    return jnp.where(riin == 0, c, -s) * same, jnp.where(riin == 0, s, c) * same
+
+
+def built_receive_matrix(index):
+    row, col = index[:, None], index[None, :]
+    riin, pp, k2 = row // 256, (row // 4) % 2, 4 * ((row // 8) % 32) + row % 4
+    pout, riout, lc = col // 256, (col // 128) % 2, col % 128
+    c, s = unit(k2 * lc, 128, 1)
+    val = jnp.where(riin == 0, jnp.where(riout == 0, c, s), jnp.where(riout == 0, -s, c))
+    return val * (pp == pout).astype(F32) * F32(1.0 / LENGTH)
+
+
+def split_matrix(m):
+    hi = lax.reduce_precision(m, exponent_bits=8, mantissa_bits=7)
+    return hi.astype(BF16), (m - hi).astype(BF16)
 
 
 def lane_twiddle(sign, width):
@@ -289,10 +312,11 @@
     back_c, back_s, history = lax.optimization_barrier((back_c, back_s, history))
 
     t1c, t1s = lane_twiddle(-1, 128)
-    lr, li = send_matrices()
+    index = lax.optimization_barrier(jnp.arange(512, dtype=jnp.int32))
+    lr, li = built_send_matrices(index)
     (send,) = call(column_forward_kernel, [(256, 2048)], [(1024, 512)],
                    block, history, jnp.asarray(t1c), jnp.asarray(t1s), t2c, t2s,
-                   *halves(lr), *halves(li), pac, pas, pbc, pbs)
+                   *split_matrix(lr), *split_matrix(li), pac, pas, pbc, pbs)
     received = exchanged(send)
 
     chirp_phase, send = lax.optimization_barrier((chirp_phase, send))
@@ -307,7 +331,7 @@
 
     cc, cs = lane_twiddle(1, 256)
     (out,) = call(column_inverse_kernel, [(2, 2, ROWS_DEV, 3072)], [(1024, 512)],
-                  returned, *halves(receive_matrix()), jnp.asarray(cc), jnp.asarray(cs))
+                  returned, *split_matrix(built_receive_matrix(index)), jnp.asarray(cc), jnp.asarray(cs))
     return out[None, None]
 
 

time: 109 us -> 111 us (1.018)
  blocking collectives: 33.3 us -> 0 us
  waiting for transfers between devices: 11.7 us -> 35.4 us
  other arithmetic: 8.69 us -> 18.1 us
  starting transfers between devices: 18.8 us -> 20.8 us
  local copies, waits for them, and re-layouts: 15.6 us -> 16.9 us
    all_to_all x1 -> x0, blocking collectives: 33.3 us -> none  [exchanged(): lax.all_to_all(block.reshape(32, rows // 32, width), 'band', 0, 0, tiled=...]
    all_to_all x1 -> x2, waiting for transfers between devices: 4.29 us -> 27.4 us  [exchanged(): lax.all_to_all(block.reshape(32, rows // 32, width), 'band', 0, 0, tiled=...]
    convert_element_type x0 -> x2, other arithmetic: none -> 9.4 us  [split_matrix(): return (hi.astype(BF16), (m - hi).astype(BF16))]
    all_to_all x1 -> x2, starting transfers between devices: 8.42 us -> 12.7 us  [exchanged(): lax.all_to_all(block.reshape(32, rows // 32, width), 'band', 0, 0, tiled=...]
    ppermute x3, waiting for transfers between devices: 5.01 us -> 7.99 us  [gathered(): pieces.append(lax.ppermute(block, axis, route))]
    ppermute x1, waiting for transfers between devices: 2.4 us -> 0.01 us  [passed_along(): return lax.ppermute(block, axis, route)]
    ppermute x3, starting transfers between devices: 6.8 us -> 4.53 us  [gathered(): pieces.append(lax.ppermute(block, axis, route))]
    unnamed x11 -> x13, local copies, waits for them, and re-layouts: 0.89 us -> 2.19 us
  transfers between devices with their start and end apart: 5 -> 6, of which waited for: 4 -> 5; matrix products, arithmetic and copies ran while one was open for 21% -> 29% of each run, Pallas kernels for 0% -> 0%
where the time goes in v11:
time: 111 us
  waiting for transfers between devices  35.4 us (32%)
  starting transfers between devices  20.8 us (19%)
  Pallas kernels  19.6 us (18%)
  other arithmetic  18.1 us (16%)
  local copies, waits for them, and re-layouts  16.9 us (15%)
    all_to_all x2, waiting for transfers between devices, exchanged(): lax.all_to_all(block.reshape(32, rows // 32, width), 'band', 0, 0, tiled=...  27.4 us
    pallas_call x3, Pallas kernels, call(): pl.pallas_call(kernel, out_shape=[jax.ShapeDtypeStruct(s, F32) for s in o...  19.6 us
    all_to_all x2, starting transfers between devices, exchanged(): lax.all_to_all(block.reshape(32, rows // 32, width), 'band', 0, 0, tiled=...  12.7 us
    convert_element_type x2, other arithmetic, split_matrix(): return (hi.astype(BF16), (m - hi).astype(BF16))  9.4 us
    sin x4, other arithmetic, unit(): return (jnp.cos(angle), jnp.sin(angle))  8.63 us
    ppermute x3, waiting for transfers between devices, gathered(): pieces.append(lax.ppermute(block, axis, route))  7.99 us
    reshape x2, local copies, waits for them, and re-layouts, arranged(): table.reshape(32, 32, 4, 8, 4).transpose(3, 1, 2, 4, 0).reshape(1024, 128)  6.1 us
    ppermute x3, starting transfers between devices, gathered(): pieces.append(lax.ppermute(block, axis, route))  4.53 us
  transfers between devices with their start and end apart: 6, of which 5 were waited for; matrix products, arithmetic and copies ran while one was open for 29% of the time, Pallas kernels for 0%

profile of v11, /device:TPU:0, one launch (start us, length us, event | category | flops | bytes accessed | tf_op | source)
XLA Modules:
  0.0 111.0 jit_solution(3973193963383893906)
XLA Ops:
  0.0 1.1 slice.8
  1.1 3.6 %collective-permute-start = (f32[2,2,32,1024]{3,2,1,0:T(8,128)S(1)}, f32[2,2,32,1024]{3,2,1,0:T(8,128)S(1)}, u32[]{:S(2)}, u32[]{:S(2)}) collective-permute-start(f32[2,2,32,1024]{3,2,1,0:T(8,128)S(1)} %slice.8), channel_id=1, source_target_pairs={{0,1},{1,2},{2,3},{4,5},{5,6},{6,7},{8,9},{9,10},{10,11},{12,13},{... | collective-permute-start | bytes 1572872 | tf_op jit(solution)/shard_map/ppermute | solution.py:23
  4.8 1.2 %fusion.22 = (f32[32,1024]{1,0:T(8,128)}, f32[32,1024]{1,0:T(8,128)}) fusion(s32[1024]{0:T(1024)S(1)} %get-tuple-element.41), kind=kLoop, calls=%fused_computation.57 | loop fusion | flops 458752 | bytes 266240 | tf_op jit(solution)/shard_map/sin | solution.py:92
  6.1 0.8 fusion.35
  6.8 0.8 fusion.30
  7.6 3.4 %fusion.10 = (bf16[256,512]{1,0:T(8,128)(2,1)}, bf16[256,512]{1,0:T(8,128)(2,1)}, bf16[256,512]{1,0:T(8,128)(2,1)}, bf16[256,512]{1,0:T(8,128)(2,1)}) fusion(s32[512]{0:T(512)S(1)} %get-tuple-element.31, s32[256]{0:T(256)S(1)} %get-tuple-element.34, s32[512]{0:T(512)S(1)} %get-tuple-element.14, s32[256]{0:T(256)S(1)} %get-tuple-element.33, ...), kind=kLoop, calls=%fused_computation.32 | loop fusion | flops 3670016 | bytes 1055232 | tf_op jit(solution)/shard_map/convert_element_type | solution.py:163
  11.0 5.8 %fusion.7 = (f32[256,1024]{1,0:T(8,128)}, f32[256,1024]{1,0:T(8,128)}) fusion(s32[256]{0:T(256)S(1)} %get-tuple-element.39, s32[1024]{0:T(1024)S(1)} %get-tuple-element.38, s32[1024]{0:T(1024)S(1)} %get-tuple-element.37, s32[256]{0:T(256)S(1)} %get-tuple-element.40), kind=kLoop, calls=%fused_computation.29 | loop fusion | flops 4194304 | bytes 2107392 | tf_op jit(solution)/shard_map/sin | solution.py:92
  16.9 0.0 collective-permute-done.hist_ref
  16.9 0.0 copy-start.2
  16.9 0.8 copy-done.2
  17.7 6.2 %shard_map.118 = f32[256,2048]{1,0:T(8,128)} custom-call(f32[2,2,32,3072]{3,2,1,0:T(8,128)} %bitcast.30, f32[2,2,32,1024]{3,2,1,0:T(8,128)} %copy-done.2, f32[32,128]{1,0:T(8,128)} %constant.315.clone.t1c, f32[32,128]{1,0:T(8,128)} %constant.316.clone.t1s, f32[32,32]{1,0:T(8,128)} %get-tuple-element.36.t2c, f32[32,32]{1,0:T(8,128)} %get-tuple-element.35.t2s, ...), custom_call_target="tpu_custom_call" | custom-call | tf_op jit(solution)/shard_map/pallas_call | solution.py:275
  23.8 0.0 copy-start.1
  23.8 8.4 %all-to-all-start = ((f32[32,8,2048]{2,1,0:T(8,128)}), f32[32,8,2048]{2,1,0:T(8,128)}, u32[]{:S(2)}, u32[]{:S(2)}) async-start(f32[32,8,2048]{2,1,0:T(8,128)} %bitcast.27), calls=%async_computation | async-start | bytes 4194304 | tf_op jit(solution)/shard_map/all_to_all | solution.py:285
  32.3 0.0 copy-done.1
  32.3 2.9 %collective-permute-start.1 = (f32[1,256,128]{2,1,0:T(8,128)S(1)}, f32[1,256,128]{2,1,0:T(8,128)S(1)}, u32[]{:S(2)}, u32[]{:S(2)}) collective-permute-start(f32[1,256,128]{2,1,0:T(8,128)S(1)} %copy-done.1), channel_id=1, source_target_pairs={{1,0},{2,1},{3,2},{0,3},{5,4},{6,5},{7,6},{4,7},{9,8},{10,9},{11,1... | collective-permute-start | bytes 393224 | tf_op jit(solution)/shard_map/ppermute | solution.py:31
  35.2 0.7 collective-permute-start.2
  36.0 0.9 collective-permute-start.3
  36.8 4.3 %collective-permute-done.1 = f32[1,256,128]{2,1,0:T(8,128)S(1)} collective-permute-done((f32[1,256,128]{2,1,0:T(8,128)S(1)}, f32[1,256,128]{2,1,0:T(8,128)S(1)}, u32[]{:S(2)}, u32[]{:S(2)}) %collective-permute-start.1) | collective-permute-done | bytes 131104 | tf_op jit(solution)/shard_map/ppermute | solution.py:31
  41.2 1.9 %collective-permute-done.2 = f32[1,256,128]{2,1,0:T(8,128)S(1)} collective-permute-done((f32[1,256,128]{2,1,0:T(8,128)S(1)}, f32[1,256,128]{2,1,0:T(8,128)S(1)}, u32[]{:S(2)}, u32[]{:S(2)}) %collective-permute-start.2) | collective-permute-done | bytes 131104 | tf_op jit(solution)/shard_map/ppermute | solution.py:31
  43.1 1.7 %collective-permute-done.3 = f32[1,256,128]{2,1,0:T(8,128)S(1)} collective-permute-done((f32[1,256,128]{2,1,0:T(8,128)S(1)}, f32[1,256,128]{2,1,0:T(8,128)S(1)}, u32[]{:S(2)}, u32[]{:S(2)}) %collective-permute-start.3) | collective-permute-done | bytes 131104 | tf_op jit(solution)/shard_map/ppermute | solution.py:31
  45.0 1.9 %dynamic-slice_sine_fusion = (f32[4,1,256,128]{3,2,1,0:T(8,128)S(1)}, f32[4,1,256,128]{3,2,1,0:T(8,128)S(1)}) fusion(f32[8,1,256,128]{3,2,1,0:T(8,128)S(1)} %bitcast_dynamic-update-slice_fusion.1, s32[]{:T(128)S(6)} %select_n.226), kind=kLoop, calls=%fused_computation.36 | loop fusion | bytes 1572868 | tf_op jit(solution)/shard_map/sin | solution.py:324
  46.8 0.2 copy.15
  47.1 0.6 cos.31
  47.7 2.0 %copy.16 = f32[8,32,4,4,32]{4,3,2,1,0:T(4,128)} copy(f32[8,32,4,4,32]{1,4,3,0,2:T(8,128)S(1)} %bitcast.25) | data formatting | bytes 1048576 | tf_op jit(solution)/shard_map/transpose | solution.py:290
  49.7 3.0 %reshape.342.chc_ref = f32[1024,128]{1,0:T(8,128)} reshape(f32[8,32,4,4,32]{4,3,2,1,0:T(4,128)} %copy.16) | data formatting | bytes 1048576 | tf_op jit(solution)/shard_map/reshape | solution.py:290
  52.7 0.2 copy.17
  52.9 0.6 sin.31
  53.5 2.0 %copy.18 = f32[8,32,4,4,32]{4,3,2,1,0:T(4,128)} copy(f32[8,32,4,4,32]{1,4,3,0,2:T(8,128)S(1)} %bitcast.26) | data formatting | bytes 1048576 | tf_op jit(solution)/shard_map/transpose | solution.py:290
  55.5 3.1 %reshape.343.chs_ref = f32[1024,128]{1,0:T(8,128)} reshape(f32[8,32,4,4,32]{4,3,2,1,0:T(4,128)} %copy.18) | data formatting | bytes 1048576 | tf_op jit(solution)/shard_map/reshape | solution.py:290
  58.6 3.6 %all-to-all-done = f32[32,8,2048]{2,1,0:T(8,128)} async-done(((f32[32,8,2048]{2,1,0:T(8,128)}), f32[32,8,2048]{2,1,0:T(8,128)}, u32[]{:S(2)}, u32[]{:S(2)}) %all-to-all-start) | async-done | bytes 2097184 | tf_op jit(solution)/shard_map/all_to_all | solution.py:285
  62.2 8.1 %shard_map.119 = f32[256,2048]{1,0:T(8,128)} custom-call(f32[256,2048]{1,0:T(8,128)} %bitcast.2.x_ref, f32[32,512]{1,0:T(8,128)} %constant.317.clone.twc_ref, f32[32,512]{1,0:T(8,128)} %constant.318.clone.tws_ref, bf16[256,256]{1,0:T(8,128)(2,1)} %constant.319.clone.bfh, bf16[256,256]{1,0:T(8,128)(2,1)} %constant.320.clone.bfl, ...), custom_call_target="tpu_custom_call" | custom-call | tf_op jit(solution)/shard_map/pallas_call | solution.py:275
  70.3 4.2 %all-to-all-start.1 = ((f32[32,8,2048]{2,1,0:T(8,128)}), f32[32,8,2048]{2,1,0:T(8,128)S(1)}, u32[]{:S(2)}, u32[]{:S(2)}) async-start(f32[32,8,2048]{2,1,0:T(8,128)} %bitcast.28), calls=%async_computation.1 | async-start | bytes 4194304 | tf_op jit(solution)/shard_map/all_to_all | solution.py:285
  74.5 6.0 %fusion = (bf16[512,512]{1,0:T(8,128)(2,1)}, bf16[512,512]{1,0:T(8,128)(2,1)}) fusion(s32[512]{0:T(512)S(1)} %get-tuple-element.31, s32[512]{0:T(512)S(1)} %get-tuple-element.30, pred[512]{0:T(512)(128)(4,1)S(1)} %get-tuple-element.32, pred[512]{0:T(512)(128)(4,1)S(1)} %get-tuple-element.13, s32[512]{0:T(512)S(1)} %get-tuple-element.14, ...), kind=kLoop, calls=%fused_computation.10 | loop fusion | flops 6553600 | bytes 1057792 | tf_op jit(solution)/shard_map/convert_element_type | solution.py:163
  80.5 23.8 %all-to-all-done.1 = f32[32,8,2048]{2,1,0:T(8,128)S(1)} async-done(((f32[32,8,2048]{2,1,0:T(8,128)}), f32[32,8,2048]{2,1,0:T(8,128)S(1)}, u32[]{:S(2)}, u32[]{:S(2)}) %all-to-all-start.1) | async-done | bytes 2097184 | tf_op jit(solution)/shard_map/all_to_all | solution.py:285
  104.3 0.0 copy-start
  104.3 1.3 %copy-done = f32[32,8,2048]{2,1,0:T(8,128)} copy-done((f32[32,8,2048]{2,1,0:T(8,128)}, f32[32,8,2048]{2,1,0:T(8,128)S(1)}, u32[]{:S(2)}) %copy-start) | copy-done | bytes 2097176
  105.6 5.4 %shard_map.120 = f32[2,2,32,3072]{3,2,1,0:T(8,128)} custom-call(f32[256,2048]{1,0:T(8,128)} %bitcast.24, bf16[512,512]{1,0:T(8,128)(2,1)} %get-tuple-element.20.mh_ref, bf16[512,512]{1,0:T(8,128)(2,1)} %get-tuple-element.19.ml_ref, f32[32,256]{1,0:T(8,128)} %constant.323.clone.twc_ref, f32[32,256]{1,0:T(8,128)} %constant.324.clone.tws_ref), custom_call_target="tpu_custom_call" | custom-call | tf_op jit(solution)/shard_map/pallas_call | solution.py:275
  (17 shorter events, 0.2 us)
Async XLA Ops:
  1.1 15.8 %collective-permute-start = (f32[2,2,32,1024]{3,2,1,0:T(8,128)S(1)}, f32[2,2,32,1024]{3,2,1,0:T(8,128)S(1)}, u32[]{:S(2)}, u32[]{:S(2)}) collective-permute-start(f32[2,2,32,1024]{3,2,1,0:T(8,128)S(1)} %slice.8), channel_id=1, source_target_pairs={{0,1},{1,2},{2,3},{4,5},{5,6},{6,7},{8,9},{9,10},{10,11},{12,13},{... | collective-permute-start | bytes 1572872 | tf_op jit(solution)/shard_map/ppermute | solution.py:23
  16.9 0.8 copy-start.2
  23.8 8.5 %copy-start.1 = (f32[1,256,128]{2,1,0:T(8,128)S(1)}, f32[1,256,128]{2,1,0:T(8,128)}, u32[]{:S(2)}) copy-start(f32[1,256,128]{2,1,0:T(8,128)} %param.13) | copy-start | bytes 393220
  23.8 38.4 %all-to-all-start = ((f32[32,8,2048]{2,1,0:T(8,128)}), f32[32,8,2048]{2,1,0:T(8,128)}, u32[]{:S(2)}, u32[]{:S(2)}) async-start(f32[32,8,2048]{2,1,0:T(8,128)} %bitcast.27), calls=%async_computation | async-start | bytes 4194304 | tf_op jit(solution)/shard_map/all_to_all | solution.py:285
  32.3 8.9 %collective-permute-start.1 = (f32[1,256,128]{2,1,0:T(8,128)S(1)}, f32[1,256,128]{2,1,0:T(8,128)S(1)}, u32[]{:S(2)}, u32[]{:S(2)}) collective-permute-start(f32[1,256,128]{2,1,0:T(8,128)S(1)} %copy-done.1), channel_id=1, source_target_pairs={{1,0},{2,1},{3,2},{0,3},{5,4},{6,5},{7,6},{4,7},{9,8},{10,9},{11,1... | collective-permute-start | bytes 393224 | tf_op jit(solution)/shard_map/ppermute | solution.py:31
  35.2 7.9 %collective-permute-start.2 = (f32[1,256,128]{2,1,0:T(8,128)S(1)}, f32[1,256,128]{2,1,0:T(8,128)S(1)}, u32[]{:S(2)}, u32[]{:S(2)}) collective-permute-start(f32[1,256,128]{2,1,0:T(8,128)S(1)} %copy-done.1), channel_id=1, source_target_pairs={{2,0},{3,1},{0,2},{1,3},{6,4},{7,5},{4,6},{5,7},{10,8},{11,9},{8,1... | collective-permute-start | bytes 393224 | tf_op jit(solution)/shard_map/ppermute | solution.py:31
  36.0 8.9 %collective-permute-start.3 = (f32[1,256,128]{2,1,0:T(8,128)S(1)}, f32[1,256,128]{2,1,0:T(8,128)S(1)}, u32[]{:S(2)}, u32[]{:S(2)}) collective-permute-start(f32[1,256,128]{2,1,0:T(8,128)S(1)} %copy-done.1), channel_id=1, source_target_pairs={{3,0},{0,1},{1,2},{2,3},{7,4},{4,5},{5,6},{6,7},{11,8},{8,9},{9,10... | collective-permute-start | bytes 393224 | tf_op jit(solution)/shard_map/ppermute | solution.py:31
  70.3 34.0 %all-to-all-start.1 = ((f32[32,8,2048]{2,1,0:T(8,128)}), f32[32,8,2048]{2,1,0:T(8,128)S(1)}, u32[]{:S(2)}, u32[]{:S(2)}) async-start(f32[32,8,2048]{2,1,0:T(8,128)} %bitcast.28), calls=%async_computation.1 | async-start | bytes 4194304 | tf_op jit(solution)/shard_map/all_to_all | solution.py:285
  104.3 1.3 %copy-start = (f32[32,8,2048]{2,1,0:T(8,128)}, f32[32,8,2048]{2,1,0:T(8,128)S(1)}, u32[]{:S(2)}) copy-start(f32[32,8,2048]{2,1,0:T(8,128)S(1)} %all-to-all-done.1) | copy-start | bytes 6291460

commit v12 on v10

--- a/solution.py
+++ b/solution.py
@@ -153,6 +153,7 @@
 
 def column_forward_kernel(blk_ref, hist_ref, t1c, t1s, t2c, t2s, lrh, lrl, lih, lil, pac, pas, pbc, pbs,
                           out_ref, xs_ref):
+    tw = [cmul(t1c[k:k + 1, :], t1s[k:k + 1, :], t2c[:, k:k + 1], t2s[:, k:k + 1]) for k in range(32)]
     for p in range(2):
         xr, xi = [], []
         for t in range(32):
@@ -164,8 +165,7 @@
                 xi.append(blk_ref[p, 1, :, (t - 8) * 128:(t - 7) * 128])
         ar, ai = fft_list(xr, xi, -1)
         for k in range(32):
-            wc, ws = cmul(t1c[k:k + 1, :], t1s[k:k + 1, :], t2c[:, k:k + 1], t2s[:, k:k + 1])
-            re, im = cmul(ar[k], ai[k], wc, ws)
+            re, im = cmul(ar[k], ai[k], *tw[k])
             xs_ref[k * 32:(k + 1) * 32, p * 256:p * 256 + 128] = re
             xs_ref[k * 32:(k + 1) * 32, p * 256 + 128:p * 256 + 256] = im
     dims = (((1,), (1,)), ((), ()))

time: 109 us -> 109 us (level)
  no operation moved by 1% of the time
where the time goes in v12:
time: 109 us; the launch traced here: 108 us
  blocking collectives  33.3 us (31%)
  Pallas kernels  19.5 us (18%)
  starting transfers between devices  18.8 us (17%)
  local copies, waits for them, and re-layouts  15.6 us (14%)
  waiting for transfers between devices  11.7 us (11%)
  other arithmetic  8.69 us (8%)
    all_to_all x1, blocking collectives, exchanged(): lax.all_to_all(block.reshape(32, rows // 32, width), 'band', 0, 0, tiled=...  33.3 us
    pallas_call x3, Pallas kernels, call(): pl.pallas_call(kernel, out_shape=[jax.ShapeDtypeStruct(s, F32) for s in o...  19.5 us
    sin x4, other arithmetic, unit(): return (jnp.cos(angle), jnp.sin(angle))  8.67 us
    all_to_all x1, starting transfers between devices, exchanged(): lax.all_to_all(block.reshape(32, rows // 32, width), 'band', 0, 0, tiled=...  8.42 us
    ppermute x3, starting transfers between devices, gathered(): pieces.append(lax.ppermute(block, axis, route))  6.8 us
    reshape x2, local copies, waits for them, and re-layouts, arranged(): table.reshape(32, 32, 4, 8, 4).transpose(3, 1, 2, 4, 0).reshape(1024, 128)  6.1 us
    ppermute x3, waiting for transfers between devices, gathered(): pieces.append(lax.ppermute(block, axis, route))  5.01 us
    all_to_all x1, waiting for transfers between devices, exchanged(): lax.all_to_all(block.reshape(32, rows // 32, width), 'band', 0, 0, tiled=...  4.29 us
  transfers between devices with their start and end apart: 5, of which 4 were waited for; matrix products, arithmetic and copies ran while one was open for 21% of the time, Pallas kernels for 0%

profile of v12, /device:TPU:0, one launch (start us, length us, event | category | flops | bytes accessed | tf_op | source)
XLA Modules:
  0.0 107.9 jit_solution(12563102953694802830)
XLA Ops:
  0.0 1.1 slice.4
  1.1 3.6 %collective-permute-start = (f32[2,2,32,1024]{3,2,1,0:T(8,128)S(1)}, f32[2,2,32,1024]{3,2,1,0:T(8,128)S(1)}, u32[]{:S(2)}, u32[]{:S(2)}) collective-permute-start(f32[2,2,32,1024]{3,2,1,0:T(8,128)S(1)} %slice.4), channel_id=1, source_target_pairs={{0,1},{1,2},{2,3},{4,5},{5,6},{6,7},{8,9},{9,10},{10,11},{12,13},{... | collective-permute-start | bytes 1572872 | tf_op jit(solution)/shard_map/ppermute | solution.py:23
  4.7 0.8 fusion.24
  5.5 0.8 fusion.19
  6.3 1.3 %fusion.11 = (f32[32,1024]{1,0:T(8,128)}, f32[32,1024]{1,0:T(8,128)}) fusion(s32[1024]{0:T(1024)S(1)} %get-tuple-element.27), kind=kLoop, calls=%fused_computation.27 | loop fusion | flops 458752 | bytes 266240 | tf_op jit(solution)/shard_map/sin | solution.py:92
  7.6 5.8 %fusion.3 = (f32[256,1024]{1,0:T(8,128)}, f32[256,1024]{1,0:T(8,128)}) fusion(s32[256]{0:T(256)S(1)} %get-tuple-element.25, s32[1024]{0:T(1024)S(1)} %get-tuple-element.24, s32[1024]{0:T(1024)S(1)} %get-tuple-element.23, s32[256]{0:T(256)S(1)} %get-tuple-element.26), kind=kLoop, calls=%fused_computation.6 | loop fusion | flops 4194304 | bytes 2107392 | tf_op jit(solution)/shard_map/sin | solution.py:92
  13.4 2.4 %collective-permute-done.hist_ref = f32[2,2,32,1024]{3,2,1,0:T(8,128)S(1)} collective-permute-done((f32[2,2,32,1024]{3,2,1,0:T(8,128)S(1)}, f32[2,2,32,1024]{3,2,1,0:T(8,128)S(1)}, u32[]{:S(2)}, u32[]{:S(2)}) %collective-permute-start) | collective-permute-done | bytes 524320 | tf_op jit(solution)/shard_map/ppermute | solution.py:23
  15.8 0.0 copy-start.1
  15.8 0.8 copy-done.1
  16.6 6.1 %shard_map.172 = f32[256,2048]{1,0:T(8,128)} custom-call(f32[2,2,32,3072]{3,2,1,0:T(8,128)} %bitcast.30, f32[2,2,32,1024]{3,2,1,0:T(8,128)} %copy-done.1, f32[32,128]{1,0:T(8,128)} %constant.178.clone.t1c, f32[32,128]{1,0:T(8,128)} %constant.179.clone.t1s, f32[32,32]{1,0:T(8,128)} %get-tuple-element.22.t2c, f32[32,32]{1,0:T(8,128)} %get-tuple-element.21.t2s, ...), custom_call_target="tpu_custom_call" | custom-call | tf_op jit(solution)/shard_map/pallas_call | solution.py:252
  22.7 0.0 copy-start
  22.7 8.4 %all-to-all-start = ((f32[32,8,2048]{2,1,0:T(8,128)}), f32[32,8,2048]{2,1,0:T(8,128)}, u32[]{:S(2)}, u32[]{:S(2)}) async-start(f32[32,8,2048]{2,1,0:T(8,128)} %bitcast.27), calls=%async_computation | async-start | bytes 4194304 | tf_op jit(solution)/shard_map/all_to_all | solution.py:262
  31.2 0.0 copy-done
  31.2 2.6 %collective-permute-start.3 = (f32[1,256,128]{2,1,0:T(8,128)S(1)}, f32[1,256,128]{2,1,0:T(8,128)S(1)}, u32[]{:S(2)}, u32[]{:S(2)}) collective-permute-start(f32[1,256,128]{2,1,0:T(8,128)S(1)} %copy-done), channel_id=1, source_target_pairs={{3,0},{0,1},{1,2},{2,3},{7,4},{4,5},{5,6},{6,7},{11,8},{8,9},{9,10... | collective-permute-start | bytes 393224 | tf_op jit(solution)/shard_map/ppermute | solution.py:31
  33.7 2.9 %collective-permute-start.2 = (f32[1,256,128]{2,1,0:T(8,128)S(1)}, f32[1,256,128]{2,1,0:T(8,128)S(1)}, u32[]{:S(2)}, u32[]{:S(2)}) collective-permute-start(f32[1,256,128]{2,1,0:T(8,128)S(1)} %copy-done), channel_id=1, source_target_pairs={{2,0},{3,1},{0,2},{1,3},{6,4},{7,5},{4,6},{5,7},{10,8},{11,9},{8,1... | collective-permute-start | bytes 393224 | tf_op jit(solution)/shard_map/ppermute | solution.py:31
  36.6 1.3 %collective-permute-start.1 = (f32[1,256,128]{2,1,0:T(8,128)S(1)}, f32[1,256,128]{2,1,0:T(8,128)S(1)}, u32[]{:S(2)}, u32[]{:S(2)}) collective-permute-start(f32[1,256,128]{2,1,0:T(8,128)S(1)} %copy-done), channel_id=1, source_target_pairs={{1,0},{2,1},{3,2},{0,3},{5,4},{6,5},{7,6},{4,7},{9,8},{10,9},{11,1... | collective-permute-start | bytes 393224 | tf_op jit(solution)/shard_map/ppermute | solution.py:31
  38.0 4.5 %collective-permute-done.1 = f32[1,256,128]{2,1,0:T(8,128)S(1)} collective-permute-done((f32[1,256,128]{2,1,0:T(8,128)S(1)}, f32[1,256,128]{2,1,0:T(8,128)S(1)}, u32[]{:S(2)}, u32[]{:S(2)}) %collective-permute-start.1) | collective-permute-done | bytes 131104 | tf_op jit(solution)/shard_map/ppermute | solution.py:31
  42.5 0.5 collective-permute-done.2
  43.0 0.0 collective-permute-done.3
  43.1 1.9 %dynamic-slice_sine_fusion = (f32[4,1,256,128]{3,2,1,0:T(8,128)S(1)}, f32[4,1,256,128]{3,2,1,0:T(8,128)S(1)}) fusion(f32[8,1,256,128]{3,2,1,0:T(8,128)S(1)} %bitcast_dynamic-update-slice_fusion.1, s32[]{:T(128)S(6)} %select_n.110), kind=kLoop, calls=%fused_computation.8 | loop fusion | bytes 1572868 | tf_op jit(solution)/shard_map/sin | solution.py:300
  45.0 0.2 copy.23
  45.2 0.2 copy.21
  45.5 0.6 cos.24
  46.1 2.0 %copy.22 = f32[8,32,4,4,32]{4,3,2,1,0:T(4,128)} copy(f32[8,32,4,4,32]{1,4,3,0,2:T(8,128)S(1)} %bitcast.25) | data formatting | bytes 1048576 | tf_op jit(solution)/shard_map/transpose | solution.py:267
  48.1 3.1 %reshape.164.chc_ref = f32[1024,128]{1,0:T(8,128)} reshape(f32[8,32,4,4,32]{4,3,2,1,0:T(4,128)} %copy.22) | data formatting | bytes 1048576 | tf_op jit(solution)/shard_map/reshape | solution.py:267
  51.2 0.6 sin.24
  51.8 2.0 %copy.24 = f32[8,32,4,4,32]{4,3,2,1,0:T(4,128)} copy(f32[8,32,4,4,32]{1,4,3,0,2:T(8,128)S(1)} %bitcast.26) | data formatting | bytes 1048576 | tf_op jit(solution)/shard_map/transpose | solution.py:267
  53.8 3.0 %reshape.165.chs_ref = f32[1024,128]{1,0:T(8,128)} reshape(f32[8,32,4,4,32]{4,3,2,1,0:T(4,128)} %copy.24) | data formatting | bytes 1048576 | tf_op jit(solution)/shard_map/reshape | solution.py:267
  56.8 4.3 %all-to-all-done = f32[32,8,2048]{2,1,0:T(8,128)} async-done(((f32[32,8,2048]{2,1,0:T(8,128)}), f32[32,8,2048]{2,1,0:T(8,128)}, u32[]{:S(2)}, u32[]{:S(2)}) %all-to-all-start) | async-done | bytes 2097184 | tf_op jit(solution)/shard_map/all_to_all | solution.py:262
  61.1 8.1 %shard_map.173 = f32[256,2048]{1,0:T(8,128)} custom-call(f32[256,2048]{1,0:T(8,128)} %bitcast.2.x_ref, f32[32,512]{1,0:T(8,128)} %constant.184.clone.twc_ref, f32[32,512]{1,0:T(8,128)} %constant.185.clone.tws_ref, bf16[256,256]{1,0:T(8,128)(2,1)} %constant.186.clone.bfh, bf16[256,256]{1,0:T(8,128)(2,1)} %constant.187.clone.bfl, ...), custom_call_target="tpu_custom_call" | custom-call | tf_op jit(solution)/shard_map/pallas_call | solution.py:252
  69.2 33.3 %all_to_all.10 = f32[32,8,2048]{2,1,0:T(8,128)} all-to-all(f32[32,8,2048]{2,1,0:T(8,128)} %bitcast.28), channel_id=1, replica_groups=mesh['band'=32,'seg'=4] {'band'}, dimensions={0} | all-to-all | bytes 4194304 | tf_op jit(solution)/shard_map/all_to_all | solution.py:262
  102.5 5.4 %shard_map.174 = f32[2,2,32,3072]{3,2,1,0:T(8,128)} custom-call(f32[256,2048]{1,0:T(8,128)} %bitcast.24, bf16[512,512]{1,0:T(8,128)(2,1)} %constant.190.clone.mh_ref, bf16[512,512]{1,0:T(8,128)(2,1)} %constant.191.clone.ml_ref, f32[32,256]{1,0:T(8,128)} %constant.192.clone.twc_ref, f32[32,256]{1,0:T(8,128)} %constant.193.clone.tws_ref), custom_call_target="tpu_custom_call" | custom-call | tf_op jit(solution)/shard_map/pallas_call | solution.py:252
  (13 shorter events, 0.1 us)
Async XLA Ops:
  1.1 14.7 %collective-permute-start = (f32[2,2,32,1024]{3,2,1,0:T(8,128)S(1)}, f32[2,2,32,1024]{3,2,1,0:T(8,128)S(1)}, u32[]{:S(2)}, u32[]{:S(2)}) collective-permute-start(f32[2,2,32,1024]{3,2,1,0:T(8,128)S(1)} %slice.4), channel_id=1, source_target_pairs={{0,1},{1,2},{2,3},{4,5},{5,6},{6,7},{8,9},{9,10},{10,11},{12,13},{... | collective-permute-start | bytes 1572872 | tf_op jit(solution)/shard_map/ppermute | solution.py:23
  15.8 0.8 copy-start.1
  22.7 8.5 %copy-start = (f32[1,256,128]{2,1,0:T(8,128)S(1)}, f32[1,256,128]{2,1,0:T(8,128)}, u32[]{:S(2)}) copy-start(f32[1,256,128]{2,1,0:T(8,128)} %param.19) | copy-start | bytes 393220
  22.7 38.4 %all-to-all-start = ((f32[32,8,2048]{2,1,0:T(8,128)}), f32[32,8,2048]{2,1,0:T(8,128)}, u32[]{:S(2)}, u32[]{:S(2)}) async-start(f32[32,8,2048]{2,1,0:T(8,128)} %bitcast.27), calls=%async_computation | async-start | bytes 4194304 | tf_op jit(solution)/shard_map/all_to_all | solution.py:262
  31.2 11.9 %collective-permute-start.3 = (f32[1,256,128]{2,1,0:T(8,128)S(1)}, f32[1,256,128]{2,1,0:T(8,128)S(1)}, u32[]{:S(2)}, u32[]{:S(2)}) collective-permute-start(f32[1,256,128]{2,1,0:T(8,128)S(1)} %copy-done), channel_id=1, source_target_pairs={{3,0},{0,1},{1,2},{2,3},{7,4},{4,5},{5,6},{6,7},{11,8},{8,9},{9,10... | collective-permute-start | bytes 393224 | tf_op jit(solution)/shard_map/ppermute | solution.py:31
  33.7 9.3 %collective-permute-start.2 = (f32[1,256,128]{2,1,0:T(8,128)S(1)}, f32[1,256,128]{2,1,0:T(8,128)S(1)}, u32[]{:S(2)}, u32[]{:S(2)}) collective-permute-start(f32[1,256,128]{2,1,0:T(8,128)S(1)} %copy-done), channel_id=1, source_target_pairs={{2,0},{3,1},{0,2},{1,3},{6,4},{7,5},{4,6},{5,7},{10,8},{11,9},{8,1... | collective-permute-start | bytes 393224 | tf_op jit(solution)/shard_map/ppermute | solution.py:31
  36.6 5.9 %collective-permute-start.1 = (f32[1,256,128]{2,1,0:T(8,128)S(1)}, f32[1,256,128]{2,1,0:T(8,128)S(1)}, u32[]{:S(2)}, u32[]{:S(2)}) collective-permute-start(f32[1,256,128]{2,1,0:T(8,128)S(1)} %copy-done), channel_id=1, source_target_pairs={{1,0},{2,1},{3,2},{0,3},{5,4},{6,5},{7,6},{4,7},{9,8},{10,9},{11,1... | collective-permute-start | bytes 393224 | tf_op jit(solution)/shard_map/ppermute | solution.py:31

commit v13 on v12

--- a/solution.py
+++ b/solution.py
@@ -151,7 +151,7 @@
     return ar * br - ai * bi, ar * bi + ai * br
 
 
-def column_forward_kernel(blk_ref, hist_ref, t1c, t1s, t2c, t2s, lrh, lrl, lih, lil, pac, pas, pbc, pbs,
+def column_forward_kernel(blk_ref, hist_ref, t1c, t1s, t2c, t2s, lh, ll, pac, pas, pbc, pbs,
                           out_ref, xs_ref):
     tw = [cmul(t1c[k:k + 1, :], t1s[k:k + 1, :], t2c[:, k:k + 1], t2s[:, k:k + 1]) for k in range(32)]
     for p in range(2):
@@ -171,8 +171,9 @@
     dims = (((1,), (1,)), ((), ()))
     for h in range(2):
         x = xs_ref[512 * h:512 * (h + 1), :]
-        ore = dot3(x, lrh[...], lrl[...], dims, a_first=False)
-        oim = dot3(x, lih[...], lil[...], dims, a_first=False)
+        both = dot3(x, lh[...], ll[...], dims, a_first=False)
+        ore = both[0:256]
+        oim = both[256:512]
         ac = pac[:, 512 * h:512 * (h + 1)]
         as_ = pas[:, 512 * h:512 * (h + 1)]
         for d in range(32):
@@ -292,7 +293,7 @@
     lr, li = send_matrices()
     (send,) = call(column_forward_kernel, [(256, 2048)], [(1024, 512)],
                    block, history, jnp.asarray(t1c), jnp.asarray(t1s), t2c, t2s,
-                   *halves(lr), *halves(li), pac, pas, pbc, pbs)
+                   *halves(np.concatenate([lr, li], axis=0)), pac, pas, pbc, pbs)
     received = exchanged(send)
 
     chirp_phase, send = lax.optimization_barrier((chirp_phase, send))

time: 109 us -> 109 us (level)
  no operation moved by 1% of the time
where the time goes in v13:
time: 109 us; the launch traced here: 108 us
  blocking collectives  33.3 us (31%)
  Pallas kernels  19.5 us (18%)
  starting transfers between devices  18.8 us (17%)
  local copies, waits for them, and re-layouts  15.6 us (14%)
  waiting for transfers between devices  11.7 us (11%)
  other arithmetic  8.69 us (8%)
    all_to_all x1, blocking collectives, exchanged(): lax.all_to_all(block.reshape(32, rows // 32, width), 'band', 0, 0, tiled=...  33.3 us
    pallas_call x3, Pallas kernels, call(): pl.pallas_call(kernel, out_shape=[jax.ShapeDtypeStruct(s, F32) for s in o...  19.5 us
    sin x4, other arithmetic, unit(): return (jnp.cos(angle), jnp.sin(angle))  8.67 us
    all_to_all x1, starting transfers between devices, exchanged(): lax.all_to_all(block.reshape(32, rows // 32, width), 'band', 0, 0, tiled=...  8.42 us
    ppermute x3, starting transfers between devices, gathered(): pieces.append(lax.ppermute(block, axis, route))  6.8 us
    reshape x2, local copies, waits for them, and re-layouts, arranged(): table.reshape(32, 32, 4, 8, 4).transpose(3, 1, 2, 4, 0).reshape(1024, 128)  6.1 us
    ppermute x3, waiting for transfers between devices, gathered(): pieces.append(lax.ppermute(block, axis, route))  5.01 us
    all_to_all x1, waiting for transfers between devices, exchanged(): lax.all_to_all(block.reshape(32, rows // 32, width), 'band', 0, 0, tiled=...  4.28 us
  transfers between devices with their start and end apart: 5, of which 4 were waited for; matrix products, arithmetic and copies ran while one was open for 21% of the time, Pallas kernels for 0%

profile of v13, /device:TPU:0, one launch (start us, length us, event | category | flops | bytes accessed | tf_op | source)
XLA Modules:
  0.0 107.8 jit_solution(540323263179606175)
XLA Ops:
  0.0 1.1 slice.4
  1.1 3.6 %collective-permute-start = (f32[2,2,32,1024]{3,2,1,0:T(8,128)S(1)}, f32[2,2,32,1024]{3,2,1,0:T(8,128)S(1)}, u32[]{:S(2)}, u32[]{:S(2)}) collective-permute-start(f32[2,2,32,1024]{3,2,1,0:T(8,128)S(1)} %slice.4), channel_id=1, source_target_pairs={{0,1},{1,2},{2,3},{4,5},{5,6},{6,7},{8,9},{9,10},{10,11},{12,13},{... | collective-permute-start | bytes 1572872 | tf_op jit(solution)/shard_map/ppermute | solution.py:23
  4.7 0.8 fusion.24
  5.5 0.8 fusion.19
  6.3 1.3 %fusion.11 = (f32[32,1024]{1,0:T(8,128)}, f32[32,1024]{1,0:T(8,128)}) fusion(s32[1024]{0:T(1024)S(1)} %get-tuple-element.27), kind=kLoop, calls=%fused_computation.27 | loop fusion | flops 458752 | bytes 266240 | tf_op jit(solution)/shard_map/sin | solution.py:92
  7.6 5.8 %fusion.3 = (f32[256,1024]{1,0:T(8,128)}, f32[256,1024]{1,0:T(8,128)}) fusion(s32[256]{0:T(256)S(1)} %get-tuple-element.25, s32[1024]{0:T(1024)S(1)} %get-tuple-element.24, s32[1024]{0:T(1024)S(1)} %get-tuple-element.23, s32[256]{0:T(256)S(1)} %get-tuple-element.26), kind=kLoop, calls=%fused_computation.6 | loop fusion | flops 4194304 | bytes 2107392 | tf_op jit(solution)/shard_map/sin | solution.py:92
  13.4 2.4 %collective-permute-done.hist_ref = f32[2,2,32,1024]{3,2,1,0:T(8,128)S(1)} collective-permute-done((f32[2,2,32,1024]{3,2,1,0:T(8,128)S(1)}, f32[2,2,32,1024]{3,2,1,0:T(8,128)S(1)}, u32[]{:S(2)}, u32[]{:S(2)}) %collective-permute-start) | collective-permute-done | bytes 524320 | tf_op jit(solution)/shard_map/ppermute | solution.py:23
  15.8 0.0 copy-start.1
  15.8 0.8 copy-done.1
  16.6 6.0 %shard_map.154 = f32[256,2048]{1,0:T(8,128)} custom-call(f32[2,2,32,3072]{3,2,1,0:T(8,128)} %bitcast.30, f32[2,2,32,1024]{3,2,1,0:T(8,128)} %copy-done.1, f32[32,128]{1,0:T(8,128)} %constant.174.clone.t1c, f32[32,128]{1,0:T(8,128)} %constant.175.clone.t1s, f32[32,32]{1,0:T(8,128)} %get-tuple-element.22.t2c, f32[32,32]{1,0:T(8,128)} %get-tuple-element.21.t2s, ...), custom_call_target="tpu_custom_call" | custom-call | tf_op jit(solution)/shard_map/pallas_call | solution.py:253
  22.7 0.0 copy-start
  22.7 8.4 %all-to-all-start = ((f32[32,8,2048]{2,1,0:T(8,128)}), f32[32,8,2048]{2,1,0:T(8,128)}, u32[]{:S(2)}, u32[]{:S(2)}) async-start(f32[32,8,2048]{2,1,0:T(8,128)} %bitcast.27), calls=%async_computation | async-start | bytes 4194304 | tf_op jit(solution)/shard_map/all_to_all | solution.py:263
  31.1 0.0 copy-done
  31.1 2.6 %collective-permute-start.3 = (f32[1,256,128]{2,1,0:T(8,128)S(1)}, f32[1,256,128]{2,1,0:T(8,128)S(1)}, u32[]{:S(2)}, u32[]{:S(2)}) collective-permute-start(f32[1,256,128]{2,1,0:T(8,128)S(1)} %copy-done), channel_id=1, source_target_pairs={{3,0},{0,1},{1,2},{2,3},{7,4},{4,5},{5,6},{6,7},{11,8},{8,9},{9,10... | collective-permute-start | bytes 393224 | tf_op jit(solution)/shard_map/ppermute | solution.py:31
  33.7 2.9 %collective-permute-start.2 = (f32[1,256,128]{2,1,0:T(8,128)S(1)}, f32[1,256,128]{2,1,0:T(8,128)S(1)}, u32[]{:S(2)}, u32[]{:S(2)}) collective-permute-start(f32[1,256,128]{2,1,0:T(8,128)S(1)} %copy-done), channel_id=1, source_target_pairs={{2,0},{3,1},{0,2},{1,3},{6,4},{7,5},{4,6},{5,7},{10,8},{11,9},{8,1... | collective-permute-start | bytes 393224 | tf_op jit(solution)/shard_map/ppermute | solution.py:31
  36.6 1.3 %collective-permute-start.1 = (f32[1,256,128]{2,1,0:T(8,128)S(1)}, f32[1,256,128]{2,1,0:T(8,128)S(1)}, u32[]{:S(2)}, u32[]{:S(2)}) collective-permute-start(f32[1,256,128]{2,1,0:T(8,128)S(1)} %copy-done), channel_id=1, source_target_pairs={{1,0},{2,1},{3,2},{0,3},{5,4},{6,5},{7,6},{4,7},{9,8},{10,9},{11,1... | collective-permute-start | bytes 393224 | tf_op jit(solution)/shard_map/ppermute | solution.py:31
  37.9 4.5 %collective-permute-done.1 = f32[1,256,128]{2,1,0:T(8,128)S(1)} collective-permute-done((f32[1,256,128]{2,1,0:T(8,128)S(1)}, f32[1,256,128]{2,1,0:T(8,128)S(1)}, u32[]{:S(2)}, u32[]{:S(2)}) %collective-permute-start.1) | collective-permute-done | bytes 131104 | tf_op jit(solution)/shard_map/ppermute | solution.py:31
  42.5 0.5 collective-permute-done.2
  43.0 0.0 collective-permute-done.3
  43.1 1.9 %dynamic-slice_sine_fusion = (f32[4,1,256,128]{3,2,1,0:T(8,128)S(1)}, f32[4,1,256,128]{3,2,1,0:T(8,128)S(1)}) fusion(f32[8,1,256,128]{3,2,1,0:T(8,128)S(1)} %bitcast_dynamic-update-slice_fusion.1, s32[]{:T(128)S(6)} %select_n.110), kind=kLoop, calls=%fused_computation.8 | loop fusion | bytes 1572868 | tf_op jit(solution)/shard_map/sin | solution.py:301
  44.9 0.2 copy.21
  45.2 0.2 copy.19
  45.4 0.6 cos.24
  46.0 2.0 %copy.20 = f32[8,32,4,4,32]{4,3,2,1,0:T(4,128)} copy(f32[8,32,4,4,32]{1,4,3,0,2:T(8,128)S(1)} %bitcast.25) | data formatting | bytes 1048576 | tf_op jit(solution)/shard_map/transpose | solution.py:268
  48.0 3.1 %reshape.164.chc_ref = f32[1024,128]{1,0:T(8,128)} reshape(f32[8,32,4,4,32]{4,3,2,1,0:T(4,128)} %copy.20) | data formatting | bytes 1048576 | tf_op jit(solution)/shard_map/reshape | solution.py:268
  51.1 0.6 sin.24
  51.7 2.0 %copy.22 = f32[8,32,4,4,32]{4,3,2,1,0:T(4,128)} copy(f32[8,32,4,4,32]{1,4,3,0,2:T(8,128)S(1)} %bitcast.26) | data formatting | bytes 1048576 | tf_op jit(solution)/shard_map/transpose | solution.py:268
  53.7 3.0 %reshape.165.chs_ref = f32[1024,128]{1,0:T(8,128)} reshape(f32[8,32,4,4,32]{4,3,2,1,0:T(4,128)} %copy.22) | data formatting | bytes 1048576 | tf_op jit(solution)/shard_map/reshape | solution.py:268
  56.8 4.3 %all-to-all-done = f32[32,8,2048]{2,1,0:T(8,128)} async-done(((f32[32,8,2048]{2,1,0:T(8,128)}), f32[32,8,2048]{2,1,0:T(8,128)}, u32[]{:S(2)}, u32[]{:S(2)}) %all-to-all-start) | async-done | bytes 2097184 | tf_op jit(solution)/shard_map/all_to_all | solution.py:263
  61.1 8.1 %shard_map.155 = f32[256,2048]{1,0:T(8,128)} custom-call(f32[256,2048]{1,0:T(8,128)} %bitcast.2.x_ref, f32[32,512]{1,0:T(8,128)} %constant.178.clone.twc_ref, f32[32,512]{1,0:T(8,128)} %constant.179.clone.tws_ref, bf16[256,256]{1,0:T(8,128)(2,1)} %constant.180.clone.bfh, bf16[256,256]{1,0:T(8,128)(2,1)} %constant.181.clone.bfl, ...), custom_call_target="tpu_custom_call" | custom-call | tf_op jit(solution)/shard_map/pallas_call | solution.py:253
  69.1 33.3 %all_to_all.10 = f32[32,8,2048]{2,1,0:T(8,128)} all-to-all(f32[32,8,2048]{2,1,0:T(8,128)} %bitcast.28), channel_id=1, replica_groups=mesh['band'=32,'seg'=4] {'band'}, dimensions={0} | all-to-all | bytes 4194304 | tf_op jit(solution)/shard_map/all_to_all | solution.py:263
  102.4 5.4 %shard_map.156 = f32[2,2,32,3072]{3,2,1,0:T(8,128)} custom-call(f32[256,2048]{1,0:T(8,128)} %bitcast.24, bf16[512,512]{1,0:T(8,128)(2,1)} %constant.184.clone.mh_ref, bf16[512,512]{1,0:T(8,128)(2,1)} %constant.185.clone.ml_ref, f32[32,256]{1,0:T(8,128)} %constant.186.clone.twc_ref, f32[32,256]{1,0:T(8,128)} %constant.187.clone.tws_ref), custom_call_target="tpu_custom_call" | custom-call | tf_op jit(solution)/shard_map/pallas_call | solution.py:253
  (13 shorter events, 0.1 us)
Async XLA Ops:
  1.1 14.7 %collective-permute-start = (f32[2,2,32,1024]{3,2,1,0:T(8,128)S(1)}, f32[2,2,32,1024]{3,2,1,0:T(8,128)S(1)}, u32[]{:S(2)}, u32[]{:S(2)}) collective-permute-start(f32[2,2,32,1024]{3,2,1,0:T(8,128)S(1)} %slice.4), channel_id=1, source_target_pairs={{0,1},{1,2},{2,3},{4,5},{5,6},{6,7},{8,9},{9,10},{10,11},{12,13},{... | collective-permute-start | bytes 1572872 | tf_op jit(solution)/shard_map/ppermute | solution.py:23
  15.8 0.8 copy-start.1
  22.7 8.4 %copy-start = (f32[1,256,128]{2,1,0:T(8,128)S(1)}, f32[1,256,128]{2,1,0:T(8,128)}, u32[]{:S(2)}) copy-start(f32[1,256,128]{2,1,0:T(8,128)} %param.17) | copy-start | bytes 393220
  22.7 38.4 %all-to-all-start = ((f32[32,8,2048]{2,1,0:T(8,128)}), f32[32,8,2048]{2,1,0:T(8,128)}, u32[]{:S(2)}, u32[]{:S(2)}) async-start(f32[32,8,2048]{2,1,0:T(8,128)} %bitcast.27), calls=%async_computation | async-start | bytes 4194304 | tf_op jit(solution)/shard_map/all_to_all | solution.py:263
  31.1 11.9 %collective-permute-start.3 = (f32[1,256,128]{2,1,0:T(8,128)S(1)}, f32[1,256,128]{2,1,0:T(8,128)S(1)}, u32[]{:S(2)}, u32[]{:S(2)}) collective-permute-start(f32[1,256,128]{2,1,0:T(8,128)S(1)} %copy-done), channel_id=1, source_target_pairs={{3,0},{0,1},{1,2},{2,3},{7,4},{4,5},{5,6},{6,7},{11,8},{8,9},{9,10... | collective-permute-start | bytes 393224 | tf_op jit(solution)/shard_map/ppermute | solution.py:31
  33.7 9.3 %collective-permute-start.2 = (f32[1,256,128]{2,1,0:T(8,128)S(1)}, f32[1,256,128]{2,1,0:T(8,128)S(1)}, u32[]{:S(2)}, u32[]{:S(2)}) collective-permute-start(f32[1,256,128]{2,1,0:T(8,128)S(1)} %copy-done), channel_id=1, source_target_pairs={{2,0},{3,1},{0,2},{1,3},{6,4},{7,5},{4,6},{5,7},{10,8},{11,9},{8,1... | collective-permute-start | bytes 393224 | tf_op jit(solution)/shard_map/ppermute | solution.py:31
  36.6 5.9 %collective-permute-start.1 = (f32[1,256,128]{2,1,0:T(8,128)S(1)}, f32[1,256,128]{2,1,0:T(8,128)S(1)}, u32[]{:S(2)}, u32[]{:S(2)}) collective-permute-start(f32[1,256,128]{2,1,0:T(8,128)S(1)} %copy-done), channel_id=1, source_target_pairs={{1,0},{2,1},{3,2},{0,3},{5,4},{6,5},{7,6},{4,7},{9,8},{10,9},{11,1... | collective-permute-start | bytes 393224 | tf_op jit(solution)/shard_map/ppermute | solution.py:31

commit v14 on v12

--- a/solution.py
+++ b/solution.py
@@ -173,12 +173,9 @@
         x = xs_ref[512 * h:512 * (h + 1), :]
         ore = dot3(x, lrh[...], lrl[...], dims, a_first=False)
         oim = dot3(x, lih[...], lil[...], dims, a_first=False)
-        ac = pac[:, 512 * h:512 * (h + 1)]
-        as_ = pas[:, 512 * h:512 * (h + 1)]
         for d in range(32):
-            bc = pbc[d:d + 1, 512 * h:512 * (h + 1)]
-            bs = pbs[d:d + 1, 512 * h:512 * (h + 1)]
-            wc, ws = cmul(ac, as_, bc, bs)
+            wc = pac[8 * d:8 * d + 8, 512 * h:512 * (h + 1)]
+            ws = pas[8 * d:8 * d + 8, 512 * h:512 * (h + 1)]
             re, im = cmul(ore[8 * d:8 * d + 8], oim[8 * d:8 * d + 8], wc, ws)
             out_ref[8 * d:8 * d + 8, 1024 * h:1024 * h + 512] = re
             out_ref[8 * d:8 * d + 8, 1024 * h + 512:1024 * h + 1024] = im
@@ -288,11 +285,13 @@
     back_c, back_s = unit((32 * (rows // 8) + lane % 32) * (kc_lane + 32 * (rows % 4)), LENGTH, 1)
     back_c, back_s, history = lax.optimization_barrier((back_c, back_s, history))
 
+    post_c, post_s = cmul(pac[None], pas[None], pbc[:, None], pbs[:, None])
+    post_c, post_s = post_c.reshape(256, 1024), post_s.reshape(256, 1024)
     t1c, t1s = lane_twiddle(-1, 128)
     lr, li = send_matrices()
     (send,) = call(column_forward_kernel, [(256, 2048)], [(1024, 512)],
                    block, history, jnp.asarray(t1c), jnp.asarray(t1s), t2c, t2s,
-                   *halves(lr), *halves(li), pac, pas, pbc, pbs)
+                   *halves(lr), *halves(li), post_c, post_s, pbc, pbs)
     received = exchanged(send)
 
     chirp_phase, send = lax.optimization_barrier((chirp_phase, send))

time: 109 us -> 110 us (level)
    sin x4 -> x2, other arithmetic: 8.67 us -> 6.71 us  [unit(): return (jnp.cos(angle), jnp.sin(angle))]
    add x0 -> x1, other arithmetic: none -> 1.62 us  [cmul(): return (ar * br - ai * bi, ar * bi + ai * br)]
where the time goes in v14:
time: 110 us; the launch traced here: 108 us
  blocking collectives  33.3 us (30%)
  Pallas kernels  20.1 us (18%)
  starting transfers between devices  18.8 us (17%)
  local copies, waits for them, and re-layouts  15.7 us (14%)
  waiting for transfers between devices  11.2 us (10%)
  other arithmetic  9.1 us (8%)
    all_to_all x1, blocking collectives, exchanged(): lax.all_to_all(block.reshape(32, rows // 32, width), 'band', 0, 0, tiled=...  33.3 us
    pallas_call x3, Pallas kernels, call(): pl.pallas_call(kernel, out_shape=[jax.ShapeDtypeStruct(s, F32) for s in o...  20.1 us
    all_to_all x1, starting transfers between devices, exchanged(): lax.all_to_all(block.reshape(32, rows // 32, width), 'band', 0, 0, tiled=...  8.42 us
    ppermute x3, starting transfers between devices, gathered(): pieces.append(lax.ppermute(block, axis, route))  6.8 us
    sin x2, other arithmetic, unit(): return (jnp.cos(angle), jnp.sin(angle))  6.71 us
    reshape x2, local copies, waits for them, and re-layouts, arranged(): table.reshape(32, 32, 4, 8, 4).transpose(3, 1, 2, 4, 0).reshape(1024, 128)  6.13 us
    ppermute x3, waiting for transfers between devices, gathered(): pieces.append(lax.ppermute(block, axis, route))  5.01 us
    all_to_all x1, waiting for transfers between devices, exchanged(): lax.all_to_all(block.reshape(32, rows // 32, width), 'band', 0, 0, tiled=...  4.24 us
  transfers between devices with their start and end apart: 5, of which 4 were waited for; matrix products, arithmetic and copies ran while one was open for 21% of the time, Pallas kernels for 0%

profile of v14, /device:TPU:0, one launch (start us, length us, event | category | flops | bytes accessed | tf_op | source)
XLA Modules:
  0.0 108.4 jit_solution(17822868847838107843)
XLA Ops:
  0.0 1.1 slice.4
  1.1 3.6 %collective-permute-start = (f32[2,2,32,1024]{3,2,1,0:T(8,128)S(1)}, f32[2,2,32,1024]{3,2,1,0:T(8,128)S(1)}, u32[]{:S(2)}, u32[]{:S(2)}) collective-permute-start(f32[2,2,32,1024]{3,2,1,0:T(8,128)S(1)} %slice.4), channel_id=1, source_target_pairs={{0,1},{1,2},{2,3},{4,5},{5,6},{6,7},{8,9},{9,10},{10,11},{12,13},{... | collective-permute-start | bytes 1572872 | tf_op jit(solution)/shard_map/ppermute | solution.py:23
  4.8 0.2 fusion.20
  5.0 6.0 %fusion.3 = (f32[256,1024]{1,0:T(8,128)}, f32[256,1024]{1,0:T(8,128)}) fusion(s32[256]{0:T(256)S(1)} %get-tuple-element.27, s32[1024]{0:T(1024)S(1)} %get-tuple-element.26, s32[1024]{0:T(1024)S(1)} %get-tuple-element.25, s32[256]{0:T(256)S(1)} %get-tuple-element.28), kind=kLoop, calls=%fused_computation.8 | loop fusion | flops 4194304 | bytes 2107392 | tf_op jit(solution)/shard_map/sin | solution.py:92
  10.9 0.8 fusion.24
  11.7 0.5 fusion.12
  12.2 0.0 copy-start
  12.2 0.0 copy-start.1
  12.2 1.6 %add_bitcast_fusion = (f32[256,1024]{1,0:T(8,128)}, f32[256,1024]{1,0:T(8,128)}) fusion(f32[32,1024]{1,0:T(8,128)S(1)} %get-tuple-element.22.pbs, f32[8,1024]{1,0:T(8,128)S(1)} %get-tuple-element.20, f32[32,1024]{1,0:T(8,128)S(1)} %get-tuple-element.21.pbc, f32[8,1024]{1,0:T(8,128)S(1)} %get-tuple-element.19), kind=kLoop, calls=%fused_computation.6 | loop fusion | flops 1572864 | bytes 2424832 | tf_op jit(solution)/shard_map/add | solution.py:151
  13.9 2.0 %collective-permute-done.hist_ref = f32[2,2,32,1024]{3,2,1,0:T(8,128)S(1)} collective-permute-done((f32[2,2,32,1024]{3,2,1,0:T(8,128)S(1)}, f32[2,2,32,1024]{3,2,1,0:T(8,128)S(1)}, u32[]{:S(2)}, u32[]{:S(2)}) %collective-permute-start) | collective-permute-done | bytes 524320 | tf_op jit(solution)/shard_map/ppermute | solution.py:23
  15.8 0.0 copy-start.3
  15.8 0.0 copy-done
  15.8 0.0 copy-done.1
  15.8 0.8 copy-done.3
  16.6 6.7 %shard_map.172 = f32[256,2048]{1,0:T(8,128)} custom-call(f32[2,2,32,3072]{3,2,1,0:T(8,128)} %bitcast.34, f32[2,2,32,1024]{3,2,1,0:T(8,128)} %copy-done.3, f32[32,128]{1,0:T(8,128)} %constant.180.clone.t1c, f32[32,128]{1,0:T(8,128)} %constant.181.clone.t1s, f32[32,32]{1,0:T(8,128)} %get-tuple-element.24.t2c, f32[32,32]{1,0:T(8,128)} %get-tuple-element.23.t2s, ...), custom_call_target="tpu_custom_call" | custom-call | tf_op jit(solution)/shard_map/pallas_call | solution.py:249
  23.3 0.0 copy-start.2
  23.3 8.4 %all-to-all-start = ((f32[32,8,2048]{2,1,0:T(8,128)}), f32[32,8,2048]{2,1,0:T(8,128)}, u32[]{:S(2)}, u32[]{:S(2)}) async-start(f32[32,8,2048]{2,1,0:T(8,128)} %bitcast.31), calls=%async_computation | async-start | bytes 4194304 | tf_op jit(solution)/shard_map/all_to_all | solution.py:259
  31.7 0.0 copy-done.2
  31.7 2.6 %collective-permute-start.3 = (f32[1,256,128]{2,1,0:T(8,128)S(1)}, f32[1,256,128]{2,1,0:T(8,128)S(1)}, u32[]{:S(2)}, u32[]{:S(2)}) collective-permute-start(f32[1,256,128]{2,1,0:T(8,128)S(1)} %copy-done.2), channel_id=1, source_target_pairs={{3,0},{0,1},{1,2},{2,3},{7,4},{4,5},{5,6},{6,7},{11,8},{8,9},{9,10... | collective-permute-start | bytes 393224 | tf_op jit(solution)/shard_map/ppermute | solution.py:31
  34.3 2.9 %collective-permute-start.2 = (f32[1,256,128]{2,1,0:T(8,128)S(1)}, f32[1,256,128]{2,1,0:T(8,128)S(1)}, u32[]{:S(2)}, u32[]{:S(2)}) collective-permute-start(f32[1,256,128]{2,1,0:T(8,128)S(1)} %copy-done.2), channel_id=1, source_target_pairs={{2,0},{3,1},{0,2},{1,3},{6,4},{7,5},{4,6},{5,7},{10,8},{11,9},{8,1... | collective-permute-start | bytes 393224 | tf_op jit(solution)/shard_map/ppermute | solution.py:31
  37.2 1.3 %collective-permute-start.1 = (f32[1,256,128]{2,1,0:T(8,128)S(1)}, f32[1,256,128]{2,1,0:T(8,128)S(1)}, u32[]{:S(2)}, u32[]{:S(2)}) collective-permute-start(f32[1,256,128]{2,1,0:T(8,128)S(1)} %copy-done.2), channel_id=1, source_target_pairs={{1,0},{2,1},{3,2},{0,3},{5,4},{6,5},{7,6},{4,7},{9,8},{10,9},{11,1... | collective-permute-start | bytes 393224 | tf_op jit(solution)/shard_map/ppermute | solution.py:31
  38.5 4.5 %collective-permute-done.1 = f32[1,256,128]{2,1,0:T(8,128)S(1)} collective-permute-done((f32[1,256,128]{2,1,0:T(8,128)S(1)}, f32[1,256,128]{2,1,0:T(8,128)S(1)}, u32[]{:S(2)}, u32[]{:S(2)}) %collective-permute-start.1) | collective-permute-done | bytes 131104 | tf_op jit(solution)/shard_map/ppermute | solution.py:31
  43.1 0.5 collective-permute-done.2
  43.6 0.0 collective-permute-done.3
  43.7 1.9 %dynamic-slice_sine_fusion = (f32[4,1,256,128]{3,2,1,0:T(8,128)S(1)}, f32[4,1,256,128]{3,2,1,0:T(8,128)S(1)}) fusion(f32[8,1,256,128]{3,2,1,0:T(8,128)S(1)} %bitcast_dynamic-update-slice_fusion.1, s32[]{:T(128)S(6)} %select_n.124), kind=kLoop, calls=%fused_computation.10 | loop fusion | bytes 1572868 | tf_op jit(solution)/shard_map/sin | solution.py:299
  45.6 0.2 copy.23
  45.8 0.2 copy.21
  46.0 0.6 cos.28
  46.6 2.0 %copy.22 = f32[8,32,4,4,32]{4,3,2,1,0:T(4,128)} copy(f32[8,32,4,4,32]{1,4,3,0,2:T(8,128)S(1)} %bitcast.29) | data formatting | bytes 1048576 | tf_op jit(solution)/shard_map/transpose | solution.py:264
  48.7 3.1 %reshape.295.chc_ref = f32[1024,128]{1,0:T(8,128)} reshape(f32[8,32,4,4,32]{4,3,2,1,0:T(4,128)} %copy.22) | data formatting | bytes 1048576 | tf_op jit(solution)/shard_map/reshape | solution.py:264
  51.7 0.6 sin.28
  52.3 2.0 %copy.24 = f32[8,32,4,4,32]{4,3,2,1,0:T(4,128)} copy(f32[8,32,4,4,32]{1,4,3,0,2:T(8,128)S(1)} %bitcast.30) | data formatting | bytes 1048576 | tf_op jit(solution)/shard_map/transpose | solution.py:264
  54.4 3.1 %reshape.296.chs_ref = f32[1024,128]{1,0:T(8,128)} reshape(f32[8,32,4,4,32]{4,3,2,1,0:T(4,128)} %copy.24) | data formatting | bytes 1048576 | tf_op jit(solution)/shard_map/reshape | solution.py:264
  57.4 4.2 %all-to-all-done = f32[32,8,2048]{2,1,0:T(8,128)} async-done(((f32[32,8,2048]{2,1,0:T(8,128)}), f32[32,8,2048]{2,1,0:T(8,128)}, u32[]{:S(2)}, u32[]{:S(2)}) %all-to-all-start) | async-done | bytes 2097184 | tf_op jit(solution)/shard_map/all_to_all | solution.py:259
  61.7 8.1 %shard_map.173 = f32[256,2048]{1,0:T(8,128)} custom-call(f32[256,2048]{1,0:T(8,128)} %bitcast.4.x_ref, f32[32,512]{1,0:T(8,128)} %constant.186.clone.twc_ref, f32[32,512]{1,0:T(8,128)} %constant.187.clone.tws_ref, bf16[256,256]{1,0:T(8,128)(2,1)} %constant.188.clone.bfh, bf16[256,256]{1,0:T(8,128)(2,1)} %constant.189.clone.bfl, ...), custom_call_target="tpu_custom_call" | custom-call | tf_op jit(solution)/shard_map/pallas_call | solution.py:249
  69.7 33.3 %all_to_all.10 = f32[32,8,2048]{2,1,0:T(8,128)} all-to-all(f32[32,8,2048]{2,1,0:T(8,128)} %bitcast.32), channel_id=1, replica_groups=mesh['band'=32,'seg'=4] {'band'}, dimensions={0} | all-to-all | bytes 4194304 | tf_op jit(solution)/shard_map/all_to_all | solution.py:259
  103.0 5.4 %shard_map.174 = f32[2,2,32,3072]{3,2,1,0:T(8,128)} custom-call(f32[256,2048]{1,0:T(8,128)} %bitcast.28, bf16[512,512]{1,0:T(8,128)(2,1)} %constant.192.clone.mh_ref, bf16[512,512]{1,0:T(8,128)(2,1)} %constant.193.clone.ml_ref, f32[32,256]{1,0:T(8,128)} %constant.194.clone.twc_ref, f32[32,256]{1,0:T(8,128)} %constant.195.clone.tws_ref), custom_call_target="tpu_custom_call" | custom-call | tf_op jit(solution)/shard_map/pallas_call | solution.py:249
  (13 shorter events, 0.1 us)
Async XLA Ops:
  1.1 14.7 %collective-permute-start = (f32[2,2,32,1024]{3,2,1,0:T(8,128)S(1)}, f32[2,2,32,1024]{3,2,1,0:T(8,128)S(1)}, u32[]{:S(2)}, u32[]{:S(2)}) collective-permute-start(f32[2,2,32,1024]{3,2,1,0:T(8,128)S(1)} %slice.4), channel_id=1, source_target_pairs={{0,1},{1,2},{2,3},{4,5},{5,6},{6,7},{8,9},{9,10},{10,11},{12,13},{... | collective-permute-start | bytes 1572872 | tf_op jit(solution)/shard_map/ppermute | solution.py:23
  12.2 3.6 %copy-start = (f32[32,1024]{1,0:T(8,128)}, f32[32,1024]{1,0:T(8,128)S(1)}, u32[]{:S(2)}) copy-start(f32[32,1024]{1,0:T(8,128)S(1)} %get-tuple-element.21.pbc) | copy-start | bytes 393220
  12.2 3.6 %copy-start.1 = (f32[32,1024]{1,0:T(8,128)}, f32[32,1024]{1,0:T(8,128)S(1)}, u32[]{:S(2)}) copy-start(f32[32,1024]{1,0:T(8,128)S(1)} %get-tuple-element.22.pbs) | copy-start | bytes 393220
  15.8 0.8 copy-start.3
  23.3 8.5 %copy-start.2 = (f32[1,256,128]{2,1,0:T(8,128)S(1)}, f32[1,256,128]{2,1,0:T(8,128)}, u32[]{:S(2)}) copy-start(f32[1,256,128]{2,1,0:T(8,128)} %param.19) | copy-start | bytes 393220
  23.3 38.4 %all-to-all-start = ((f32[32,8,2048]{2,1,0:T(8,128)}), f32[32,8,2048]{2,1,0:T(8,128)}, u32[]{:S(2)}, u32[]{:S(2)}) async-start(f32[32,8,2048]{2,1,0:T(8,128)} %bitcast.31), calls=%async_computation | async-start | bytes 4194304 | tf_op jit(solution)/shard_map/all_to_all | solution.py:259
  31.7 11.9 %collective-permute-start.3 = (f32[1,256,128]{2,1,0:T(8,128)S(1)}, f32[1,256,128]{2,1,0:T(8,128)S(1)}, u32[]{:S(2)}, u32[]{:S(2)}) collective-permute-start(f32[1,256,128]{2,1,0:T(8,128)S(1)} %copy-done.2), channel_id=1, source_target_pairs={{3,0},{0,1},{1,2},{2,3},{7,4},{4,5},{5,6},{6,7},{11,8},{8,9},{9,10... | collective-permute-start | bytes 393224 | tf_op jit(solution)/shard_map/ppermute | solution.py:31
  34.3 9.3 %collective-permute-start.2 = (f32[1,256,128]{2,1,0:T(8,128)S(1)}, f32[1,256,128]{2,1,0:T(8,128)S(1)}, u32[]{:S(2)}, u32[]{:S(2)}) collective-permute-start(f32[1,256,128]{2,1,0:T(8,128)S(1)} %copy-done.2), channel_id=1, source_target_pairs={{2,0},{3,1},{0,2},{1,3},{6,4},{7,5},{4,6},{5,7},{10,8},{11,9},{8,1... | collective-permute-start | bytes 393224 | tf_op jit(solution)/shard_map/ppermute | solution.py:31
  37.2 5.9 %collective-permute-start.1 = (f32[1,256,128]{2,1,0:T(8,128)S(1)}, f32[1,256,128]{2,1,0:T(8,128)S(1)}, u32[]{:S(2)}, u32[]{:S(2)}) collective-permute-start(f32[1,256,128]{2,1,0:T(8,128)S(1)} %copy-done.2), channel_id=1, source_target_pairs={{1,0},{2,1},{3,2},{0,3},{5,4},{6,5},{7,6},{4,7},{9,8},{10,9},{11,1... | collective-permute-start | bytes 393224 | tf_op jit(solution)/shard_map/ppermute | solution.py:31
